TPU v7x, 768 devices: a whole 4x8x12 slice. The times are simulated.
768 devices in a mesh: pipe: 4 (over y_lo), dp: 48 (over y_hi, z, core), tensor: 4 (over x).
Axes of the slice: x: 4, y: 8 (y_hi: 2, y_lo: 4; y = y_hi * 4 + y_lo), z: 12, core: 2. Of those that a mesh axis runs over, the one named last changes fastest.
Arguments:
- grad_out: bfloat16 [4, 4, 48, 96, 6144], P('pipe', None, 'dp'), may hold values from -6 to 6
- qkv_saved: bfloat16 [4, 4, 48, 96, 4, 384], P('pipe', None, 'dp', None, 'tensor'), may hold values from -5 to 5
- w_out: bfloat16 [4, 6144, 4, 128], P('pipe', None, 'tensor'), may hold values from -0.078125 to 0.078125
- w_qkv: bfloat16 [4, 6144, 4, 384], P('pipe', None, 'tensor'), may hold values from -0.15625 to 0.15625
- plan: int32 [4, 4], P('pipe'), may hold values from 0 to 3, each once within a row
Outputs:
- input_grad: bfloat16 [4, 48, 96, 2, 6144], P('pipe', 'dp', 'tensor')
- out_proj_grad: float32 [4, 6144, 4, 128], P('pipe', 'dp', 'tensor')
All inputs are finite; a program needn't handle non-finite values.
Results may differ from a plain program's by a relative error of at most 0.028.
Values may be sent and summed in bfloat16 or wider, within the bound.
No kernel may reach another device: no remote copies, remote signals or barrier semaphores. Data moves between devices by JAX's collectives and lax.ppermute only.
A program may use at most 64 MiB of HBM per device.

v0:
```python
import jax
import jax.numpy as jnp
from jax import lax
from jax.sharding import PartitionSpec as P

BMICRO = 2


def shifted(block, axis, distance):
    devices = range(lax.axis_size(axis))
    route = [(i - distance, i) for i in devices if i - distance in devices]
    return lax.ppermute(block, axis, route)


def head_forward(queries, key_rows, values):
    score_scale = queries.shape[-1] ** (-0.5)
    scores = jnp.dot(queries, key_rows.T, preferred_element_type=jnp.float32) * score_scale
    row_ids = lax.broadcasted_iota(jnp.int32, scores.shape, 0)
    col_ids = lax.broadcasted_iota(jnp.int32, scores.shape, 1)
    scores = jnp.where(col_ids <= row_ids, scores, -1e30)
    row_max = jnp.max(scores, axis=1, keepdims=True)
    weights = jnp.exp(scores - row_max)
    softmax = weights / jnp.sum(weights, axis=1, keepdims=True)
    soft_low = softmax.astype(jnp.bfloat16)
    attended = jnp.dot(soft_low, values, preferred_element_type=jnp.float32).astype(jnp.bfloat16)
    return (softmax, soft_low, attended)


def head_backward(queries, key_rows, values, softmax, soft_low, attended, grad_head):
    score_scale = queries.shape[-1] ** (-0.5)
    row_dot = jnp.sum(
        grad_head.astype(jnp.float32) * attended.astype(jnp.float32), axis=1, keepdims=True
    )
    grad_values = jnp.dot(soft_low.T, grad_head, preferred_element_type=jnp.float32)
    grad_probs = jnp.dot(grad_head, values.T, preferred_element_type=jnp.float32)
    grad_scores = (softmax * (grad_probs - row_dot)).astype(jnp.bfloat16)
    grad_query = jnp.dot(grad_scores, key_rows, preferred_element_type=jnp.float32) * score_scale
    grad_keys = jnp.dot(grad_scores.T, queries, preferred_element_type=jnp.float32) * score_scale
    return jnp.concatenate([grad_query, grad_keys, grad_values], axis=1).astype(jnp.bfloat16)


def body(grad_out, qkv_saved, w_out, w_qkv, plan):
    gradients = grad_out[0, :, 0]
    saved_qkv = qkv_saved[0, :, 0, :, 0]
    out_proj = w_out[0, :, 0]
    qkv_proj = w_qkv[0, :, 0]
    head_size = out_proj.shape[1]
    seq_len = gradients.shape[1]
    queries = saved_qkv[:, :, :head_size]
    key_rows = saved_qkv[:, :, head_size : 2 * head_size]
    values = saved_qkv[:, :, 2 * head_size :]
    softmax, soft_low, attended = jax.vmap(head_forward)(queries, key_rows, values)
    current = plan[0, :BMICRO]
    grad_current = jnp.take(gradients, current, axis=0)
    grad_heads = jnp.einsum(
        "msd,dh->msh", grad_current, out_proj, preferred_element_type=jnp.float32
    ).astype(jnp.bfloat16)
    grad_qkv = jax.vmap(head_backward)(
        jnp.take(queries, current, axis=0),
        jnp.take(key_rows, current, axis=0),
        jnp.take(values, current, axis=0),
        jnp.take(softmax, current, axis=0),
        jnp.take(soft_low, current, axis=0),
        jnp.take(attended, current, axis=0),
        grad_heads,
    )
    share_rows = seq_len // lax.axis_size("tensor")
    partials = jnp.einsum("bsk,dk->sbd", grad_qkv, qkv_proj, preferred_element_type=jnp.float32)
    summed = lax.psum(partials.astype(jnp.bfloat16), "tensor").astype(jnp.float32)
    own_rows = lax.dynamic_slice_in_dim(
        summed, lax.axis_index("tensor") * share_rows, share_rows, 0
    )
    received = shifted(own_rows.astype(jnp.bfloat16), "pipe", -1)
    weight_grad = lax.psum_scatter(
        jnp.einsum("msc,msh->ch", gradients, attended, preferred_element_type=jnp.float32),
        "dp",
        scatter_dimension=0,
        tiled=True,
    )
    return (received[None, None], weight_grad[None, :, None, :])


def solution(mesh):
    in_specs = (
        P("pipe", None, "dp", None, None),
        P("pipe", None, "dp", None, "tensor", None),
        P("pipe", None, "tensor", None),
        P("pipe", None, "tensor", None),
        P("pipe", None),
    )
    out_specs = (P("pipe", "dp", "tensor", None, None), P("pipe", "dp", "tensor", None))
    return jax.shard_map(body, mesh=mesh, in_specs=in_specs, out_specs=out_specs, check_vma=False)
```

profile of v0, /device:TPU:6, one launch (start us, length us, event | category | flops | bytes accessed | tf_op | source)
XLA Modules:
  0.0 247.1 jit_solution(1039753206126935575)
XLA Ops:
  8.1 0.8 compare_and_fusion
  8.8 0.7 fusion.37
  9.5 1.0 fusion.49
  10.5 1.2 fusion.50
  11.7 1.1 convolution_convert_fusion.1
  12.9 0.6 gather_fusion.2
  13.5 4.4 %gather_fusion.1 = bf16[2,96,6144]{2,1,0:T(8,128)(2,1)} fusion(bf16[4,96,6144]{2,1,0:T(8,128)(2,1)} %bitcast.39, s32[1024]{0:T(1024)S(1)} %pad_clamp_fusion.1), kind=kCustom, calls=%fused_computation.5 | custom fusion | bytes 4718600 | tf_op jit(solution)/shard_map/jit(_take)/gather | solution.py:54
  17.9 0.6 gather_fusion
  18.5 0.6 gather_fusion.4
  19.0 0.6 gather_fusion.3
  19.6 0.6 gather_fusion.5
  20.2 0.6 gather_fusion.6
  20.7 2.7 %multiply_reduce_fusion = (f32[2,96]{1,0:T(2,128)S(1)}, bf16[2,96,128]{2,1,0:T(8,128)(2,1)S(1)}) fusion(bf16[2,96,128]{2,1,0:T(8,128)(2,1)S(1)} %gather_fusion.4, pred[2]{0:T(512)(128)(4,1)S(1)} %get-tuple-element.7, bf16[1,6144,1,128]{3,1,2,0:T(8,128)(2,1)S(1)} %copy-done, bf16[2,96,6144]{2,1,0:T(8,128)(2,1)} %gather_fusion.1), kind=kOutput, calls=%fused_computation.37 | convolution fusion | flops 303316800 | bytes 4031234 | tf_op jit(solution)/shard_map/msd,dh->msh/dot_general | solution.py:55
  23.7 0.2 fusion.13
  23.9 0.2 fusion.14
  24.3 3.2 %fusion.1 = bf16[96,2,6144]{2,0,1:T(8,128)(2,1)} fusion(bf16[1,6144,1,384]{3,1,2,0:T(8,128)(2,1)S(1)} %copy-done.1, bf16[2,96,128]{2,1,0:T(8,128)(2,1)S(1)} %convolution_convert_fusion.2, bf16[2,96,128]{2,1,0:T(8,128)(2,1)S(1)} %fusion.14, bf16[2,96,128]{2,1,0:T(8,128)(2,1)S(1)} %fusion.13), kind=kOutput, calls=%fused_computation.10 | convolution fusion | flops 907591680 | bytes 7225344 | tf_op jit(solution)/shard_map/bsk,dk->sbd/dot_general | solution.py:68
  27.6 5.0 %convolution_bitcast_fusion = f32[6144,128]{0,1:T(8,128)} fusion(bf16[4,96,128]{2,1,0:T(8,128)(2,1)S(1)} %convolution_convert_fusion.1, bf16[1,4,1,96,6144]{4,3,2,1,0:T(8,128)(2,1)} %param.7), kind=kOutput, calls=%fused_computation.9 | convolution fusion | flops 603979776 | bytes 7962624 | tf_op jit(solution)/shard_map/msc,msh->ch/dot_general | solution.py:75
  32.7 79.1 %all-reduce.2.cloned.1.call-done = bf16[96,2,6144]{2,0,1:T(8,128)(2,1)} async-done(((bf16[96,2,6144]{2,0,1:T(8,128)(2,1)}), bf16[96,2,6144]{2,0,1:T(8,128)(2,1)}) %all-reduce.2.cloned.1.call-update) | async-done | bytes 2359312 | tf_op jit(solution)/shard_map/psum | solution.py:69
  111.7 1.1 convert_convert_fusion
  112.8 1.3 collective-permute-start
  114.1 31.9 %collective-permute-done = bf16[24,2,6144]{2,0,1:T(8,128)(2,1)S(1)} collective-permute-done((bf16[24,2,6144]{2,0,1:T(8,128)(2,1)S(1)}, bf16[24,2,6144]{2,0,1:T(8,128)(2,1)S(1)}, u32[]{:S(2)}, u32[]{:S(2)}) %collective-permute-start) | collective-permute-done | bytes 589856 | tf_op jit(solution)/shard_map/ppermute | solution.py:12
  146.1 1.4 copy.9
  147.5 90.6 %reduce-scatter.2.cloned.1.call-done = f32[128,128]{0,1:T(8,128)} async-done(((f32[6144,128]{0,1:T(8,128)}), f32[128,128]{0,1:T(8,128)}) %reduce-scatter.2.cloned.1.call-update) | async-done | bytes 65552 | tf_op jit(solution)/shard_map/reduce_scatter | solution.py:74
  238.1 1.6 copy.10
  (14 shorter events, 0.6 us)
Async XLA Ops:
  8.0 12.7 %copy-start = (bf16[1,6144,1,128]{3,1,2,0:T(8,128)(2,1)S(1)}, bf16[1,6144,1,128]{3,1,2,0:T(8,128)(2,1)}, u32[]{:S(2)}) copy-start(bf16[1,6144,1,128]{3,1,2,0:T(8,128)(2,1)} %param.9) | copy-start | bytes 4718596
  8.0 103.7 %all-reduce.2.cloned.1.call-start = ((), (), s32[]{:S(2)}) async-start(), calls=%async_computation.1 | async-start | bytes 4718592 | tf_op jit(solution)/shard_map/psum | solution.py:69
  20.7 3.6 %copy-start.1 = (bf16[1,6144,1,384]{3,1,2,0:T(8,128)(2,1)S(1)}, bf16[1,6144,1,384]{3,1,2,0:T(8,128)(2,1)}, u32[]{:S(2)}) copy-start(bf16[1,6144,1,384]{3,1,2,0:T(8,128)(2,1)} %param.10) | copy-start | bytes 14155780
  27.6 210.6 %reduce-scatter.2.cloned.1.call-start = ((), (), s32[]{:S(2)}) async-start(), calls=%async_computation.2 | async-start | bytes 3211264 | tf_op jit(solution)/shard_map/reduce_scatter | solution.py:74
  112.8 33.2 %collective-permute-start = (bf16[24,2,6144]{2,0,1:T(8,128)(2,1)S(1)}, bf16[24,2,6144]{2,0,1:T(8,128)(2,1)S(1)}, u32[]{:S(2)}, u32[]{:S(2)}) collective-permute-start(bf16[24,2,6144]{2,0,1:T(8,128)(2,1)S(1)} %convert_convert_fusion), channel_id=1, source_target_pairs={{192,0},{384,192},{576,384},{193,1},{385,193},{577,385},{194,2},{3... | collective-permute-start | bytes 1769480 | tf_op jit(solution)/shard_map/ppermute | solution.py:12
Sparse Core Ops, SparseCore 0:
  27.7 83.9 all-reduce.1
Sparse Core Ops, SparseCore 1:
  33.3 204.7 reduce-scatter.1
where the time goes:
time: 248 us; the launch traced here: 247 us
  waiting for transfers between devices  202 us (81%)
  between operations  15.6 us (6%)
  matrix products  14.1 us (6%)
  local copies, waits for them, and re-layouts  11.8 us (5%)
  other arithmetic  2.59 us (1%)
    reduce_scatter x1, waiting for transfers between devices, body(): lax.psum_scatter(jnp.einsum('msc,msh->ch', gradients, attended, preferred...  90.6 us
    psum x1, waiting for transfers between devices, body(): lax.psum(partials.astype(jnp.bfloat16), 'tensor').astype(jnp.float32)  79.1 us
    ppermute x1, waiting for transfers between devices, shifted(): return lax.ppermute(block, axis, route)  31.9 us
    dot_general x1, matrix products, body(): jnp.einsum('msc,msh->ch', gradients, attended, preferred_element_type=jnp...  5.02 us
  transfers between devices with their start and end apart: 3, of which 3 were waited for; matrix products, arithmetic and copies ran while one was open for 3% of the time, Pallas kernels for 0%

commit v1 on v0

--- a/solution.py
+++ b/solution.py
@@ -10,6 +10,19 @@
     devices = range(lax.axis_size(axis))
     route = [(i - distance, i) for i in devices if i - distance in devices]
     return lax.ppermute(block, axis, route)
+
+
+def exchange(block, axis):
+    n = lax.axis_size(axis)
+    parts = block.reshape(n, block.shape[0] // n, *block.shape[1:])
+    return lax.all_to_all(parts, axis, 0, 0, tiled=True).astype(jnp.float32)
+
+
+def ordered_sum(parts):
+    total = parts[0]
+    for index in range(1, parts.shape[0]):
+        total = total + parts[index]
+    return total
 
 
 def head_forward(queries, key_rows, values):
@@ -45,11 +58,12 @@
     out_proj = w_out[0, :, 0]
     qkv_proj = w_qkv[0, :, 0]
     head_size = out_proj.shape[1]
-    seq_len = gradients.shape[1]
     queries = saved_qkv[:, :, :head_size]
     key_rows = saved_qkv[:, :, head_size : 2 * head_size]
     values = saved_qkv[:, :, 2 * head_size :]
     softmax, soft_low, attended = jax.vmap(head_forward)(queries, key_rows, values)
+    weight_part = jnp.einsum("msc,msh->ch", gradients, attended, preferred_element_type=jnp.float32)
+    weight_grad = jnp.sum(exchange(weight_part.astype(jnp.bfloat16), "dp"), axis=0)
     current = plan[0, :BMICRO]
     grad_current = jnp.take(gradients, current, axis=0)
     grad_heads = jnp.einsum(
@@ -64,19 +78,9 @@
         jnp.take(attended, current, axis=0),
         grad_heads,
     )
-    share_rows = seq_len // lax.axis_size("tensor")
     partials = jnp.einsum("bsk,dk->sbd", grad_qkv, qkv_proj, preferred_element_type=jnp.float32)
-    summed = lax.psum(partials.astype(jnp.bfloat16), "tensor").astype(jnp.float32)
-    own_rows = lax.dynamic_slice_in_dim(
-        summed, lax.axis_index("tensor") * share_rows, share_rows, 0
-    )
+    own_rows = ordered_sum(exchange(partials.astype(jnp.bfloat16), "tensor"))
     received = shifted(own_rows.astype(jnp.bfloat16), "pipe", -1)
-    weight_grad = lax.psum_scatter(
-        jnp.einsum("msc,msh->ch", gradients, attended, preferred_element_type=jnp.float32),
-        "dp",
-        scatter_dimension=0,
-        tiled=True,
-    )
     return (received[None, None], weight_grad[None, :, None, :])
 
 

time: 248 us -> 144 us (0.58)
  the two profiles are of different devices: /device:TPU:6 before, /device:TPU:1 now
where the time goes in v1:
time: 144 us; the launch traced here: 143 us
  waiting for transfers between devices  65.5 us (45%)
  starting transfers between devices  38.2 us (27%)
  local copies, waits for them, and re-layouts  18.1 us (13%)
  matrix products  13.2 us (9%)
  other arithmetic  7.25 us (5%)
    all_to_all x2, waiting for transfers between devices, exchange(): return lax.all_to_all(parts, axis, 0, 0, tiled=True).astype(jnp.float32)  37.6 us
    all_to_all x2, starting transfers between devices, exchange(): return lax.all_to_all(parts, axis, 0, 0, tiled=True).astype(jnp.float32)  36.9 us
    ppermute x1, waiting for transfers between devices, shifted(): return lax.ppermute(block, axis, route)  28 us
    reshape x2, local copies, waits for them, and re-layouts, exchange(): parts = block.reshape(n, block.shape[0] // n, *block.shape[1:])  5.44 us
    gather x1, local copies, waits for them, and re-layouts, body(): grad_current = jnp.take(gradients, current, axis=0)  4.44 us
    convert_element_type x1, other arithmetic, exchange(): return lax.all_to_all(parts, axis, 0, 0, tiled=True).astype(jnp.float32)  4.31 us
    dot_general x1, matrix products, body(): jnp.einsum('bsk,dk->sbd', grad_qkv, qkv_proj, preferred_element_type=jnp....  4.15 us
    unnamed x6, local copies, waits for them, and re-layouts  3.83 us
  transfers between devices with their start and end apart: 3, of which 3 were waited for; matrix products, arithmetic and copies ran while one was open for 7% of the time, Pallas kernels for 0%

profile of v1, /device:TPU:1, one launch (start us, length us, event | category | flops | bytes accessed | tf_op | source)
XLA Modules:
  0.0 143.0 jit_solution(16079730265410790881)
XLA Ops:
  0.6 0.8 fusion.40
  1.4 0.7 compare_and_fusion
  2.1 1.0 fusion.52
  3.1 1.2 fusion.53
  4.4 1.1 convolution_convert_fusion.1
  5.5 0.6 gather_fusion.2
  6.6 0.6 gather_fusion.4
  8.9 4.4 %gather_fusion.1 = bf16[2,96,6144]{2,1,0:T(8,128)(2,1)} fusion(bf16[4,96,6144]{2,1,0:T(8,128)(2,1)} %bitcast.50, s32[1024]{0:T(1024)S(1)} %pad_clamp_fusion.1), kind=kCustom, calls=%fused_computation.5 | custom fusion | bytes 4718600 | tf_op jit(solution)/shard_map/jit(_take)/gather | solution.py:68
  13.3 2.6 %multiply_reduce_fusion = (f32[2,96]{1,0:T(2,128)S(1)}, bf16[2,96,128]{2,1,0:T(8,128)(2,1)S(1)}) fusion(bf16[2,96,128]{2,1,0:T(8,128)(2,1)S(1)} %gather_fusion.4, pred[2]{0:T(512)(128)(4,1)S(1)} %get-tuple-element.7, bf16[1,6144,1,128]{3,1,2,0:T(8,128)(2,1)S(1)} %copy-done, bf16[2,96,6144]{2,1,0:T(8,128)(2,1)} %gather_fusion.1), kind=kOutput, calls=%fused_computation.44 | convolution fusion | flops 303316800 | bytes 4031234 | tf_op jit(solution)/shard_map/msd,dh->msh/dot_general | solution.py:69
  16.8 4.2 %convolution_convert_fusion = bf16[2,96,6144]{2,1,0:T(8,128)(2,1)S(1)} fusion(bf16[1,6144,1,384]{3,1,2,0:T(8,128)(2,1)} %param.10, bf16[2,96,128]{2,1,0:T(8,128)(2,1)S(1)} %convolution_convert_fusion.2, bf16[2,96,128]{2,1,0:T(8,128)(2,1)S(1)} %fusion.16, bf16[2,96,128]{2,1,0:T(8,128)(2,1)S(1)} %fusion.15), kind=kOutput, calls=%fused_computation.8 | convolution fusion | flops 907591680 | bytes 7225344 | tf_op jit(solution)/shard_map/bsk,dk->sbd/dot_general | solution.py:81
  20.9 3.8 %copy.12 = bf16[4,24,2,6144]{3,2,1,0:T(2,128)(2,1)} copy(bf16[4,24,2,6144]{3,1,0,2:T(8,128)(2,1)S(1)} %bitcast.51) | data formatting | bytes 4718592 | tf_op jit(solution)/shard_map/reshape | solution.py:17
  24.7 4.8 %all-to-all-start = ((bf16[4,24,2,6144]{3,2,1,0:T(2,128)(2,1)}), bf16[4,24,2,6144]{3,2,1,0:T(2,128)(2,1)}, u32[]{:S(2)}, u32[]{:S(2)}) async-start(bf16[4,24,2,6144]{3,2,1,0:T(2,128)(2,1)} %copy.12), calls=%async_computation | async-start | bytes 4718592 | tf_op jit(solution)/shard_map/all_to_all | solution.py:18
  29.6 3.4 %fusion.7 = bf16[16,48,8,128]{3,2,1,0:T(8,128)(2,1)S(1)} fusion(bf16[4,96,128]{2,1,0:T(8,128)(2,1)S(1)} %convolution_convert_fusion.1, bf16[1,4,1,96,6144]{4,3,2,1,0:T(8,128)(2,1)} %param.7), kind=kOutput, calls=%fused_computation.18 | convolution fusion | flops 604766208 | bytes 6389760 | tf_op jit(solution)/shard_map/msc,msh->ch/dot_general | solution.py:65
  33.0 1.6 %copy.21 = bf16[16,48,8,128]{3,2,0,1:T(8,128)(2,1)} copy(bf16[16,48,8,128]{3,2,1,0:T(8,128)(2,1)S(1)} %fusion.7) | data formatting | bytes 3145728 | tf_op jit(solution)/shard_map/reshape | solution.py:17
  34.6 14.4 %all-to-all-done = bf16[4,24,2,6144]{3,2,1,0:T(2,128)(2,1)} async-done(((bf16[4,24,2,6144]{3,2,1,0:T(2,128)(2,1)}), bf16[4,24,2,6144]{3,2,1,0:T(2,128)(2,1)}, u32[]{:S(2)}, u32[]{:S(2)}) %all-to-all-start) | async-done | bytes 2359328 | tf_op jit(solution)/shard_map/all_to_all | solution.py:18
  48.9 32.0 %all-to-all-start.1 = ((bf16[48,128,128]{1,2,0:T(8,128)(2,1)}), bf16[48,128,128]{1,2,0:T(8,128)(2,1)S(1)}, u32[]{:S(2)}, u32[]{:S(2)}) async-start(bf16[48,128,128]{1,2,0:T(8,128)(2,1)} %bitcast.49), calls=%async_computation.1 | async-start | bytes 3145728 | tf_op jit(solution)/shard_map/all_to_all | solution.py:18
  81.0 4.3 %convert_element_type.51 = f32[4,24,2,6144]{3,2,1,0:T(2,128)S(1)} convert(bf16[4,24,2,6144]{3,2,1,0:T(2,128)(2,1)} %all-to-all-done) | non-fusion elementwise | flops 1179648 | bytes 7077888 | tf_op jit(solution)/shard_map/convert_element_type | solution.py:18
  85.3 1.2 fusion.22
  86.5 1.3 collective-permute-start
  87.8 28.0 %collective-permute-done = bf16[24,2,6144]{2,1,0:T(2,128)(2,1)S(1)} collective-permute-done((bf16[24,2,6144]{2,1,0:T(2,128)(2,1)S(1)}, bf16[24,2,6144]{2,1,0:T(2,128)(2,1)S(1)}, u32[]{:S(2)}, u32[]{:S(2)}) %collective-permute-start) | collective-permute-done | bytes 589856 | tf_op jit(solution)/shard_map/ppermute | solution.py:12
  115.8 0.8 copy-done.1
  116.6 23.2 %all-to-all-done.1 = bf16[48,128,128]{1,2,0:T(8,128)(2,1)S(1)} async-done(((bf16[48,128,128]{1,2,0:T(8,128)(2,1)}), bf16[48,128,128]{1,2,0:T(8,128)(2,1)S(1)}, u32[]{:S(2)}, u32[]{:S(2)}) %all-to-all-start.1) | async-done | bytes 1572896 | tf_op jit(solution)/shard_map/all_to_all | solution.py:18
  140.0 0.7 copy.15
  140.7 2.3 %copy.23 = bf16[1,1,24,2,6144]{4,3,2,1,0:T(2,128)(2,1)} copy(bf16[1,1,24,2,6144]{4,3,2,1,0:T(2,128)(2,1)} %bitcast.52) | data formatting | bytes 1179648
  (16 shorter events, 3.4 us)
Async XLA Ops:
  0.6 12.7 %copy-start = (bf16[1,6144,1,128]{3,1,2,0:T(8,128)(2,1)S(1)}, bf16[1,6144,1,128]{3,1,2,0:T(8,128)(2,1)}, u32[]{:S(2)}) copy-start(bf16[1,6144,1,128]{3,1,2,0:T(8,128)(2,1)} %param.9) | copy-start | bytes 4718596
  24.7 24.2 %all-to-all-start = ((bf16[4,24,2,6144]{3,2,1,0:T(2,128)(2,1)}), bf16[4,24,2,6144]{3,2,1,0:T(2,128)(2,1)}, u32[]{:S(2)}, u32[]{:S(2)}) async-start(bf16[4,24,2,6144]{3,2,1,0:T(2,128)(2,1)} %copy.12), calls=%async_computation | async-start | bytes 4718592 | tf_op jit(solution)/shard_map/all_to_all | solution.py:18
  48.9 90.8 %all-to-all-start.1 = ((bf16[48,128,128]{1,2,0:T(8,128)(2,1)}), bf16[48,128,128]{1,2,0:T(8,128)(2,1)S(1)}, u32[]{:S(2)}, u32[]{:S(2)}) async-start(bf16[48,128,128]{1,2,0:T(8,128)(2,1)} %bitcast.49), calls=%async_computation.1 | async-start | bytes 3145728 | tf_op jit(solution)/shard_map/all_to_all | solution.py:18
  86.5 29.3 %collective-permute-start = (bf16[24,2,6144]{2,1,0:T(2,128)(2,1)S(1)}, bf16[24,2,6144]{2,1,0:T(2,128)(2,1)S(1)}, u32[]{:S(2)}, u32[]{:S(2)}) collective-permute-start(bf16[24,2,6144]{2,1,0:T(2,128)(2,1)S(1)} %fusion.22), channel_id=1, source_target_pairs={{192,0},{384,192},{576,384},{193,1},{385,193},{577,385},{194,2},{3... | collective-permute-start | bytes 1769480 | tf_op jit(solution)/shard_map/ppermute | solution.py:12
  115.8 0.8 copy-start.1

commit v2 on v1

--- a/solution.py
+++ b/solution.py
@@ -1,9 +1,10 @@
 import jax
 import jax.numpy as jnp
 from jax import lax
-from jax.sharding import PartitionSpec as P
+from jax.sharding import Mesh, PartitionSpec as P
 
 BMICRO = 2
+DP_PARTS = ("dp_y", "dp_z", "dp_core")
 
 
 def shifted(block, axis, distance):
@@ -12,17 +13,13 @@
     return lax.ppermute(block, axis, route)
 
 
-def exchange(block, axis):
+def rotated(block, axis, shift):
     n = lax.axis_size(axis)
-    parts = block.reshape(n, block.shape[0] // n, *block.shape[1:])
-    return lax.all_to_all(parts, axis, 0, 0, tiled=True).astype(jnp.float32)
+    return lax.ppermute(block, axis, [(i, (i + shift) % n) for i in range(n)])
 
 
-def ordered_sum(parts):
-    total = parts[0]
-    for index in range(1, parts.shape[0]):
-        total = total + parts[index]
-    return total
+def swapped(block, axis):
+    return lax.ppermute(block, axis, [(0, 1), (1, 0)])
 
 
 def head_forward(queries, key_rows, values):
@@ -52,22 +49,51 @@
     return jnp.concatenate([grad_query, grad_keys, grad_values], axis=1).astype(jnp.bfloat16)
 
 
+def weight_grad_sum(weight_part):
+    n_y, n_z, n_core = (lax.axis_size(a) for a in DP_PARTS)
+    rows = weight_part.shape[0] // (n_y * n_z * n_core)
+    blocks = weight_part.reshape(n_y, n_z, n_core, rows, weight_part.shape[1])
+    core = lax.axis_index("dp_core")
+    keep = lax.dynamic_index_in_dim(blocks, core, axis=2, keepdims=False)
+    give = lax.dynamic_index_in_dim(blocks, 1 - core, axis=2, keepdims=False)
+    pair = keep + swapped(give, "dp_core")
+    y = lax.axis_index("dp_y")
+    keep = lax.dynamic_index_in_dim(pair, y, axis=0, keepdims=False)
+    give = lax.dynamic_index_in_dim(pair, 1 - y, axis=0, keepdims=False)
+    quad = keep + swapped(give.astype(jnp.bfloat16), "dp_y").astype(jnp.float32)
+    z = lax.axis_index("dp_z")
+    low = quad.astype(jnp.bfloat16)
+    ring = lax.dynamic_slice_in_dim(jnp.concatenate([low, low], axis=0), z, n_z, axis=0)
+    total = lax.dynamic_index_in_dim(quad, z, axis=0, keepdims=False)
+    for shift in range(1, n_z):
+        total = total + rotated(ring[shift], "dp_z", shift).astype(jnp.float32)
+    return total
+
+
+def input_grad_sum(partials):
+    n = partials.shape[0]
+    total = partials[0].astype(jnp.float32)
+    for shift in range(1, n):
+        total = total + rotated(partials[shift], "tensor", shift).astype(jnp.float32)
+    return total
+
+
 def body(grad_out, qkv_saved, w_out, w_qkv, plan):
     gradients = grad_out[0, :, 0]
     saved_qkv = qkv_saved[0, :, 0, :, 0]
     out_proj = w_out[0, :, 0]
     qkv_proj = w_qkv[0, :, 0]
     head_size = out_proj.shape[1]
+    seq_len = gradients.shape[1]
     queries = saved_qkv[:, :, :head_size]
     key_rows = saved_qkv[:, :, head_size : 2 * head_size]
     values = saved_qkv[:, :, 2 * head_size :]
     softmax, soft_low, attended = jax.vmap(head_forward)(queries, key_rows, values)
     weight_part = jnp.einsum("msc,msh->ch", gradients, attended, preferred_element_type=jnp.float32)
-    weight_grad = jnp.sum(exchange(weight_part.astype(jnp.bfloat16), "dp"), axis=0)
+    weight_grad = weight_grad_sum(weight_part)
     current = plan[0, :BMICRO]
-    grad_current = jnp.take(gradients, current, axis=0)
     grad_heads = jnp.einsum(
-        "msd,dh->msh", grad_current, out_proj, preferred_element_type=jnp.float32
+        "msd,dh->msh", gradients, out_proj, preferred_element_type=jnp.float32
     ).astype(jnp.bfloat16)
     grad_qkv = jax.vmap(head_backward)(
         jnp.take(queries, current, axis=0),
@@ -76,21 +102,31 @@
         jnp.take(softmax, current, axis=0),
         jnp.take(soft_low, current, axis=0),
         jnp.take(attended, current, axis=0),
-        grad_heads,
+        jnp.take(grad_heads, current, axis=0),
     )
+    n_tensor = lax.axis_size("tensor")
+    share_rows = seq_len // n_tensor
+    start = lax.axis_index("tensor") * share_rows
+    grad_qkv = lax.dynamic_slice_in_dim(jnp.concatenate([grad_qkv, grad_qkv], axis=1), start, seq_len, axis=1)
     partials = jnp.einsum("bsk,dk->sbd", grad_qkv, qkv_proj, preferred_element_type=jnp.float32)
-    own_rows = ordered_sum(exchange(partials.astype(jnp.bfloat16), "tensor"))
+    partials = partials.astype(jnp.bfloat16).reshape(n_tensor, share_rows, *partials.shape[1:])
+    own_rows = input_grad_sum(partials)
     received = shifted(own_rows.astype(jnp.bfloat16), "pipe", -1)
     return (received[None, None], weight_grad[None, :, None, :])
 
 
 def solution(mesh):
+    n_pipe, n_dp, n_tensor = (mesh.shape[a] for a in ("pipe", "dp", "tensor"))
+    n_y = 2
+    n_core = 2
+    parts = mesh.devices.reshape(n_pipe, n_y, n_dp // (n_y * n_core), n_core, n_tensor)
+    staged = Mesh(parts, ("pipe", *DP_PARTS, "tensor"))
     in_specs = (
-        P("pipe", None, "dp", None, None),
-        P("pipe", None, "dp", None, "tensor", None),
+        P("pipe", None, DP_PARTS, None, None),
+        P("pipe", None, DP_PARTS, None, "tensor", None),
         P("pipe", None, "tensor", None),
         P("pipe", None, "tensor", None),
         P("pipe", None),
     )
-    out_specs = (P("pipe", "dp", "tensor", None, None), P("pipe", "dp", "tensor", None))
-    return jax.shard_map(body, mesh=mesh, in_specs=in_specs, out_specs=out_specs, check_vma=False)
+    out_specs = (P("pipe", DP_PARTS, "tensor", None, None), P("pipe", DP_PARTS, "tensor", None))
+    return jax.shard_map(body, mesh=staged, in_specs=in_specs, out_specs=out_specs, check_vma=False)

time: 144 us -> 148 us (1.028)
  the two profiles are of different devices: /device:TPU:1 before, /device:TPU:40 now
where the time goes in v2:
time: 148 us; the launch traced here: 147 us
  starting transfers between devices  78.2 us (53%)
  local copies, waits for them, and re-layouts  27.5 us (19%)
  waiting for transfers between devices  19.4 us (13%)
  matrix products  16.2 us (11%)
  other arithmetic  4.71 us (3%)
    ppermute x14, starting transfers between devices, rotated(): return lax.ppermute(block, axis, [(i, (i + shift) % n) for i in range(n)])  70.2 us
    ppermute x14, waiting for transfers between devices, rotated(): return lax.ppermute(block, axis, [(i, (i + shift) % n) for i in range(n)])  17.5 us
    dynamic_slice x2, local copies, waits for them, and re-layouts, weight_grad_sum(): keep = lax.dynamic_index_in_dim(blocks, core, axis=2, keepdims=False)  10.7 us
    reshape x1, local copies, waits for them, and re-layouts, weight_grad_sum(): blocks = weight_part.reshape(n_y, n_z, n_core, rows, weight_part.shape[1])  5.47 us
    dot_general x1, matrix products, body(): jnp.einsum('msc,msh->ch', gradients, attended, preferred_element_type=jnp...  5 us
    ppermute x2, starting transfers between devices, swapped(): return lax.ppermute(block, axis, [(0, 1), (1, 0)])  4.77 us
    dot_general x1, matrix products, body(): jnp.einsum('bsk,dk->sbd', grad_qkv, qkv_proj, preferred_element_type=jnp....  4.17 us
    dot_general x1, matrix products, body(): jnp.einsum('msd,dh->msh', gradients, out_proj, preferred_element_type=jnp...  3.72 us
  transfers between devices with their start and end apart: 17, of which 5 were waited for; matrix products, arithmetic and copies ran while one was open for 16% of the time, Pallas kernels for 0%

profile of v2, /device:TPU:40, one launch (start us, length us, event | category | flops | bytes accessed | tf_op | source)
XLA Modules:
  0.0 147.1 jit_solution(3805920510574820717)
XLA Ops:
  3.1 5.0 %convolution_bitcast_fusion = f32[6144,128]{0,1:T(8,128)} fusion(bf16[4,96,128]{2,1,0:T(8,128)(2,1)S(1)} %convolution_convert_fusion.1, bf16[1,4,1,96,6144]{4,3,2,1,0:T(8,128)(2,1)} %param.7), kind=kOutput, calls=%fused_computation.9 | convolution fusion | flops 603979776 | bytes 7962624 | tf_op jit(solution)/shard_map/msc,msh->ch/dot_general | solution.py:92
  8.1 5.5 %reshape.59 = f32[2,12,2,128,128]{3,2,1,0,4:T(2,128)} reshape(f32[6144,128]{0,1:T(8,128)} %convolution_bitcast_fusion) | data formatting | bytes 6291456 | tf_op jit(solution)/shard_map/reshape | solution.py:55
  13.6 7.2 %constant_dynamic-slice_fusion.1 = (f32[2,12,1,128,128]{3,2,1,0,4:T(1,128)}, f32[2,12,1,128,128]{3,2,1,0,4:T(1,128)S(1)}) fusion(f32[2,12,2,128,128]{3,2,1,0,4:T(2,128)} %reshape.59, s32[]{:T(128)S(6)} %select_n.66, s32[]{:T(128)S(6)} %select_n.67), kind=kLoop, calls=%fused_computation.90 | loop fusion | bytes 6291464 | tf_op jit(solution)/shard_map/jit(dynamic_index_in_dim)/dynamic_slice | solution.py:57
  20.8 2.9 %copy.10 = f32[2,12,1,128,128]{4,3,1,0,2:T(8,128)} copy(f32[2,12,1,128,128]{3,2,1,0,4:T(1,128)S(1)} %get-tuple-element.12) | data formatting | bytes 3145728 | tf_op jit(solution)/shard_map/jit(dynamic_index_in_dim)/dynamic_slice | solution.py:58
  27.3 3.7 %fusion.10 = bf16[4,96,128]{2,1,0:T(8,128)(2,1)S(1)} fusion(bf16[1,6144,1,128]{3,1,2,0:T(8,128)(2,1)S(1)} %copy-done, bf16[1,4,1,96,6144]{4,3,2,1,0:T(8,128)(2,1)} %param.7), kind=kOutput, calls=%fused_computation.22 | convolution fusion | flops 604028928 | bytes 6389760 | tf_op jit(solution)/shard_map/msd,dh->msh/dot_general | solution.py:95
  35.5 4.2 %fusion.1 = bf16[96,2,6144]{2,0,1:T(8,128)(2,1)S(1)} fusion(bf16[1,6144,1,384]{3,1,2,0:T(8,128)(2,1)} %param.10, s32[]{:T(128)S(6)} %select_n.65, bf16[2,96,128]{2,1,0:T(8,128)(2,1)S(1)} %fusion.17, bf16[2,96,128]{2,1,0:T(8,128)(2,1)S(1)} %fusion.18, bf16[2,96,128]{2,1,0:T(8,128)(2,1)S(1)} %convolution_convert_fusion.2), kind=kOutput, calls=%fused_computation.10 | convolution fusion | flops 908034048 | bytes 7225348 | tf_op jit(solution)/shard_map/bsk,dk->sbd/dot_general | solution.py:111
  41.6 3.4 %collective-permute-start = (bf16[24,2,6144]{2,0,1:T(8,128)(2,1)}, bf16[24,2,6144]{2,0,1:T(8,128)(2,1)}, u32[]{:S(2)}, u32[]{:S(2)}) collective-permute-start(bf16[24,2,6144]{2,0,1:T(8,128)(2,1)} %get-tuple-element.13), channel_id=1, source_target_pairs={{0,1},{1,2},{2,3},{3,0},{4,5},{5,6},{6,7},{7,4},{8,9},{9,10},{10,1... | collective-permute-start | bytes 1769480 | tf_op jit(solution)/shard_map/ppermute | solution.py:18
  45.0 4.7 %collective-permute-start.1 = (bf16[24,2,6144]{2,0,1:T(8,128)(2,1)}, bf16[24,2,6144]{2,0,1:T(8,128)(2,1)}, u32[]{:S(2)}, u32[]{:S(2)}) collective-permute-start(bf16[24,2,6144]{2,0,1:T(8,128)(2,1)} %get-tuple-element.15), channel_id=1, source_target_pairs={{0,2},{1,3},{2,0},{3,1},{4,6},{5,7},{6,4},{7,5},{8,10},{9,11},{10,... | collective-permute-start | bytes 1769480 | tf_op jit(solution)/shard_map/ppermute | solution.py:18
  49.7 3.4 %collective-permute-start.2 = (bf16[24,2,6144]{2,0,1:T(8,128)(2,1)}, bf16[24,2,6144]{2,0,1:T(8,128)(2,1)}, u32[]{:S(2)}, u32[]{:S(2)}) collective-permute-start(bf16[24,2,6144]{2,0,1:T(8,128)(2,1)} %get-tuple-element.14), channel_id=1, source_target_pairs={{0,3},{1,0},{2,1},{3,2},{4,7},{5,4},{6,5},{7,6},{8,11},{9,8},{10,9... | collective-permute-start | bytes 1769480 | tf_op jit(solution)/shard_map/ppermute | solution.py:18
  53.1 3.5 %copy.9 = f32[2,12,1,128,128]{4,3,1,0,2:T(8,128)S(1)} copy(f32[2,12,1,128,128]{3,2,1,0,4:T(1,128)} %get-tuple-element.11) | data formatting | bytes 3145728 | tf_op jit(solution)/shard_map/jit(dynamic_index_in_dim)/dynamic_slice | solution.py:57
  58.3 2.9 %collective-permute-start.5 = (bf16[12,128,128]{2,1,0:T(8,128)(2,1)S(1)}, bf16[12,128,128]{2,1,0:T(8,128)(2,1)S(1)}, u32[]{:S(2)}, u32[]{:S(2)}) collective-permute-start(bf16[12,128,128]{2,1,0:T(8,128)(2,1)S(1)} %fusion.19), channel_id=1, source_target_pairs={{0,96},{96,0},{1,97},{97,1},{2,98},{98,2},{3,99},{99,3},{4,100},{1... | collective-permute-start | bytes 1179656 | tf_op jit(solution)/shard_map/ppermute | solution.py:22
  61.2 13.2 %collective-permute-done.1 = bf16[24,2,6144]{2,0,1:T(8,128)(2,1)} collective-permute-done((bf16[24,2,6144]{2,0,1:T(8,128)(2,1)}, bf16[24,2,6144]{2,0,1:T(8,128)(2,1)}, u32[]{:S(2)}, u32[]{:S(2)}) %collective-permute-start.1) | collective-permute-done | bytes 589856 | tf_op jit(solution)/shard_map/ppermute | solution.py:18
  77.8 3.3 %collective-permute-start.3 = (bf16[24,2,6144]{2,0,1:T(8,128)(2,1)S(1)}, bf16[24,2,6144]{2,0,1:T(8,128)(2,1)S(1)}, u32[]{:S(2)}, u32[]{:S(2)}) collective-permute-start(bf16[24,2,6144]{2,0,1:T(8,128)(2,1)S(1)} %add_convert_fusion), channel_id=1, source_target_pairs={{192,0},{384,192},{576,384},{193,1},{385,193},{577,385},{194,2},{3... | collective-permute-start | bytes 1769480 | tf_op jit(solution)/shard_map/ppermute | solution.py:13
  83.3 13.9 %collective-permute-start.10 = (bf16[128,128]{1,0:T(8,128)(2,1)S(1)}, bf16[128,128]{1,0:T(8,128)(2,1)S(1)}, u32[]{:S(2)}, u32[]{:S(2)}) collective-permute-start(bf16[128,128]{1,0:T(8,128)(2,1)S(1)} %get-tuple-element.22), channel_id=1, source_target_pairs={{0,40},{8,48},{16,56},{24,64},{32,72},{40,80},{48,88},{56,0},{64,8... | collective-permute-start | bytes 98312 | tf_op jit(solution)/shard_map/ppermute | solution.py:18
  97.3 10.0 %collective-permute-start.11 = (bf16[128,128]{1,0:T(8,128)(2,1)S(1)}, bf16[128,128]{1,0:T(8,128)(2,1)S(1)}, u32[]{:S(2)}, u32[]{:S(2)}) collective-permute-start(bf16[128,128]{1,0:T(8,128)(2,1)S(1)} %get-tuple-element.21), channel_id=1, source_target_pairs={{0,48},{8,56},{16,64},{24,72},{32,80},{40,88},{48,0},{56,8},{64,16... | collective-permute-start | bytes 98312 | tf_op jit(solution)/shard_map/ppermute | solution.py:18
  107.3 3.7 %collective-permute-start.12 = (bf16[128,128]{1,0:T(8,128)(2,1)S(1)}, bf16[128,128]{1,0:T(8,128)(2,1)S(1)}, u32[]{:S(2)}, u32[]{:S(2)}) collective-permute-start(bf16[128,128]{1,0:T(8,128)(2,1)S(1)} %get-tuple-element.20), channel_id=1, source_target_pairs={{0,56},{8,64},{16,72},{24,80},{32,88},{40,0},{48,8},{56,16},{64,24... | collective-permute-start | bytes 98312 | tf_op jit(solution)/shard_map/ppermute | solution.py:18
  110.9 2.9 %collective-permute-start.13 = (bf16[128,128]{1,0:T(8,128)(2,1)S(1)}, bf16[128,128]{1,0:T(8,128)(2,1)S(1)}, u32[]{:S(2)}, u32[]{:S(2)}) collective-permute-start(bf16[128,128]{1,0:T(8,128)(2,1)S(1)} %get-tuple-element.19), channel_id=1, source_target_pairs={{0,64},{8,72},{16,80},{24,88},{32,0},{40,8},{48,16},{56,24},{64,32... | collective-permute-start | bytes 98312 | tf_op jit(solution)/shard_map/ppermute | solution.py:18
  113.9 8.1 %collective-permute-start.14 = (bf16[128,128]{1,0:T(8,128)(2,1)S(1)}, bf16[128,128]{1,0:T(8,128)(2,1)S(1)}, u32[]{:S(2)}, u32[]{:S(2)}) collective-permute-start(bf16[128,128]{1,0:T(8,128)(2,1)S(1)} %get-tuple-element.18), channel_id=1, source_target_pairs={{0,72},{8,80},{16,88},{24,0},{32,8},{40,16},{48,24},{56,32},{64,40... | collective-permute-start | bytes 98312 | tf_op jit(solution)/shard_map/ppermute | solution.py:18
  121.9 2.5 %collective-permute-start.15 = (bf16[128,128]{1,0:T(8,128)(2,1)S(1)}, bf16[128,128]{1,0:T(8,128)(2,1)S(1)}, u32[]{:S(2)}, u32[]{:S(2)}) collective-permute-start(bf16[128,128]{1,0:T(8,128)(2,1)S(1)} %get-tuple-element.17), channel_id=1, source_target_pairs={{0,80},{8,88},{16,0},{24,8},{32,16},{40,24},{48,32},{56,40},{64,48... | collective-permute-start | bytes 98312 | tf_op jit(solution)/shard_map/ppermute | solution.py:18
  124.5 3.0 %collective-permute-start.16 = (bf16[128,128]{1,0:T(8,128)(2,1)S(1)}, bf16[128,128]{1,0:T(8,128)(2,1)S(1)}, u32[]{:S(2)}, u32[]{:S(2)}) collective-permute-start(bf16[128,128]{1,0:T(8,128)(2,1)S(1)} %get-tuple-element.26), channel_id=1, source_target_pairs={{0,88},{8,0},{16,8},{24,16},{32,24},{40,32},{48,40},{56,48},{64,56... | collective-permute-start | bytes 98312 | tf_op jit(solution)/shard_map/ppermute | solution.py:18
  127.5 2.8 %collective-permute-start.6 = (bf16[128,128]{1,0:T(8,128)(2,1)S(1)}, bf16[128,128]{1,0:T(8,128)(2,1)S(1)}, u32[]{:S(2)}, u32[]{:S(2)}) collective-permute-start(bf16[128,128]{1,0:T(8,128)(2,1)S(1)} %get-tuple-element.16), channel_id=1, source_target_pairs={{0,8},{8,16},{16,24},{24,32},{32,40},{40,48},{48,56},{56,64},{64,7... | collective-permute-start | bytes 98312 | tf_op jit(solution)/shard_map/ppermute | solution.py:18
  130.4 4.2 %collective-permute-start.7 = (bf16[128,128]{1,0:T(8,128)(2,1)S(1)}, bf16[128,128]{1,0:T(8,128)(2,1)S(1)}, u32[]{:S(2)}, u32[]{:S(2)}) collective-permute-start(bf16[128,128]{1,0:T(8,128)(2,1)S(1)} %get-tuple-element.25), channel_id=1, source_target_pairs={{0,16},{8,24},{16,32},{24,40},{32,48},{40,56},{48,64},{56,72},{64,... | collective-permute-start | bytes 98312 | tf_op jit(solution)/shard_map/ppermute | solution.py:18
  136.5 5.7 %collective-permute-start.9 = (bf16[128,128]{1,0:T(8,128)(2,1)S(1)}, bf16[128,128]{1,0:T(8,128)(2,1)S(1)}, u32[]{:S(2)}, u32[]{:S(2)}) collective-permute-start(bf16[128,128]{1,0:T(8,128)(2,1)S(1)} %get-tuple-element.23), channel_id=1, source_target_pairs={{0,32},{8,40},{16,48},{24,56},{32,64},{40,72},{48,80},{56,88},{64,... | collective-permute-start | bytes 98312 | tf_op jit(solution)/shard_map/ppermute | solution.py:18
  144.1 2.3 %collective-permute-done.9 = bf16[128,128]{1,0:T(8,128)(2,1)S(1)} collective-permute-done((bf16[128,128]{1,0:T(8,128)(2,1)S(1)}, bf16[128,128]{1,0:T(8,128)(2,1)S(1)}, u32[]{:S(2)}, u32[]{:S(2)}) %collective-permute-start.9) | collective-permute-done | bytes 32800 | tf_op jit(solution)/shard_map/ppermute | solution.py:18
  (53 shorter events, 24.1 us)
Async XLA Ops:
  0.6 26.6 %copy-start = (bf16[1,6144,1,128]{3,1,2,0:T(8,128)(2,1)S(1)}, bf16[1,6144,1,128]{3,1,2,0:T(8,128)(2,1)}, u32[]{:S(2)}) copy-start(bf16[1,6144,1,128]{3,1,2,0:T(8,128)(2,1)} %param.9) | copy-start | bytes 4718596
  20.8 5.8 %copy-start.2 = (s32[1,4]{1,0:T(1,128)S(1)}, s32[1,4]{1,0:T(1,128)}, u32[]{:S(2)}) copy-start(s32[1,4]{1,0:T(1,128)} %param.11) | copy-start | bytes 52
  23.7 32.9 %collective-permute-start.4 = (f32[2,12,128,128]{3,2,1,0:T(8,128)}, f32[2,12,128,128]{3,2,1,0:T(8,128)}, u32[]{:S(2)}, u32[]{:S(2)}) collective-permute-start(f32[2,12,128,128]{3,2,1,0:T(8,128)} %bitcast.93), channel_id=1, source_target_pairs={{0,4},{4,0},{1,5},{5,1},{2,6},{6,2},{3,7},{7,3},{8,12},{12,8},{9,1... | collective-permute-start | bytes 4718600 | tf_op jit(solution)/shard_map/ppermute | solution.py:22
  39.7 2.0 %copy-start.1 = (bf16[96,2,6144]{2,0,1:T(8,128)(2,1)}, bf16[96,2,6144]{2,0,1:T(8,128)(2,1)S(1)}, u32[]{:S(2)}) copy-start(bf16[96,2,6144]{2,0,1:T(8,128)(2,1)S(1)} %fusion.1) | copy-start | bytes 7077892
  41.6 19.5 %collective-permute-start = (bf16[24,2,6144]{2,0,1:T(8,128)(2,1)}, bf16[24,2,6144]{2,0,1:T(8,128)(2,1)}, u32[]{:S(2)}, u32[]{:S(2)}) collective-permute-start(bf16[24,2,6144]{2,0,1:T(8,128)(2,1)} %get-tuple-element.13), channel_id=1, source_target_pairs={{0,1},{1,2},{2,3},{3,0},{4,5},{5,6},{6,7},{7,4},{8,9},{9,10},{10,1... | collective-permute-start | bytes 1769480 | tf_op jit(solution)/shard_map/ppermute | solution.py:18
  45.0 29.4 %collective-permute-start.1 = (bf16[24,2,6144]{2,0,1:T(8,128)(2,1)}, bf16[24,2,6144]{2,0,1:T(8,128)(2,1)}, u32[]{:S(2)}, u32[]{:S(2)}) collective-permute-start(bf16[24,2,6144]{2,0,1:T(8,128)(2,1)} %get-tuple-element.15), channel_id=1, source_target_pairs={{0,2},{1,3},{2,0},{3,1},{4,6},{5,7},{6,4},{7,5},{8,10},{9,11},{10,... | collective-permute-start | bytes 1769480 | tf_op jit(solution)/shard_map/ppermute | solution.py:18
  49.7 26.3 %collective-permute-start.2 = (bf16[24,2,6144]{2,0,1:T(8,128)(2,1)}, bf16[24,2,6144]{2,0,1:T(8,128)(2,1)}, u32[]{:S(2)}, u32[]{:S(2)}) collective-permute-start(bf16[24,2,6144]{2,0,1:T(8,128)(2,1)} %get-tuple-element.14), channel_id=1, source_target_pairs={{0,3},{1,0},{2,1},{3,2},{4,7},{5,4},{6,5},{7,6},{8,11},{9,8},{10,9... | collective-permute-start | bytes 1769480 | tf_op jit(solution)/shard_map/ppermute | solution.py:18
  58.3 24.7 %collective-permute-start.5 = (bf16[12,128,128]{2,1,0:T(8,128)(2,1)S(1)}, bf16[12,128,128]{2,1,0:T(8,128)(2,1)S(1)}, u32[]{:S(2)}, u32[]{:S(2)}) collective-permute-start(bf16[12,128,128]{2,1,0:T(8,128)(2,1)S(1)} %fusion.19), channel_id=1, source_target_pairs={{0,96},{96,0},{1,97},{97,1},{2,98},{98,2},{3,99},{99,3},{4,100},{1... | collective-permute-start | bytes 1179656 | tf_op jit(solution)/shard_map/ppermute | solution.py:22
  77.8 36.0 %collective-permute-start.3 = (bf16[24,2,6144]{2,0,1:T(8,128)(2,1)S(1)}, bf16[24,2,6144]{2,0,1:T(8,128)(2,1)S(1)}, u32[]{:S(2)}, u32[]{:S(2)}) collective-permute-start(bf16[24,2,6144]{2,0,1:T(8,128)(2,1)S(1)} %add_convert_fusion), channel_id=1, source_target_pairs={{192,0},{384,192},{576,384},{193,1},{385,193},{577,385},{194,2},{3... | collective-permute-start | bytes 1769480 | tf_op jit(solution)/shard_map/ppermute | solution.py:13
  83.3 38.6 %collective-permute-start.10 = (bf16[128,128]{1,0:T(8,128)(2,1)S(1)}, bf16[128,128]{1,0:T(8,128)(2,1)S(1)}, u32[]{:S(2)}, u32[]{:S(2)}) collective-permute-start(bf16[128,128]{1,0:T(8,128)(2,1)S(1)} %get-tuple-element.22), channel_id=1, source_target_pairs={{0,40},{8,48},{16,56},{24,64},{32,72},{40,80},{48,88},{56,0},{64,8... | collective-permute-start | bytes 98312 | tf_op jit(solution)/shard_map/ppermute | solution.py:18
  97.3 27.2 %collective-permute-start.11 = (bf16[128,128]{1,0:T(8,128)(2,1)S(1)}, bf16[128,128]{1,0:T(8,128)(2,1)S(1)}, u32[]{:S(2)}, u32[]{:S(2)}) collective-permute-start(bf16[128,128]{1,0:T(8,128)(2,1)S(1)} %get-tuple-element.21), channel_id=1, source_target_pairs={{0,48},{8,56},{16,64},{24,72},{32,80},{40,88},{48,0},{56,8},{64,16... | collective-permute-start | bytes 98312 | tf_op jit(solution)/shard_map/ppermute | solution.py:18
  107.3 20.3 %collective-permute-start.12 = (bf16[128,128]{1,0:T(8,128)(2,1)S(1)}, bf16[128,128]{1,0:T(8,128)(2,1)S(1)}, u32[]{:S(2)}, u32[]{:S(2)}) collective-permute-start(bf16[128,128]{1,0:T(8,128)(2,1)S(1)} %get-tuple-element.20), channel_id=1, source_target_pairs={{0,56},{8,64},{16,72},{24,80},{32,88},{40,0},{48,8},{56,16},{64,24... | collective-permute-start | bytes 98312 | tf_op jit(solution)/shard_map/ppermute | solution.py:18
  110.9 19.4 %collective-permute-start.13 = (bf16[128,128]{1,0:T(8,128)(2,1)S(1)}, bf16[128,128]{1,0:T(8,128)(2,1)S(1)}, u32[]{:S(2)}, u32[]{:S(2)}) collective-permute-start(bf16[128,128]{1,0:T(8,128)(2,1)S(1)} %get-tuple-element.19), channel_id=1, source_target_pairs={{0,64},{8,72},{16,80},{24,88},{32,0},{40,8},{48,16},{56,24},{64,32... | collective-permute-start | bytes 98312 | tf_op jit(solution)/shard_map/ppermute | solution.py:18
  113.9 20.7 %collective-permute-start.14 = (bf16[128,128]{1,0:T(8,128)(2,1)S(1)}, bf16[128,128]{1,0:T(8,128)(2,1)S(1)}, u32[]{:S(2)}, u32[]{:S(2)}) collective-permute-start(bf16[128,128]{1,0:T(8,128)(2,1)S(1)} %get-tuple-element.18), channel_id=1, source_target_pairs={{0,72},{8,80},{16,88},{24,0},{32,8},{40,16},{48,24},{56,32},{64,40... | collective-permute-start | bytes 98312 | tf_op jit(solution)/shard_map/ppermute | solution.py:18
  121.9 14.6 %collective-permute-start.15 = (bf16[128,128]{1,0:T(8,128)(2,1)S(1)}, bf16[128,128]{1,0:T(8,128)(2,1)S(1)}, u32[]{:S(2)}, u32[]{:S(2)}) collective-permute-start(bf16[128,128]{1,0:T(8,128)(2,1)S(1)} %get-tuple-element.17), channel_id=1, source_target_pairs={{0,80},{8,88},{16,0},{24,8},{32,16},{40,24},{48,32},{56,40},{64,48... | collective-permute-start | bytes 98312 | tf_op jit(solution)/shard_map/ppermute | solution.py:18
  124.5 19.2 %collective-permute-start.16 = (bf16[128,128]{1,0:T(8,128)(2,1)S(1)}, bf16[128,128]{1,0:T(8,128)(2,1)S(1)}, u32[]{:S(2)}, u32[]{:S(2)}) collective-permute-start(bf16[128,128]{1,0:T(8,128)(2,1)S(1)} %get-tuple-element.26), channel_id=1, source_target_pairs={{0,88},{8,0},{16,8},{24,16},{32,24},{40,32},{48,40},{56,48},{64,56... | collective-permute-start | bytes 98312 | tf_op jit(solution)/shard_map/ppermute | solution.py:18
  127.5 16.2 %collective-permute-start.6 = (bf16[128,128]{1,0:T(8,128)(2,1)S(1)}, bf16[128,128]{1,0:T(8,128)(2,1)S(1)}, u32[]{:S(2)}, u32[]{:S(2)}) collective-permute-start(bf16[128,128]{1,0:T(8,128)(2,1)S(1)} %get-tuple-element.16), channel_id=1, source_target_pairs={{0,8},{8,16},{16,24},{24,32},{32,40},{40,48},{48,56},{56,64},{64,7... | collective-permute-start | bytes 98312 | tf_op jit(solution)/shard_map/ppermute | solution.py:18
  130.4 13.3 %collective-permute-start.7 = (bf16[128,128]{1,0:T(8,128)(2,1)S(1)}, bf16[128,128]{1,0:T(8,128)(2,1)S(1)}, u32[]{:S(2)}, u32[]{:S(2)}) collective-permute-start(bf16[128,128]{1,0:T(8,128)(2,1)S(1)} %get-tuple-element.25), channel_id=1, source_target_pairs={{0,16},{8,24},{16,32},{24,40},{32,48},{40,56},{48,64},{56,72},{64,... | collective-permute-start | bytes 98312 | tf_op jit(solution)/shard_map/ppermute | solution.py:18
  134.6 9.5 %collective-permute-start.8 = (bf16[128,128]{1,0:T(8,128)(2,1)S(1)}, bf16[128,128]{1,0:T(8,128)(2,1)S(1)}, u32[]{:S(2)}, u32[]{:S(2)}) collective-permute-start(bf16[128,128]{1,0:T(8,128)(2,1)S(1)} %get-tuple-element.24), channel_id=1, source_target_pairs={{0,24},{8,32},{16,40},{24,48},{32,56},{40,64},{48,72},{56,80},{64,... | collective-permute-start | bytes 98312 | tf_op jit(solution)/shard_map/ppermute | solution.py:18
  136.5 9.8 %collective-permute-start.9 = (bf16[128,128]{1,0:T(8,128)(2,1)S(1)}, bf16[128,128]{1,0:T(8,128)(2,1)S(1)}, u32[]{:S(2)}, u32[]{:S(2)}) collective-permute-start(bf16[128,128]{1,0:T(8,128)(2,1)S(1)} %get-tuple-element.23), channel_id=1, source_target_pairs={{0,32},{8,40},{16,48},{24,56},{32,64},{40,72},{48,80},{56,88},{64,... | collective-permute-start | bytes 98312 | tf_op jit(solution)/shard_map/ppermute | solution.py:18

commit v3 on v1

--- a/solution.py
+++ b/solution.py
@@ -1,9 +1,11 @@
 import jax
 import jax.numpy as jnp
 from jax import lax
-from jax.sharding import PartitionSpec as P
+from jax.sharding import Mesh, PartitionSpec as P
 
 BMICRO = 2
+DP_PARTS = ("dp_y", "dp_z", "dp_core")
+DP_FAR = ("dp_y", "dp_z")
 
 
 def shifted(block, axis, distance):
@@ -15,14 +17,24 @@
 def exchange(block, axis):
     n = lax.axis_size(axis)
     parts = block.reshape(n, block.shape[0] // n, *block.shape[1:])
-    return lax.all_to_all(parts, axis, 0, 0, tiled=True).astype(jnp.float32)
+    return lax.all_to_all(parts, axis, 0, 0, tiled=True)
 
 
 def ordered_sum(parts):
-    total = parts[0]
+    total = parts[0].astype(jnp.float32)
     for index in range(1, parts.shape[0]):
-        total = total + parts[index]
+        total = total + parts[index].astype(jnp.float32)
     return total
+
+
+def weight_grad_sum(weight_part):
+    n_far = lax.axis_size(DP_FAR)
+    n_core = lax.axis_size("dp_core")
+    rows = weight_part.shape[0] // (n_far * n_core)
+    blocks = weight_part.reshape(n_far, n_core, rows, weight_part.shape[1])
+    pair = lax.all_to_all(blocks, "dp_core", 1, 1, tiled=True)
+    pair = pair[:, 0] + pair[:, 1]
+    return jnp.sum(lax.all_to_all(pair.astype(jnp.bfloat16), DP_FAR, 0, 0, tiled=True).astype(jnp.float32), axis=0)
 
 
 def head_forward(queries, key_rows, values):
@@ -63,11 +75,10 @@
     values = saved_qkv[:, :, 2 * head_size :]
     softmax, soft_low, attended = jax.vmap(head_forward)(queries, key_rows, values)
     weight_part = jnp.einsum("msc,msh->ch", gradients, attended, preferred_element_type=jnp.float32)
-    weight_grad = jnp.sum(exchange(weight_part.astype(jnp.bfloat16), "dp"), axis=0)
+    weight_grad = weight_grad_sum(weight_part)
     current = plan[0, :BMICRO]
-    grad_current = jnp.take(gradients, current, axis=0)
     grad_heads = jnp.einsum(
-        "msd,dh->msh", grad_current, out_proj, preferred_element_type=jnp.float32
+        "msd,dh->msh", gradients, out_proj, preferred_element_type=jnp.float32
     ).astype(jnp.bfloat16)
     grad_qkv = jax.vmap(head_backward)(
         jnp.take(queries, current, axis=0),
@@ -76,21 +87,29 @@
         jnp.take(softmax, current, axis=0),
         jnp.take(soft_low, current, axis=0),
         jnp.take(attended, current, axis=0),
-        grad_heads,
+        jnp.take(grad_heads, current, axis=0),
     )
-    partials = jnp.einsum("bsk,dk->sbd", grad_qkv, qkv_proj, preferred_element_type=jnp.float32)
-    own_rows = ordered_sum(exchange(partials.astype(jnp.bfloat16), "tensor"))
+    n_tensor = lax.axis_size("tensor")
+    grouped = grad_qkv.reshape(grad_qkv.shape[0], n_tensor, grad_qkv.shape[1] // n_tensor, grad_qkv.shape[2])
+    partials = jnp.einsum("bjsk,dk->jsbd", grouped, qkv_proj, preferred_element_type=jnp.float32)
+    parts = lax.all_to_all(partials.astype(jnp.bfloat16), "tensor", 0, 0, tiled=True)
+    own_rows = ordered_sum(parts)
     received = shifted(own_rows.astype(jnp.bfloat16), "pipe", -1)
     return (received[None, None], weight_grad[None, :, None, :])
 
 
 def solution(mesh):
+    n_pipe, n_dp, n_tensor = (mesh.shape[a] for a in ("pipe", "dp", "tensor"))
+    n_y = 2
+    n_core = 2
+    parts = mesh.devices.reshape(n_pipe, n_y, n_dp // (n_y * n_core), n_core, n_tensor)
+    staged = Mesh(parts, ("pipe", *DP_PARTS, "tensor"))
     in_specs = (
-        P("pipe", None, "dp", None, None),
-        P("pipe", None, "dp", None, "tensor", None),
+        P("pipe", None, DP_PARTS, None, None),
+        P("pipe", None, DP_PARTS, None, "tensor", None),
         P("pipe", None, "tensor", None),
         P("pipe", None, "tensor", None),
         P("pipe", None),
     )
-    out_specs = (P("pipe", "dp", "tensor", None, None), P("pipe", "dp", "tensor", None))
-    return jax.shard_map(body, mesh=mesh, in_specs=in_specs, out_specs=out_specs, check_vma=False)
+    out_specs = (P("pipe", DP_PARTS, "tensor", None, None), P("pipe", DP_PARTS, "tensor", None))
+    return jax.shard_map(body, mesh=staged, in_specs=in_specs, out_specs=out_specs, check_vma=False)

time: 144 us -> 133 us (0.924)
  the two profiles are of different devices: /device:TPU:1 before, /device:TPU:6 now
where the time goes in v3:
time: 133 us; the launch traced here: 131 us
  waiting for transfers between devices  57.4 us (43%)
  starting transfers between devices  32.2 us (24%)
  local copies, waits for them, and re-layouts  18.4 us (14%)
  matrix products  16.5 us (12%)
  other arithmetic  5.9 us (4%)
    all_to_all x1, waiting for transfers between devices, weight_grad_sum(): lax.all_to_all(pair.astype(jnp.bfloat16), DP_FAR, 0, 0, tiled=True)  32.3 us
    all_to_all x1, waiting for transfers between devices, body(): lax.all_to_all(partials.astype(jnp.bfloat16), 'tensor', 0, 0, tiled=True)  25.1 us
    all_to_all x1, starting transfers between devices, body(): lax.all_to_all(partials.astype(jnp.bfloat16), 'tensor', 0, 0, tiled=True)  13.9 us
    all_to_all x1, starting transfers between devices, weight_grad_sum(): lax.all_to_all(pair.astype(jnp.bfloat16), DP_FAR, 0, 0, tiled=True)  11.6 us
    reshape x2, local copies, waits for them, and re-layouts, weight_grad_sum(): blocks = weight_part.reshape(n_far, n_core, rows, weight_part.shape[1])  11.3 us
    all_to_all x1, starting transfers between devices, weight_grad_sum(): pair = lax.all_to_all(blocks, 'dp_core', 1, 1, tiled=True)  5.35 us
    dot_general x1, matrix products, body(): jnp.einsum('msc,msh->ch', gradients, attended, preferred_element_type=jnp...  5.04 us
    dot_general x1, matrix products, body(): jnp.einsum('bjsk,dk->jsbd', grouped, qkv_proj, preferred_element_type=jnp...  4.53 us
  transfers between devices with their start and end apart: 4, of which 2 were waited for; matrix products, arithmetic and copies ran while one was open for 16% of the time, Pallas kernels for 0%

profile of v3, /device:TPU:6, one launch (start us, length us, event | category | flops | bytes accessed | tf_op | source)
XLA Modules:
  0.0 131.3 jit_solution(2335482462618226979)
XLA Ops:
  0.7 1.3 fusion.50
  2.0 1.1 convolution_convert_fusion.1
  3.1 5.0 %convolution_bitcast_fusion = f32[6144,128]{0,1:T(8,128)} fusion(bf16[4,96,128]{2,1,0:T(8,128)(2,1)S(1)} %convolution_convert_fusion.1, bf16[1,4,1,96,6144]{4,3,2,1,0:T(8,128)(2,1)} %param.7), kind=kOutput, calls=%fused_computation.9 | convolution fusion | flops 603979776 | bytes 7962624 | tf_op jit(solution)/shard_map/msc,msh->ch/dot_general | solution.py:77
  8.2 5.4 %reshape.66 = f32[24,2,128,128]{2,1,0,3:T(2,128)} reshape(f32[6144,128]{0,1:T(8,128)} %convolution_bitcast_fusion) | data formatting | bytes 6291456 | tf_op jit(solution)/shard_map/reshape | solution.py:34
  13.6 5.8 %copy.20 = f32[24,2,128,128]{3,2,0,1:T(8,128)} copy(f32[24,2,128,128]{2,1,0,3:T(2,128)} %reshape.66) | data formatting | bytes 6291456 | tf_op jit(solution)/shard_map/reshape | solution.py:34
  19.4 5.4 %all-to-all-start.1 = ((f32[24,2,128,128]{3,2,0,1:T(8,128)}), f32[24,2,128,128]{3,2,0,1:T(8,128)}, u32[]{:S(2)}, u32[]{:S(2)}) async-start(f32[24,2,128,128]{3,2,0,1:T(8,128)} %copy.20), calls=%async_computation.1 | async-start | bytes 6291456 | tf_op jit(solution)/shard_map/all_to_all | solution.py:35
  24.9 3.7 %fusion.11 = bf16[4,96,128]{2,1,0:T(8,128)(2,1)S(1)} fusion(bf16[1,6144,1,128]{3,1,2,0:T(8,128)(2,1)S(1)} %copy-done, bf16[1,4,1,96,6144]{4,3,2,1,0:T(8,128)(2,1)} %param.7), kind=kOutput, calls=%fused_computation.24 | convolution fusion | flops 604028928 | bytes 6389760 | tf_op jit(solution)/shard_map/msd,dh->msh/dot_general | solution.py:80
  28.7 0.6 gather_fusion.4
  29.2 0.6 gather_fusion.2
  29.8 0.6 gather_fusion.1
  31.3 0.6 gather_fusion.5
  31.9 0.6 gather_fusion.3
  32.5 0.6 gather_fusion.6
  33.7 4.5 %fusion.1 = bf16[4,24,2,6144]{3,1,0,2:T(8,128)(2,1)S(1)} fusion(bf16[1,6144,1,384]{3,1,2,0:T(8,128)(2,1)} %param.10, bf16[2,4,24,128]{3,2,1,0:T(8,128)(2,1)S(1)} %bitcast.56, bf16[2,4,24,128]{3,2,1,0:T(8,128)(2,1)S(1)} %bitcast.57, bf16[2,4,24,128]{3,2,1,0:T(8,128)(2,1)S(1)} %bitcast.54), kind=kOutput, calls=%fused_computation.10 | convolution fusion | flops 907591680 | bytes 7225344 | tf_op jit(solution)/shard_map/bjsk,dk->jsbd/dot_general | solution.py:94
  38.2 1.7 %copy.19 = bf16[4,24,2,6144]{3,1,2,0:T(8,128)(2,1)} copy(bf16[4,24,2,6144]{3,1,0,2:T(8,128)(2,1)S(1)} %fusion.1) | data formatting | bytes 4718592 | tf_op jit(solution)/shard_map/convert_element_type | solution.py:95
  39.9 13.9 %all-to-all-start = ((bf16[4,24,2,6144]{3,1,2,0:T(8,128)(2,1)}), bf16[4,24,2,6144]{3,1,2,0:T(8,128)(2,1)}, u32[]{:S(2)}, u32[]{:S(2)}) async-start(bf16[4,24,2,6144]{3,1,2,0:T(8,128)(2,1)} %copy.19), calls=%async_computation | async-start | bytes 4718592 | tf_op jit(solution)/shard_map/all_to_all | solution.py:95
  53.8 3.0 %fusion.20 = bf16[24,128,128]{2,1,0:T(8,128)(2,1)} fusion(f32[24,2,128,128]{3,2,0,1:T(8,128)} %all-to-all-done.1), kind=kLoop, calls=%fused_computation.34 | loop fusion | flops 786432 | bytes 3932160 | tf_op jit(solution)/shard_map/convert_element_type | solution.py:37
  56.9 25.1 %all-to-all-done = bf16[4,24,2,6144]{3,1,2,0:T(8,128)(2,1)} async-done(((bf16[4,24,2,6144]{3,1,2,0:T(8,128)(2,1)}), bf16[4,24,2,6144]{3,1,2,0:T(8,128)(2,1)}, u32[]{:S(2)}, u32[]{:S(2)}) %all-to-all-start) | async-done | bytes 2359328 | tf_op jit(solution)/shard_map/all_to_all | solution.py:95
  81.9 11.6 %all-to-all-start.2 = ((bf16[24,128,128]{2,1,0:T(8,128)(2,1)}), bf16[24,128,128]{2,1,0:T(8,128)(2,1)S(1)}, u32[]{:S(2)}, u32[]{:S(2)}) async-start(bf16[24,128,128]{2,1,0:T(8,128)(2,1)} %fusion.20), calls=%async_computation.2 | async-start | bytes 1572864 | tf_op jit(solution)/shard_map/all_to_all | solution.py:37
  93.6 1.9 %fusion.21 = bf16[24,2,6144]{2,0,1:T(8,128)(2,1)S(1)} fusion(bf16[4,24,2,6144]{3,1,2,0:T(8,128)(2,1)} %all-to-all-done), kind=kLoop, calls=%fused_computation.35 | loop fusion | flops 2359296 | bytes 2949120 | tf_op jit(solution)/shard_map/add | solution.py:26
  95.4 1.3 collective-permute-start
  96.7 32.3 %all-to-all-done.2 = bf16[24,128,128]{2,1,0:T(8,128)(2,1)S(1)} async-done(((bf16[24,128,128]{2,1,0:T(8,128)(2,1)}), bf16[24,128,128]{2,1,0:T(8,128)(2,1)S(1)}, u32[]{:S(2)}, u32[]{:S(2)}) %all-to-all-start.2) | async-done | bytes 786464 | tf_op jit(solution)/shard_map/all_to_all | solution.py:37
  129.1 0.7 convert_reduce_fusion
  129.8 1.4 %copy.21 = bf16[1,1,24,2,6144]{4,3,2,1,0:T(2,128)(2,1)} copy(bf16[1,1,24,2,6144]{4,2,3,1,0:T(8,128)(2,1)S(1)} %bitcast.50) | data formatting | bytes 1179648
  (21 shorter events, 1.7 us)
Async XLA Ops:
  0.6 24.3 %copy-start = (bf16[1,6144,1,128]{3,1,2,0:T(8,128)(2,1)S(1)}, bf16[1,6144,1,128]{3,1,2,0:T(8,128)(2,1)}, u32[]{:S(2)}) copy-start(bf16[1,6144,1,128]{3,1,2,0:T(8,128)(2,1)} %param.9) | copy-start | bytes 4718596
  19.4 5.4 %copy-start.2 = (s32[1,4]{1,0:T(1,128)S(1)}, s32[1,4]{1,0:T(1,128)}, u32[]{:S(2)}) copy-start(s32[1,4]{1,0:T(1,128)} %param.11) | copy-start | bytes 52
  19.4 5.4 %copy-start.1 = (bf16[1,4,1,96,1,384]{5,3,4,2,1,0:T(8,128)(2,1)S(1)}, bf16[1,4,1,96,1,384]{5,3,4,2,1,0:T(8,128)(2,1)}, u32[]{:S(2)}) copy-start(bf16[1,4,1,96,1,384]{5,3,4,2,1,0:T(8,128)(2,1)} %param.8) | copy-start | bytes 884740
  19.4 20.5 %all-to-all-start.1 = ((f32[24,2,128,128]{3,2,0,1:T(8,128)}), f32[24,2,128,128]{3,2,0,1:T(8,128)}, u32[]{:S(2)}, u32[]{:S(2)}) async-start(f32[24,2,128,128]{3,2,0,1:T(8,128)} %copy.20), calls=%async_computation.1 | async-start | bytes 6291456 | tf_op jit(solution)/shard_map/all_to_all | solution.py:35
  39.9 42.0 %all-to-all-start = ((bf16[4,24,2,6144]{3,1,2,0:T(8,128)(2,1)}), bf16[4,24,2,6144]{3,1,2,0:T(8,128)(2,1)}, u32[]{:S(2)}, u32[]{:S(2)}) async-start(bf16[4,24,2,6144]{3,1,2,0:T(8,128)(2,1)} %copy.19), calls=%async_computation | async-start | bytes 4718592 | tf_op jit(solution)/shard_map/all_to_all | solution.py:95
  81.9 47.2 %all-to-all-start.2 = ((bf16[24,128,128]{2,1,0:T(8,128)(2,1)}), bf16[24,128,128]{2,1,0:T(8,128)(2,1)S(1)}, u32[]{:S(2)}, u32[]{:S(2)}) async-start(bf16[24,128,128]{2,1,0:T(8,128)(2,1)} %fusion.20), calls=%async_computation.2 | async-start | bytes 1572864 | tf_op jit(solution)/shard_map/all_to_all | solution.py:37
  95.4 34.4 %collective-permute-start = (bf16[24,2,6144]{2,0,1:T(8,128)(2,1)S(1)}, bf16[24,2,6144]{2,0,1:T(8,128)(2,1)S(1)}, u32[]{:S(2)}, u32[]{:S(2)}) collective-permute-start(bf16[24,2,6144]{2,0,1:T(8,128)(2,1)S(1)} %fusion.21), channel_id=1, source_target_pairs={{192,0},{384,192},{576,384},{193,1},{385,193},{577,385},{194,2},{3... | collective-permute-start | bytes 1769480 | tf_op jit(solution)/shard_map/ppermute | solution.py:14

commit v4 on v3

--- a/solution.py
+++ b/solution.py
@@ -28,13 +28,9 @@
 
 
 def weight_grad_sum(weight_part):
-    n_far = lax.axis_size(DP_FAR)
-    n_core = lax.axis_size("dp_core")
-    rows = weight_part.shape[0] // (n_far * n_core)
-    blocks = weight_part.reshape(n_far, n_core, rows, weight_part.shape[1])
-    pair = lax.all_to_all(blocks, "dp_core", 1, 1, tiled=True)
-    pair = pair[:, 0] + pair[:, 1]
-    return jnp.sum(lax.all_to_all(pair.astype(jnp.bfloat16), DP_FAR, 0, 0, tiled=True).astype(jnp.float32), axis=0)
+    pair = lax.all_to_all(weight_part, "dp_core", 2, 2, tiled=True)
+    pair = (pair[:, :, 0] + pair[:, :, 1]).astype(jnp.bfloat16)
+    return jnp.sum(lax.all_to_all(pair, DP_FAR, 1, 1, tiled=True).astype(jnp.float32), axis=1).T
 
 
 def head_forward(queries, key_rows, values):
@@ -74,7 +70,10 @@
     key_rows = saved_qkv[:, :, head_size : 2 * head_size]
     values = saved_qkv[:, :, 2 * head_size :]
     softmax, soft_low, attended = jax.vmap(head_forward)(queries, key_rows, values)
-    weight_part = jnp.einsum("msc,msh->ch", gradients, attended, preferred_element_type=jnp.float32)
+    n_far = lax.axis_size(DP_FAR)
+    n_core = lax.axis_size("dp_core")
+    weight_part = jnp.einsum("msc,msh->hc", gradients, attended, preferred_element_type=jnp.float32)
+    weight_part = weight_part.reshape(weight_part.shape[0], n_far, n_core, -1)
     weight_grad = weight_grad_sum(weight_part)
     current = plan[0, :BMICRO]
     grad_heads = jnp.einsum(

time: 133 us -> 132 us (level)
  local copies, waits for them, and re-layouts: 18.4 us -> 16.8 us
    reshape x2 -> x0, local copies, waits for them, and re-layouts: 11.3 us -> none  [weight_grad_sum(): blocks = weight_part.reshape(n_far, n_core, rows, weight_part.shape[1])]
    dot_general x0 -> x1, local copies, waits for them, and re-layouts: none -> 8.1 us  [body(): jnp.einsum('msc,msh->hc', gradients, attended, preferred_element_type=jnp...]
    unnamed x7 -> x8, local copies, waits for them, and re-layouts: 1.44 us -> 3.01 us
  transfers between devices with their start and end apart: 4 -> 4, of which waited for: 2 -> 2; matrix products, arithmetic and copies ran while one was open for 16% -> 17% of each run, Pallas kernels for 0% -> 0%
where the time goes in v4:
time: 132 us; the launch traced here: 130 us
  waiting for transfers between devices  57.4 us (43%)
  starting transfers between devices  32.2 us (24%)
  matrix products  17.3 us (13%)
  local copies, waits for them, and re-layouts  16.8 us (13%)
  other arithmetic  5.92 us (4%)
    all_to_all x1, waiting for transfers between devices, weight_grad_sum(): lax.all_to_all(pair, DP_FAR, 1, 1, tiled=True).astype(jnp.float32)  32.3 us
    all_to_all x1, waiting for transfers between devices, body(): lax.all_to_all(partials.astype(jnp.bfloat16), 'tensor', 0, 0, tiled=True)  25 us
    all_to_all x1, starting transfers between devices, body(): lax.all_to_all(partials.astype(jnp.bfloat16), 'tensor', 0, 0, tiled=True)  14 us
    all_to_all x1, starting transfers between devices, weight_grad_sum(): lax.all_to_all(pair, DP_FAR, 1, 1, tiled=True).astype(jnp.float32)  11.6 us
    dot_general x1, local copies, waits for them, and re-layouts, body(): jnp.einsum('msc,msh->hc', gradients, attended, preferred_element_type=jnp...  8.1 us
    dot_general x1, matrix products, body(): jnp.einsum('msc,msh->hc', gradients, attended, preferred_element_type=jnp...  5.78 us
    all_to_all x1, starting transfers between devices, weight_grad_sum(): pair = lax.all_to_all(weight_part, 'dp_core', 2, 2, tiled=True)  5.35 us
    dot_general x1, matrix products, body(): jnp.einsum('bjsk,dk->jsbd', grouped, qkv_proj, preferred_element_type=jnp...  4.53 us
  transfers between devices with their start and end apart: 4, of which 2 were waited for; matrix products, arithmetic and copies ran while one was open for 17% of the time, Pallas kernels for 0%

profile of v4, /device:TPU:6, one launch (start us, length us, event | category | flops | bytes accessed | tf_op | source)
XLA Modules:
  0.0 130.5 jit_solution(6679764471282328127)
XLA Ops:
  0.7 1.3 fusion.55
  2.0 1.1 convolution_convert_fusion.1
  3.1 8.1 %dot_general.40 = bf16[24,2,128,4,96]{2,1,0,4,3:T(2,128)(2,1)} reshape(bf16[6144,4,96]{0,2,1:T(8,128)(2,1)} %bitcast.52) | data formatting | bytes 9437184 | tf_op jit(solution)/shard_map/msc,msh->hc/dot_general | solution.py:75
  11.2 5.8 %fusion.7 = f32[128,24,2,128]{3,0,1,2:T(8,128)} fusion(bf16[24,2,128,4,96]{2,1,0,4,3:T(2,128)(2,1)} %dot_general.40, bf16[4,96,128]{2,1,0:T(8,128)(2,1)S(1)} %convolution_convert_fusion.1), kind=kOutput, calls=%fused_computation.15 | convolution fusion | flops 603979776 | bytes 7962624 | tf_op jit(solution)/shard_map/msc,msh->hc/dot_general | solution.py:75
  17.0 5.4 %all-to-all-start.1 = ((f32[128,24,2,128]{3,0,1,2:T(8,128)}), f32[128,24,2,128]{3,0,1,2:T(8,128)}, u32[]{:S(2)}, u32[]{:S(2)}) async-start(f32[128,24,2,128]{3,0,1,2:T(8,128)} %fusion.7), calls=%async_computation.1 | async-start | bytes 6291456 | tf_op jit(solution)/shard_map/all_to_all | solution.py:31
  22.5 3.7 %fusion.15 = bf16[4,96,128]{2,1,0:T(8,128)(2,1)S(1)} fusion(bf16[1,6144,1,128]{3,1,2,0:T(8,128)(2,1)S(1)} %copy-done, bf16[1,4,1,96,6144]{4,3,2,1,0:T(8,128)(2,1)} %param.7), kind=kOutput, calls=%fused_computation.25 | convolution fusion | flops 604028928 | bytes 6389760 | tf_op jit(solution)/shard_map/msd,dh->msh/dot_general | solution.py:79
  26.2 0.6 gather_fusion.4
  26.8 0.6 gather_fusion.2
  27.4 0.6 gather_fusion.1
  28.9 0.6 gather_fusion.5
  29.5 0.6 gather_fusion.3
  30.0 0.6 gather_fusion.6
  31.3 4.5 %fusion.1 = bf16[4,24,2,6144]{3,1,0,2:T(8,128)(2,1)S(1)} fusion(bf16[1,6144,1,384]{3,1,2,0:T(8,128)(2,1)} %param.10, bf16[2,4,24,128]{3,2,1,0:T(8,128)(2,1)S(1)} %bitcast.59, bf16[2,4,24,128]{3,2,1,0:T(8,128)(2,1)S(1)} %bitcast.60, bf16[2,4,24,128]{3,2,1,0:T(8,128)(2,1)S(1)} %bitcast.58), kind=kOutput, calls=%fused_computation.9 | convolution fusion | flops 907591680 | bytes 7225344 | tf_op jit(solution)/shard_map/bjsk,dk->jsbd/dot_general | solution.py:93
  35.8 1.7 %copy.15 = bf16[4,24,2,6144]{3,1,2,0:T(8,128)(2,1)} copy(bf16[4,24,2,6144]{3,1,0,2:T(8,128)(2,1)S(1)} %fusion.1) | data formatting | bytes 4718592 | tf_op jit(solution)/shard_map/convert_element_type | solution.py:94
  37.5 14.0 %all-to-all-start = ((bf16[4,24,2,6144]{3,1,2,0:T(8,128)(2,1)}), bf16[4,24,2,6144]{3,1,2,0:T(8,128)(2,1)}, u32[]{:S(2)}, u32[]{:S(2)}) async-start(bf16[4,24,2,6144]{3,1,2,0:T(8,128)(2,1)} %copy.15), calls=%async_computation | async-start | bytes 4718592 | tf_op jit(solution)/shard_map/all_to_all | solution.py:94
  51.5 3.0 %fusion.24 = bf16[128,24,128]{2,0,1:T(8,128)(2,1)} fusion(f32[128,24,2,128]{3,0,1,2:T(8,128)} %all-to-all-done.1), kind=kLoop, calls=%fused_computation.35 | loop fusion | flops 786432 | bytes 3932160 | tf_op jit(solution)/shard_map/convert_element_type | solution.py:32
  54.5 25.0 %all-to-all-done = bf16[4,24,2,6144]{3,1,2,0:T(8,128)(2,1)} async-done(((bf16[4,24,2,6144]{3,1,2,0:T(8,128)(2,1)}), bf16[4,24,2,6144]{3,1,2,0:T(8,128)(2,1)}, u32[]{:S(2)}, u32[]{:S(2)}) %all-to-all-start) | async-done | bytes 2359328 | tf_op jit(solution)/shard_map/all_to_all | solution.py:94
  79.6 11.6 %all-to-all-start.2 = ((bf16[128,24,128]{2,0,1:T(8,128)(2,1)}), bf16[128,24,128]{2,0,1:T(8,128)(2,1)S(1)}, u32[]{:S(2)}, u32[]{:S(2)}) async-start(bf16[128,24,128]{2,0,1:T(8,128)(2,1)} %fusion.24), calls=%async_computation.2 | async-start | bytes 1572864 | tf_op jit(solution)/shard_map/all_to_all | solution.py:33
  91.2 1.9 %fusion.25 = bf16[24,2,6144]{2,0,1:T(8,128)(2,1)S(1)} fusion(bf16[4,24,2,6144]{3,1,2,0:T(8,128)(2,1)} %all-to-all-done), kind=kLoop, calls=%fused_computation.36 | loop fusion | flops 2359296 | bytes 2949120 | tf_op jit(solution)/shard_map/add | solution.py:26
  93.1 1.3 collective-permute-start
  94.4 32.3 %all-to-all-done.2 = bf16[128,24,128]{2,0,1:T(8,128)(2,1)S(1)} async-done(((bf16[128,24,128]{2,0,1:T(8,128)(2,1)}), bf16[128,24,128]{2,0,1:T(8,128)(2,1)S(1)}, u32[]{:S(2)}, u32[]{:S(2)}) %all-to-all-start.2) | async-done | bytes 786464 | tf_op jit(solution)/shard_map/all_to_all | solution.py:33
  126.7 0.7 convert_reduce_fusion
  127.5 1.6 %copy.19 = f32[1,128,1,128]{3,2,1,0:T(1,128)} copy(f32[1,128,1,128]{1,3,2,0:T(8,128)} %bitcast.57) | data formatting | bytes 131072
  129.0 1.4 %copy.18 = bf16[1,1,24,2,6144]{4,3,2,1,0:T(2,128)(2,1)} copy(bf16[1,1,24,2,6144]{4,2,3,1,0:T(8,128)(2,1)S(1)} %bitcast.53) | data formatting | bytes 1179648
  (21 shorter events, 1.7 us)
Async XLA Ops:
  0.6 21.9 %copy-start = (bf16[1,6144,1,128]{3,1,2,0:T(8,128)(2,1)S(1)}, bf16[1,6144,1,128]{3,1,2,0:T(8,128)(2,1)}, u32[]{:S(2)}) copy-start(bf16[1,6144,1,128]{3,1,2,0:T(8,128)(2,1)} %param.9) | copy-start | bytes 4718596
  17.0 5.4 %copy-start.2 = (s32[1,4]{1,0:T(1,128)S(1)}, s32[1,4]{1,0:T(1,128)}, u32[]{:S(2)}) copy-start(s32[1,4]{1,0:T(1,128)} %param.11) | copy-start | bytes 52
  17.0 5.4 %copy-start.1 = (bf16[1,4,1,96,1,384]{5,3,4,2,1,0:T(8,128)(2,1)S(1)}, bf16[1,4,1,96,1,384]{5,3,4,2,1,0:T(8,128)(2,1)}, u32[]{:S(2)}) copy-start(bf16[1,4,1,96,1,384]{5,3,4,2,1,0:T(8,128)(2,1)} %param.8) | copy-start | bytes 884740
  17.0 20.5 %all-to-all-start.1 = ((f32[128,24,2,128]{3,0,1,2:T(8,128)}), f32[128,24,2,128]{3,0,1,2:T(8,128)}, u32[]{:S(2)}, u32[]{:S(2)}) async-start(f32[128,24,2,128]{3,0,1,2:T(8,128)} %fusion.7), calls=%async_computation.1 | async-start | bytes 6291456 | tf_op jit(solution)/shard_map/all_to_all | solution.py:31
  37.5 42.1 %all-to-all-start = ((bf16[4,24,2,6144]{3,1,2,0:T(8,128)(2,1)}), bf16[4,24,2,6144]{3,1,2,0:T(8,128)(2,1)}, u32[]{:S(2)}, u32[]{:S(2)}) async-start(bf16[4,24,2,6144]{3,1,2,0:T(8,128)(2,1)} %copy.15), calls=%async_computation | async-start | bytes 4718592 | tf_op jit(solution)/shard_map/all_to_all | solution.py:94
  79.6 47.2 %all-to-all-start.2 = ((bf16[128,24,128]{2,0,1:T(8,128)(2,1)}), bf16[128,24,128]{2,0,1:T(8,128)(2,1)S(1)}, u32[]{:S(2)}, u32[]{:S(2)}) async-start(bf16[128,24,128]{2,0,1:T(8,128)(2,1)} %fusion.24), calls=%async_computation.2 | async-start | bytes 1572864 | tf_op jit(solution)/shard_map/all_to_all | solution.py:33
  93.1 36.0 %collective-permute-start = (bf16[24,2,6144]{2,0,1:T(8,128)(2,1)S(1)}, bf16[24,2,6144]{2,0,1:T(8,128)(2,1)S(1)}, u32[]{:S(2)}, u32[]{:S(2)}) collective-permute-start(bf16[24,2,6144]{2,0,1:T(8,128)(2,1)S(1)} %fusion.25), channel_id=1, source_target_pairs={{192,0},{384,192},{576,384},{193,1},{385,193},{577,385},{194,2},{3... | collective-permute-start | bytes 1769480 | tf_op jit(solution)/shard_map/ppermute | solution.py:14

commit v5 on v4

--- a/solution.py
+++ b/solution.py
@@ -24,6 +24,15 @@
     total = parts[0].astype(jnp.float32)
     for index in range(1, parts.shape[0]):
         total = total + parts[index].astype(jnp.float32)
+    return total
+
+
+def rotated_sum(parts, axis):
+    n = parts.shape[0]
+    total = parts[0].astype(jnp.float32)
+    for shift in range(1, n):
+        moved = lax.ppermute(parts[shift], axis, [(i, (i + shift) % n) for i in range(n)])
+        total = total + moved.astype(jnp.float32)
     return total
 
 
@@ -89,10 +98,12 @@
         jnp.take(grad_heads, current, axis=0),
     )
     n_tensor = lax.axis_size("tensor")
-    grouped = grad_qkv.reshape(grad_qkv.shape[0], n_tensor, grad_qkv.shape[1] // n_tensor, grad_qkv.shape[2])
+    seq_len = grad_qkv.shape[1]
+    start = lax.axis_index("tensor") * (seq_len // n_tensor)
+    grad_qkv = lax.dynamic_slice_in_dim(jnp.concatenate([grad_qkv, grad_qkv], axis=1), start, seq_len, axis=1)
+    grouped = grad_qkv.reshape(grad_qkv.shape[0], n_tensor, seq_len // n_tensor, grad_qkv.shape[2])
     partials = jnp.einsum("bjsk,dk->jsbd", grouped, qkv_proj, preferred_element_type=jnp.float32)
-    parts = lax.all_to_all(partials.astype(jnp.bfloat16), "tensor", 0, 0, tiled=True)
-    own_rows = ordered_sum(parts)
+    own_rows = rotated_sum(partials.astype(jnp.bfloat16), "tensor")
     received = shifted(own_rows.astype(jnp.bfloat16), "pipe", -1)
     return (received[None, None], weight_grad[None, :, None, :])
 

time: 132 us -> 109 us (0.83)
  waiting for transfers between devices: 57.4 us -> 31.2 us
  blocking collectives: 0 us -> 6.26 us
  matrix products: 17.3 us -> 15.5 us
    all_to_all x1, waiting for transfers between devices: 32.3 us -> 1.42 us  [weight_grad_sum(): lax.all_to_all(pair, DP_FAR, 1, 1, tiled=True).astype(jnp.float32)]
    ppermute x1, waiting for transfers between devices: 0.01 us -> 29.7 us  [shifted(): return lax.ppermute(block, axis, route)]
    all_to_all x2 -> x0, waiting for transfers between devices: 25.1 us -> none  [the longest x1 25 us: body(): lax.all_to_all(partials.astype(jnp.bfloat16), 'tensor', 0, 0, tiled=True)]
    all_to_all x2 -> x0, starting transfers between devices: 19.3 us -> none  [the longest x1 14 us: body(): lax.all_to_all(partials.astype(jnp.bfloat16), 'tensor', 0, 0, tiled=True)]
    ppermute x0 -> x3, starting transfers between devices: none -> 16.7 us  [rotated_sum(): lax.ppermute(parts[shift], axis, [(i, (i + shift) % n) for i in range(n)])]
    all_to_all x0 -> x1, blocking collectives: none -> 6.26 us  [weight_grad_sum(): pair = lax.all_to_all(weight_part, 'dp_core', 2, 2, tiled=True)]
    convert_element_type x1, other arithmetic: 3.04 us -> 1.08 us  [weight_grad_sum(): pair = (pair[:, :, 0] + pair[:, :, 1]).astype(jnp.bfloat16)]
    convert_element_type x0 -> x1, other arithmetic: none -> 1.89 us  [body(): received = shifted(own_rows.astype(jnp.bfloat16), 'pipe', -1)]
  transfers between devices with their start and end apart: 4 -> 5, of which waited for: 2 -> 2; matrix products, arithmetic and copies ran while one was open for 17% -> 15% of each run, Pallas kernels for 0% -> 0%
where the time goes in v5:
time: 109 us; the launch traced here: 107 us
  waiting for transfers between devices  31.2 us (29%)
  starting transfers between devices  31.1 us (29%)
  local copies, waits for them, and re-layouts  17.6 us (16%)
  matrix products  15.5 us (14%)
  blocking collectives  6.26 us (6%)
  other arithmetic  4.88 us (4%)
    ppermute x1, waiting for transfers between devices, shifted(): return lax.ppermute(block, axis, route)  29.7 us
    ppermute x3, starting transfers between devices, rotated_sum(): lax.ppermute(parts[shift], axis, [(i, (i + shift) % n) for i in range(n)])  16.7 us
    all_to_all x1, starting transfers between devices, weight_grad_sum(): lax.all_to_all(pair, DP_FAR, 1, 1, tiled=True).astype(jnp.float32)  13.1 us
    dot_general x1, local copies, waits for them, and re-layouts, body(): jnp.einsum('msc,msh->hc', gradients, attended, preferred_element_type=jnp...  8.09 us
    all_to_all x1, blocking collectives, weight_grad_sum(): pair = lax.all_to_all(weight_part, 'dp_core', 2, 2, tiled=True)  6.26 us
    dot_general x1, matrix products, body(): jnp.einsum('bjsk,dk->jsbd', grouped, qkv_proj, preferred_element_type=jnp...  4.52 us
    dot_general x1, matrix products, body(): jnp.einsum('msc,msh->hc', gradients, attended, preferred_element_type=jnp...  4.11 us
    dot_general x1, matrix products, body(): jnp.einsum('msd,dh->msh', gradients, out_proj, preferred_element_type=jnp...  3.72 us
  transfers between devices with their start and end apart: 5, of which 2 were waited for; matrix products, arithmetic and copies ran while one was open for 15% of the time, Pallas kernels for 0%

profile of v5, /device:TPU:6, one launch (start us, length us, event | category | flops | bytes accessed | tf_op | source)
XLA Modules:
  0.0 107.3 jit_solution(8765543102062225940)
XLA Ops:
  0.6 0.8 fusion.46
  1.4 0.7 compare_and_fusion
  2.1 1.0 fusion.55
  3.2 1.2 %fusion.56 = (f32[4,96]{1,0:T(4,128)S(1)}, f32[4,96,96]{1,2,0:T(8,128)S(1)}) fusion(pred[96,96]{0,1:T(8,128)(4,1)S(1)} %iota_compare_fusion, bf16[4,96,384]{2,1,0:T(8,128)(2,1)} %bitcast.70), kind=kOutput, calls=%fused_computation.86 | convolution fusion | flops 9584735 | bytes 354816 | tf_op jit(solution)/shard_map/vmap()/sub | solution.py:52
  4.4 1.1 %convolution_convert_fusion.1 = bf16[4,96,128]{2,1,0:T(8,128)(2,1)S(1)} fusion(bf16[4,96,96]{1,2,0:T(8,128)(2,1)S(1)} %get-tuple-element.9, bf16[4,96,384]{2,1,0:T(8,128)(2,1)} %bitcast.71), kind=kOutput, calls=%fused_computation.29 | convolution fusion | flops 9486336 | bytes 270336 | tf_op jit(solution)/shard_map/vmap()/dot_general | solution.py:55
  6.6 3.7 %fusion.18 = bf16[4,96,128]{2,1,0:T(8,128)(2,1)S(1)} fusion(bf16[1,6144,1,128]{3,1,2,0:T(8,128)(2,1)S(1)} %copy-done, bf16[1,4,1,96,6144]{4,3,2,1,0:T(8,128)(2,1)} %param.7), kind=kOutput, calls=%fused_computation.28 | convolution fusion | flops 604028928 | bytes 6389760 | tf_op jit(solution)/shard_map/msd,dh->msh/dot_general | solution.py:88
  11.9 0.6 gather_fusion.6
  14.4 4.5 %fusion.1 = bf16[4,24,2,6144]{3,1,0,2:T(8,128)(2,1)S(1)} fusion(bf16[2,4,24,384]{3,2,1,0:T(8,128)(2,1)S(1)} %bitcast.68, bf16[1,6144,1,384]{3,1,2,0:T(8,128)(2,1)} %param.10), kind=kOutput, calls=%fused_computation.9 | convolution fusion | flops 907149312 | bytes 7225344 | tf_op jit(solution)/shard_map/bjsk,dk->jsbd/dot_general | solution.py:105
  18.9 1.4 %copy-done.1 = bf16[4,24,2,6144]{3,1,0,2:T(8,128)(2,1)} copy-done((bf16[4,24,2,6144]{3,1,0,2:T(8,128)(2,1)}, bf16[4,24,2,6144]{3,1,0,2:T(8,128)(2,1)S(1)}, u32[]{:S(2)}) %copy-start.1) | copy-done | bytes 2359320
  20.4 0.9 slice_bitcast_fusion.2
  21.3 11.4 %collective-permute-start = (bf16[24,2,6144]{2,0,1:T(8,128)(2,1)}, bf16[24,2,6144]{2,0,1:T(8,128)(2,1)}, u32[]{:S(2)}, u32[]{:S(2)}) collective-permute-start(bf16[24,2,6144]{2,0,1:T(8,128)(2,1)} %get-tuple-element.11), channel_id=1, source_target_pairs={{0,1},{1,2},{2,3},{3,0},{4,5},{5,6},{6,7},{7,4},{8,9},{9,10},{10,1... | collective-permute-start | bytes 1769480 | tf_op jit(solution)/shard_map/ppermute | solution.py:34
  32.7 1.9 %collective-permute-start.2 = (bf16[24,2,6144]{2,0,1:T(8,128)(2,1)S(1)}, bf16[24,2,6144]{2,0,1:T(8,128)(2,1)}, u32[]{:S(2)}, u32[]{:S(2)}) collective-permute-start(bf16[24,2,6144]{2,0,1:T(8,128)(2,1)S(1)} %get-tuple-element.12), channel_id=1, source_target_pairs={{0,3},{1,0},{2,1},{3,2},{4,7},{5,4},{6,5},{7,6},{8,11},{9,8},{10,9... | collective-permute-start | bytes 1769480 | tf_op jit(solution)/shard_map/ppermute | solution.py:34
  34.6 3.4 %collective-permute-start.1 = (bf16[24,2,6144]{2,0,1:T(8,128)(2,1)S(1)}, bf16[24,2,6144]{2,0,1:T(8,128)(2,1)}, u32[]{:S(2)}, u32[]{:S(2)}) collective-permute-start(bf16[24,2,6144]{2,0,1:T(8,128)(2,1)S(1)} %get-tuple-element.13), channel_id=1, source_target_pairs={{0,2},{1,3},{2,0},{3,1},{4,6},{5,7},{6,4},{7,5},{8,10},{9,11},{10,... | collective-permute-start | bytes 1769480 | tf_op jit(solution)/shard_map/ppermute | solution.py:34
  38.0 8.1 %dot_general.40 = bf16[24,2,128,4,96]{2,1,0,4,3:T(2,128)(2,1)} reshape(bf16[6144,4,96]{0,2,1:T(8,128)(2,1)} %bitcast.66) | data formatting | bytes 9437184 | tf_op jit(solution)/shard_map/msc,msh->hc/dot_general | solution.py:84
  46.1 4.1 %fusion.7 = f32[128,24,2,128]{3,0,1,2:T(8,128)S(1)} fusion(bf16[24,2,128,4,96]{2,1,0,4,3:T(2,128)(2,1)} %dot_general.40, bf16[4,96,128]{2,1,0:T(8,128)(2,1)S(1)} %convolution_convert_fusion.1), kind=kOutput, calls=%fused_computation.15 | convolution fusion | flops 603979776 | bytes 7962624 | tf_op jit(solution)/shard_map/msc,msh->hc/dot_general | solution.py:84
  50.2 6.3 %all_to_all.10 = f32[128,24,2,128]{3,0,1,2:T(8,128)S(1)} all-to-all(f32[128,24,2,128]{3,0,1,2:T(8,128)S(1)} %fusion.7), channel_id=1, replica_groups=mesh['pipe'=4,'dp_y'=2,'dp_z'=12,'dp_core'=2,'tensor'=4] {'dp_core'}, dimensions={2} | all-to-all | bytes 6291456 | tf_op jit(solution)/shard_map/all_to_all | solution.py:40
  56.5 1.1 %fusion.27 = bf16[128,24,128]{2,0,1:T(8,128)(2,1)} fusion(f32[128,24,2,128]{3,0,1,2:T(8,128)S(1)} %all_to_all.10), kind=kLoop, calls=%fused_computation.38 | loop fusion | flops 786432 | bytes 3932160 | tf_op jit(solution)/shard_map/convert_element_type | solution.py:41
  57.6 13.1 %all-to-all-start.1 = ((bf16[128,24,128]{2,0,1:T(8,128)(2,1)}), bf16[128,24,128]{2,0,1:T(8,128)(2,1)S(1)}, u32[]{:S(2)}, u32[]{:S(2)}) async-start(bf16[128,24,128]{2,0,1:T(8,128)(2,1)} %fusion.27), calls=%async_computation.1 | async-start | bytes 1572864 | tf_op jit(solution)/shard_map/all_to_all | solution.py:42
  70.7 1.9 %fusion.14 = bf16[24,2,6144]{2,0,1:T(8,128)(2,1)S(1)} fusion(bf16[24,2,6144]{2,0,1:T(8,128)(2,1)} %collective-permute-done.2, bf16[24,2,6144]{2,0,1:T(8,128)(2,1)} %collective-permute-done.1, bf16[24,2,6144]{2,0,1:T(8,128)(2,1)} %collective-permute-done, bf16[4,24,2,6144]{3,1,0,2:T(8,128)(2,1)} %copy-done.1), kind=kLoop, calls=%fused_computation.23 | loop fusion | flops 2359296 | bytes 2949120 | tf_op jit(solution)/shard_map/convert_element_type | solution.py:107
  72.6 1.3 %collective-permute-start.3 = (bf16[24,2,6144]{2,0,1:T(8,128)(2,1)S(1)}, bf16[24,2,6144]{2,0,1:T(8,128)(2,1)S(1)}, u32[]{:S(2)}, u32[]{:S(2)}) collective-permute-start(bf16[24,2,6144]{2,0,1:T(8,128)(2,1)S(1)} %fusion.14), channel_id=1, source_target_pairs={{192,0},{384,192},{576,384},{193,1},{385,193},{577,385},{194,2},{3... | collective-permute-start | bytes 1769480 | tf_op jit(solution)/shard_map/ppermute | solution.py:14
  73.9 29.7 %collective-permute-done.3 = bf16[24,2,6144]{2,0,1:T(8,128)(2,1)S(1)} collective-permute-done((bf16[24,2,6144]{2,0,1:T(8,128)(2,1)S(1)}, bf16[24,2,6144]{2,0,1:T(8,128)(2,1)S(1)}, u32[]{:S(2)}, u32[]{:S(2)}) %collective-permute-start.3) | collective-permute-done | bytes 589856 | tf_op jit(solution)/shard_map/ppermute | solution.py:14
  103.6 1.4 %copy.23 = bf16[1,1,24,2,6144]{4,3,2,1,0:T(2,128)(2,1)} copy(bf16[1,1,24,2,6144]{4,2,3,1,0:T(8,128)(2,1)S(1)} %bitcast.67) | data formatting | bytes 1179648
  105.0 1.4 %all-to-all-done.1 = bf16[128,24,128]{2,0,1:T(8,128)(2,1)S(1)} async-done(((bf16[128,24,128]{2,0,1:T(8,128)(2,1)}), bf16[128,24,128]{2,0,1:T(8,128)(2,1)S(1)}, u32[]{:S(2)}, u32[]{:S(2)}) %all-to-all-start.1) | async-done | bytes 786464 | tf_op jit(solution)/shard_map/all_to_all | solution.py:42
  106.6 0.7 copy.24
  (23 shorter events, 4.7 us)
Async XLA Ops:
  0.6 6.0 %copy-start = (bf16[1,6144,1,128]{3,1,2,0:T(8,128)(2,1)S(1)}, bf16[1,6144,1,128]{3,1,2,0:T(8,128)(2,1)}, u32[]{:S(2)}) copy-start(bf16[1,6144,1,128]{3,1,2,0:T(8,128)(2,1)} %param.9) | copy-start | bytes 4718596
  18.9 1.4 %copy-start.1 = (bf16[4,24,2,6144]{3,1,0,2:T(8,128)(2,1)}, bf16[4,24,2,6144]{3,1,0,2:T(8,128)(2,1)S(1)}, u32[]{:S(2)}) copy-start(bf16[4,24,2,6144]{3,1,0,2:T(8,128)(2,1)S(1)} %fusion.1) | copy-start | bytes 7077892
  21.3 49.4 %collective-permute-start = (bf16[24,2,6144]{2,0,1:T(8,128)(2,1)}, bf16[24,2,6144]{2,0,1:T(8,128)(2,1)}, u32[]{:S(2)}, u32[]{:S(2)}) collective-permute-start(bf16[24,2,6144]{2,0,1:T(8,128)(2,1)} %get-tuple-element.11), channel_id=1, source_target_pairs={{0,1},{1,2},{2,3},{3,0},{4,5},{5,6},{6,7},{7,4},{8,9},{9,10},{10,1... | collective-permute-start | bytes 1769480 | tf_op jit(solution)/shard_map/ppermute | solution.py:34
  32.7 38.0 %collective-permute-start.2 = (bf16[24,2,6144]{2,0,1:T(8,128)(2,1)S(1)}, bf16[24,2,6144]{2,0,1:T(8,128)(2,1)}, u32[]{:S(2)}, u32[]{:S(2)}) collective-permute-start(bf16[24,2,6144]{2,0,1:T(8,128)(2,1)S(1)} %get-tuple-element.12), channel_id=1, source_target_pairs={{0,3},{1,0},{2,1},{3,2},{4,7},{5,4},{6,5},{7,6},{8,11},{9,8},{10,9... | collective-permute-start | bytes 1769480 | tf_op jit(solution)/shard_map/ppermute | solution.py:34
  34.6 36.1 %collective-permute-start.1 = (bf16[24,2,6144]{2,0,1:T(8,128)(2,1)S(1)}, bf16[24,2,6144]{2,0,1:T(8,128)(2,1)}, u32[]{:S(2)}, u32[]{:S(2)}) collective-permute-start(bf16[24,2,6144]{2,0,1:T(8,128)(2,1)S(1)} %get-tuple-element.13), channel_id=1, source_target_pairs={{0,2},{1,3},{2,0},{3,1},{4,6},{5,7},{6,4},{7,5},{8,10},{9,11},{10,... | collective-permute-start | bytes 1769480 | tf_op jit(solution)/shard_map/ppermute | solution.py:34
  57.6 48.9 %all-to-all-start.1 = ((bf16[128,24,128]{2,0,1:T(8,128)(2,1)}), bf16[128,24,128]{2,0,1:T(8,128)(2,1)S(1)}, u32[]{:S(2)}, u32[]{:S(2)}) async-start(bf16[128,24,128]{2,0,1:T(8,128)(2,1)} %fusion.27), calls=%async_computation.1 | async-start | bytes 1572864 | tf_op jit(solution)/shard_map/all_to_all | solution.py:42
  72.6 31.0 %collective-permute-start.3 = (bf16[24,2,6144]{2,0,1:T(8,128)(2,1)S(1)}, bf16[24,2,6144]{2,0,1:T(8,128)(2,1)S(1)}, u32[]{:S(2)}, u32[]{:S(2)}) collective-permute-start(bf16[24,2,6144]{2,0,1:T(8,128)(2,1)S(1)} %fusion.14), channel_id=1, source_target_pairs={{192,0},{384,192},{576,384},{193,1},{385,193},{577,385},{194,2},{3... | collective-permute-start | bytes 1769480 | tf_op jit(solution)/shard_map/ppermute | solution.py:14

commit v6 on v5

--- a/solution.py
+++ b/solution.py
@@ -5,7 +5,6 @@
 
 BMICRO = 2
 DP_PARTS = ("dp_y", "dp_z", "dp_core")
-DP_FAR = ("dp_y", "dp_z")
 
 
 def shifted(block, axis, distance):
@@ -37,9 +36,13 @@
 
 
 def weight_grad_sum(weight_part):
-    pair = lax.all_to_all(weight_part, "dp_core", 2, 2, tiled=True)
-    pair = (pair[:, :, 0] + pair[:, :, 1]).astype(jnp.bfloat16)
-    return jnp.sum(lax.all_to_all(pair, DP_FAR, 1, 1, tiled=True).astype(jnp.float32), axis=1).T
+    pair = lax.all_to_all(weight_part, "dp_core", 3, 3, tiled=True)
+    pair = (pair[:, :, :, 0] + pair[:, :, :, 1]).astype(jnp.bfloat16)
+    ring = jnp.sum(lax.all_to_all(pair, "dp_z", 2, 2, tiled=True).astype(jnp.float32), axis=2)
+    y = lax.axis_index("dp_y")
+    keep = lax.dynamic_index_in_dim(ring, y, axis=1, keepdims=False)
+    give = lax.dynamic_index_in_dim(ring, 1 - y, axis=1, keepdims=False)
+    return (keep + lax.ppermute(give, "dp_y", [(0, 1), (1, 0)])).T
 
 
 def head_forward(queries, key_rows, values):
@@ -79,10 +82,8 @@
     key_rows = saved_qkv[:, :, head_size : 2 * head_size]
     values = saved_qkv[:, :, 2 * head_size :]
     softmax, soft_low, attended = jax.vmap(head_forward)(queries, key_rows, values)
-    n_far = lax.axis_size(DP_FAR)
-    n_core = lax.axis_size("dp_core")
     weight_part = jnp.einsum("msc,msh->hc", gradients, attended, preferred_element_type=jnp.float32)
-    weight_part = weight_part.reshape(weight_part.shape[0], n_far, n_core, -1)
+    weight_part = weight_part.reshape(weight_part.shape[0], *(lax.axis_size(a) for a in DP_PARTS), -1)
     weight_grad = weight_grad_sum(weight_part)
     current = plan[0, :BMICRO]
     grad_heads = jnp.einsum(

time: 109 us -> 113 us (1.037)
  the two profiles are of different devices: /device:TPU:6 before, /device:TPU:106 now
where the time goes in v6:
time: 113 us; the launch traced here: 112 us
  waiting for transfers between devices  34 us (30%)
  starting transfers between devices  31.4 us (28%)
  local copies, waits for them, and re-layouts  19.2 us (17%)
  matrix products  15.5 us (14%)
  blocking collectives  6.26 us (6%)
  other arithmetic  4.84 us (4%)
    all_to_all x1, waiting for transfers between devices, weight_grad_sum(): lax.all_to_all(pair, 'dp_z', 2, 2, tiled=True).astype(jnp.float32)  27.6 us
    all_to_all x1, starting transfers between devices, weight_grad_sum(): lax.all_to_all(pair, 'dp_z', 2, 2, tiled=True).astype(jnp.float32)  14.8 us
    ppermute x3, starting transfers between devices, rotated_sum(): lax.ppermute(parts[shift], axis, [(i, (i + shift) % n) for i in range(n)])  10.5 us
    dot_general x1, local copies, waits for them, and re-layouts, body(): jnp.einsum('msc,msh->hc', gradients, attended, preferred_element_type=jnp...  8.1 us
    ppermute x1, waiting for transfers between devices, weight_grad_sum(): return (keep + lax.ppermute(give, 'dp_y', [(0, 1), (1, 0)])).T  6.42 us
    all_to_all x1, blocking collectives, weight_grad_sum(): pair = lax.all_to_all(weight_part, 'dp_core', 3, 3, tiled=True)  6.26 us
    dot_general x1, matrix products, body(): jnp.einsum('bjsk,dk->jsbd', grouped, qkv_proj, preferred_element_type=jnp...  4.53 us
    unnamed x8, local copies, waits for them, and re-layouts  4.24 us
  transfers between devices with their start and end apart: 6, of which 2 were waited for; matrix products, arithmetic and copies ran while one was open for 15% of the time, Pallas kernels for 0%

profile of v6, /device:TPU:106, one launch (start us, length us, event | category | flops | bytes accessed | tf_op | source)
XLA Modules:
  0.0 112.1 jit_solution(3417072059583197637)
XLA Ops:
  0.7 0.8 fusion.47
  2.1 1.0 fusion.56
  3.1 1.2 %fusion.57 = (f32[4,96]{1,0:T(4,128)S(1)}, f32[4,96,96]{1,2,0:T(8,128)S(1)}) fusion(pred[96,96]{0,1:T(8,128)(4,1)S(1)} %iota_compare_fusion, bf16[4,96,384]{2,1,0:T(8,128)(2,1)} %bitcast.79), kind=kOutput, calls=%fused_computation.89 | convolution fusion | flops 9584735 | bytes 354816 | tf_op jit(solution)/shard_map/vmap()/sub | solution.py:55
  4.3 1.1 convolution_convert_fusion.1
  7.8 3.7 %fusion.18 = bf16[4,96,128]{2,1,0:T(8,128)(2,1)S(1)} fusion(bf16[1,6144,1,128]{3,1,2,0:T(8,128)(2,1)S(1)} %copy-done, bf16[1,4,1,96,6144]{4,3,2,1,0:T(8,128)(2,1)} %param.7), kind=kOutput, calls=%fused_computation.28 | convolution fusion | flops 604028928 | bytes 6389760 | tf_op jit(solution)/shard_map/msd,dh->msh/dot_general | solution.py:89
  14.4 4.5 %fusion.1 = bf16[4,24,2,6144]{3,1,0,2:T(8,128)(2,1)S(1)} fusion(bf16[2,4,24,384]{3,2,1,0:T(8,128)(2,1)S(1)} %bitcast.77, bf16[1,6144,1,384]{3,1,2,0:T(8,128)(2,1)} %param.10), kind=kOutput, calls=%fused_computation.9 | convolution fusion | flops 907149312 | bytes 7225344 | tf_op jit(solution)/shard_map/bjsk,dk->jsbd/dot_general | solution.py:106
  18.9 1.4 %copy-done.1 = bf16[4,24,2,6144]{3,1,0,2:T(8,128)(2,1)} copy-done((bf16[4,24,2,6144]{3,1,0,2:T(8,128)(2,1)}, bf16[4,24,2,6144]{3,1,0,2:T(8,128)(2,1)S(1)}, u32[]{:S(2)}) %copy-start.1) | copy-done | bytes 2359320
  20.3 0.9 slice_bitcast_fusion.2
  21.3 2.4 %collective-permute-start.2 = (bf16[24,2,6144]{2,0,1:T(8,128)(2,1)}, bf16[24,2,6144]{2,0,1:T(8,128)(2,1)}, u32[]{:S(2)}, u32[]{:S(2)}) collective-permute-start(bf16[24,2,6144]{2,0,1:T(8,128)(2,1)} %get-tuple-element.14), channel_id=1, source_target_pairs={{0,3},{1,0},{2,1},{3,2},{4,7},{5,4},{6,5},{7,6},{8,11},{9,8},{10,9... | collective-permute-start | bytes 1769480 | tf_op jit(solution)/shard_map/ppermute | solution.py:33
  23.7 4.3 %collective-permute-start.1 = (bf16[24,2,6144]{2,0,1:T(8,128)(2,1)S(1)}, bf16[24,2,6144]{2,0,1:T(8,128)(2,1)}, u32[]{:S(2)}, u32[]{:S(2)}) collective-permute-start(bf16[24,2,6144]{2,0,1:T(8,128)(2,1)S(1)} %get-tuple-element.15), channel_id=1, source_target_pairs={{0,2},{1,3},{2,0},{3,1},{4,6},{5,7},{6,4},{7,5},{8,10},{9,11},{10,... | collective-permute-start | bytes 1769480 | tf_op jit(solution)/shard_map/ppermute | solution.py:33
  28.1 3.7 %collective-permute-start = (bf16[24,2,6144]{2,0,1:T(8,128)(2,1)S(1)}, bf16[24,2,6144]{2,0,1:T(8,128)(2,1)}, u32[]{:S(2)}, u32[]{:S(2)}) collective-permute-start(bf16[24,2,6144]{2,0,1:T(8,128)(2,1)S(1)} %get-tuple-element.13), channel_id=1, source_target_pairs={{0,1},{1,2},{2,3},{3,0},{4,5},{5,6},{6,7},{7,4},{8,9},{9,10},{10,1... | collective-permute-start | bytes 1769480 | tf_op jit(solution)/shard_map/ppermute | solution.py:33
  31.8 8.1 %dot_general.40 = bf16[2,12,2,128,4,96]{3,2,1,0,5,4:T(2,128)(2,1)} reshape(bf16[6144,4,96]{0,2,1:T(8,128)(2,1)} %bitcast.75) | data formatting | bytes 9437184 | tf_op jit(solution)/shard_map/msc,msh->hc/dot_general | solution.py:85
  39.9 4.1 %fusion.7 = f32[128,2,12,2,128]{4,0,2,1,3:T(8,128)S(1)} fusion(bf16[2,12,2,128,4,96]{3,2,1,0,5,4:T(2,128)(2,1)} %dot_general.40, bf16[4,96,128]{2,1,0:T(8,128)(2,1)S(1)} %convolution_convert_fusion.1), kind=kOutput, calls=%fused_computation.15 | convolution fusion | flops 603979776 | bytes 7962624 | tf_op jit(solution)/shard_map/msc,msh->hc/dot_general | solution.py:85
  44.0 6.3 %all_to_all.10 = f32[128,2,12,2,128]{4,0,2,1,3:T(8,128)S(1)} all-to-all(f32[128,2,12,2,128]{4,0,2,1,3:T(8,128)S(1)} %fusion.7), channel_id=1, replica_groups=mesh['pipe'=4,'dp_y'=2,'dp_z'=12,'dp_core'=2,'tensor'=4] {'dp_core'}, dimensions={3} | all-to-all | bytes 6291456 | tf_op jit(solution)/shard_map/all_to_all | solution.py:39
  50.5 0.9 copy.34
  51.4 14.8 %all-to-all-start.1 = ((bf16[128,2,12,128]{3,0,1,2:T(8,128)(2,1)}), bf16[128,2,12,128]{3,0,1,2:T(8,128)(2,1)S(1)}, u32[]{:S(2)}, u32[]{:S(2)}) async-start(bf16[128,2,12,128]{3,0,1,2:T(8,128)(2,1)} %copy.34), calls=%async_computation.1 | async-start | bytes 1572864 | tf_op jit(solution)/shard_map/all_to_all | solution.py:41
  66.2 1.9 %fusion.14 = bf16[24,2,6144]{2,0,1:T(8,128)(2,1)S(1)} fusion(bf16[24,2,6144]{2,0,1:T(8,128)(2,1)} %collective-permute-done.2, bf16[24,2,6144]{2,0,1:T(8,128)(2,1)} %collective-permute-done.1, bf16[24,2,6144]{2,0,1:T(8,128)(2,1)} %collective-permute-done, bf16[4,24,2,6144]{3,1,0,2:T(8,128)(2,1)} %copy-done.1), kind=kLoop, calls=%fused_computation.23 | loop fusion | flops 2359296 | bytes 2949120 | tf_op jit(solution)/shard_map/convert_element_type | solution.py:108
  68.1 3.3 %collective-permute-start.3 = (bf16[24,2,6144]{2,0,1:T(8,128)(2,1)S(1)}, bf16[24,2,6144]{2,0,1:T(8,128)(2,1)S(1)}, u32[]{:S(2)}, u32[]{:S(2)}) collective-permute-start(bf16[24,2,6144]{2,0,1:T(8,128)(2,1)S(1)} %fusion.14), channel_id=1, source_target_pairs={{192,0},{384,192},{576,384},{193,1},{385,193},{577,385},{194,2},{3... | collective-permute-start | bytes 1769480 | tf_op jit(solution)/shard_map/ppermute | solution.py:13
  71.4 27.6 %all-to-all-done.1 = bf16[128,2,12,128]{3,0,1,2:T(8,128)(2,1)S(1)} async-done(((bf16[128,2,12,128]{3,0,1,2:T(8,128)(2,1)}), bf16[128,2,12,128]{3,0,1,2:T(8,128)(2,1)S(1)}, u32[]{:S(2)}, u32[]{:S(2)}) %all-to-all-start.1) | async-done | bytes 786464 | tf_op jit(solution)/shard_map/all_to_all | solution.py:41
  99.8 2.9 %collective-permute-start.4 = (f32[128,128]{1,0:T(8,128)S(1)}, f32[128,128]{1,0:T(8,128)S(1)}, u32[]{:S(2)}, u32[]{:S(2)}) collective-permute-start(f32[128,128]{1,0:T(8,128)S(1)} %dynamic-slice_bitcast_fusion), channel_id=1, source_target_pairs={{0,96},{96,0},{1,97},{97,1},{2,98},{98,2},{3,99},{99,3},{4,100},{1... | collective-permute-start | bytes 196616 | tf_op jit(solution)/shard_map/ppermute | solution.py:45
  102.7 1.4 %copy.36 = bf16[1,1,24,2,6144]{4,3,2,1,0:T(2,128)(2,1)} copy(bf16[1,1,24,2,6144]{4,2,3,1,0:T(8,128)(2,1)S(1)} %bitcast.76) | data formatting | bytes 1179648
  104.1 6.4 %collective-permute-done.4 = f32[128,128]{1,0:T(8,128)S(1)} collective-permute-done((f32[128,128]{1,0:T(8,128)S(1)}, f32[128,128]{1,0:T(8,128)S(1)}, u32[]{:S(2)}, u32[]{:S(2)}) %collective-permute-start.4) | collective-permute-done | bytes 65568 | tf_op jit(solution)/shard_map/ppermute | solution.py:45
  110.5 0.8 fusion.34
  111.4 0.7 copy.37
  (30 shorter events, 6.8 us)
Async XLA Ops:
  0.6 7.1 %copy-start = (bf16[1,6144,1,128]{3,1,2,0:T(8,128)(2,1)S(1)}, bf16[1,6144,1,128]{3,1,2,0:T(8,128)(2,1)}, u32[]{:S(2)}) copy-start(bf16[1,6144,1,128]{3,1,2,0:T(8,128)(2,1)} %param.9) | copy-start | bytes 4718596
  18.9 1.4 %copy-start.1 = (bf16[4,24,2,6144]{3,1,0,2:T(8,128)(2,1)}, bf16[4,24,2,6144]{3,1,0,2:T(8,128)(2,1)S(1)}, u32[]{:S(2)}) copy-start(bf16[4,24,2,6144]{3,1,0,2:T(8,128)(2,1)S(1)} %fusion.1) | copy-start | bytes 7077892
  21.3 44.9 %collective-permute-start.2 = (bf16[24,2,6144]{2,0,1:T(8,128)(2,1)}, bf16[24,2,6144]{2,0,1:T(8,128)(2,1)}, u32[]{:S(2)}, u32[]{:S(2)}) collective-permute-start(bf16[24,2,6144]{2,0,1:T(8,128)(2,1)} %get-tuple-element.14), channel_id=1, source_target_pairs={{0,3},{1,0},{2,1},{3,2},{4,7},{5,4},{6,5},{7,6},{8,11},{9,8},{10,9... | collective-permute-start | bytes 1769480 | tf_op jit(solution)/shard_map/ppermute | solution.py:33
  23.7 42.5 %collective-permute-start.1 = (bf16[24,2,6144]{2,0,1:T(8,128)(2,1)S(1)}, bf16[24,2,6144]{2,0,1:T(8,128)(2,1)}, u32[]{:S(2)}, u32[]{:S(2)}) collective-permute-start(bf16[24,2,6144]{2,0,1:T(8,128)(2,1)S(1)} %get-tuple-element.15), channel_id=1, source_target_pairs={{0,2},{1,3},{2,0},{3,1},{4,6},{5,7},{6,4},{7,5},{8,10},{9,11},{10,... | collective-permute-start | bytes 1769480 | tf_op jit(solution)/shard_map/ppermute | solution.py:33
  28.1 38.2 %collective-permute-start = (bf16[24,2,6144]{2,0,1:T(8,128)(2,1)S(1)}, bf16[24,2,6144]{2,0,1:T(8,128)(2,1)}, u32[]{:S(2)}, u32[]{:S(2)}) collective-permute-start(bf16[24,2,6144]{2,0,1:T(8,128)(2,1)S(1)} %get-tuple-element.13), channel_id=1, source_target_pairs={{0,1},{1,2},{2,3},{3,0},{4,5},{5,6},{6,7},{7,4},{8,9},{9,10},{10,1... | collective-permute-start | bytes 1769480 | tf_op jit(solution)/shard_map/ppermute | solution.py:33
  51.4 47.6 %all-to-all-start.1 = ((bf16[128,2,12,128]{3,0,1,2:T(8,128)(2,1)}), bf16[128,2,12,128]{3,0,1,2:T(8,128)(2,1)S(1)}, u32[]{:S(2)}, u32[]{:S(2)}) async-start(bf16[128,2,12,128]{3,0,1,2:T(8,128)(2,1)} %copy.34), calls=%async_computation.1 | async-start | bytes 1572864 | tf_op jit(solution)/shard_map/all_to_all | solution.py:41
  68.1 34.5 %collective-permute-start.3 = (bf16[24,2,6144]{2,0,1:T(8,128)(2,1)S(1)}, bf16[24,2,6144]{2,0,1:T(8,128)(2,1)S(1)}, u32[]{:S(2)}, u32[]{:S(2)}) collective-permute-start(bf16[24,2,6144]{2,0,1:T(8,128)(2,1)S(1)} %fusion.14), channel_id=1, source_target_pairs={{192,0},{384,192},{576,384},{193,1},{385,193},{577,385},{194,2},{3... | collective-permute-start | bytes 1769480 | tf_op jit(solution)/shard_map/ppermute | solution.py:13
  99.1 0.6 copy-start.2
  99.8 10.8 %collective-permute-start.4 = (f32[128,128]{1,0:T(8,128)S(1)}, f32[128,128]{1,0:T(8,128)S(1)}, u32[]{:S(2)}, u32[]{:S(2)}) collective-permute-start(f32[128,128]{1,0:T(8,128)S(1)} %dynamic-slice_bitcast_fusion), channel_id=1, source_target_pairs={{0,96},{96,0},{1,97},{97,1},{2,98},{98,2},{3,99},{99,3},{4,100},{1... | collective-permute-start | bytes 196616 | tf_op jit(solution)/shard_map/ppermute | solution.py:45

commit v7 on v5

--- a/solution.py
+++ b/solution.py
@@ -1,6 +1,7 @@
 import jax
 import jax.numpy as jnp
 from jax import lax
+from jax.experimental.layout import Layout, with_layout_constraint
 from jax.sharding import Mesh, PartitionSpec as P
 
 BMICRO = 2
@@ -37,9 +38,12 @@
 
 
 def weight_grad_sum(weight_part):
-    pair = lax.all_to_all(weight_part, "dp_core", 2, 2, tiled=True)
-    pair = (pair[:, :, 0] + pair[:, :, 1]).astype(jnp.bfloat16)
-    return jnp.sum(lax.all_to_all(pair, DP_FAR, 1, 1, tiled=True).astype(jnp.float32), axis=1).T
+    n_far = lax.axis_size(DP_FAR)
+    n_core = lax.axis_size("dp_core")
+    blocks = weight_part.reshape(n_far, n_core, weight_part.shape[0] // (n_far * n_core), weight_part.shape[1])
+    pair = lax.all_to_all(blocks, "dp_core", 1, 1, tiled=True)
+    pair = (pair[:, 0].astype(jnp.float32) + pair[:, 1].astype(jnp.float32)).astype(jnp.bfloat16)
+    return jnp.sum(lax.all_to_all(pair, DP_FAR, 0, 0, tiled=True).astype(jnp.float32), axis=0)
 
 
 def head_forward(queries, key_rows, values):
@@ -79,10 +83,8 @@
     key_rows = saved_qkv[:, :, head_size : 2 * head_size]
     values = saved_qkv[:, :, 2 * head_size :]
     softmax, soft_low, attended = jax.vmap(head_forward)(queries, key_rows, values)
-    n_far = lax.axis_size(DP_FAR)
-    n_core = lax.axis_size("dp_core")
-    weight_part = jnp.einsum("msc,msh->hc", gradients, attended, preferred_element_type=jnp.float32)
-    weight_part = weight_part.reshape(weight_part.shape[0], n_far, n_core, -1)
+    weight_part = jnp.einsum("msc,msh->ch", gradients, attended, preferred_element_type=jnp.float32)
+    weight_part = with_layout_constraint(weight_part.astype(jnp.bfloat16), Layout((0, 1)))
     weight_grad = weight_grad_sum(weight_part)
     current = plan[0, :BMICRO]
     grad_heads = jnp.einsum(

time: 109 us -> 96.6 us (0.89)
  local copies, waits for them, and re-layouts: 17.6 us -> 8.08 us
  matrix products: 15.5 us -> 13.6 us
  blocking collectives: 6.26 us -> 5 us
    dot_general x1 -> x0, local copies, waits for them, and re-layouts: 8.09 us -> none  [body(): jnp.einsum('msc,msh->hc', gradients, attended, preferred_element_type=jnp...]
    dot_general x1, matrix products: 4.11 us -> 2 us  [body(): jnp.einsum('msc,msh->ch', gradients, attended, preferred_element_type=jnp...]
    unnamed x6 -> x9, local copies, waits for them, and re-layouts: 3.59 us -> 1.96 us
    all_to_all x1, blocking collectives: 6.26 us -> 5 us  [weight_grad_sum(): pair = lax.all_to_all(blocks, 'dp_core', 1, 1, tiled=True)]
  transfers between devices with their start and end apart: 5 -> 5, of which waited for: 2 -> 2; matrix products, arithmetic and copies ran while one was open for 15% -> 7% of each run, Pallas kernels for 0% -> 0%
where the time goes in v7:
time: 96.6 us; the launch traced here: 95.3 us
  waiting for transfers between devices  31.2 us (32%)
  starting transfers between devices  31.1 us (32%)
  matrix products  13.6 us (14%)
  local copies, waits for them, and re-layouts  8.08 us (8%)
  other arithmetic  5.56 us (6%)
  blocking collectives  5 us (5%)
    ppermute x1, waiting for transfers between devices, shifted(): return lax.ppermute(block, axis, route)  29.7 us
    ppermute x3, starting transfers between devices, rotated_sum(): lax.ppermute(parts[shift], axis, [(i, (i + shift) % n) for i in range(n)])  16.7 us
    all_to_all x1, starting transfers between devices, weight_grad_sum(): lax.all_to_all(pair, DP_FAR, 0, 0, tiled=True).astype(jnp.float32)  13.1 us
    all_to_all x1, blocking collectives, weight_grad_sum(): pair = lax.all_to_all(blocks, 'dp_core', 1, 1, tiled=True)  5 us
    dot_general x1, matrix products, body(): jnp.einsum('bjsk,dk->jsbd', grouped, qkv_proj, preferred_element_type=jnp...  4.68 us
    dot_general x1, matrix products, body(): jnp.einsum('msd,dh->msh', gradients, out_proj, preferred_element_type=jnp...  3.72 us
    dot_general x1, matrix products, body(): jnp.einsum('msc,msh->ch', gradients, attended, preferred_element_type=jnp...  2 us
    unnamed x9, local copies, waits for them, and re-layouts  1.96 us
  transfers between devices with their start and end apart: 5, of which 2 were waited for; matrix products, arithmetic and copies ran while one was open for 7% of the time, Pallas kernels for 0%

profile of v7, /device:TPU:6, one launch (start us, length us, event | category | flops | bytes accessed | tf_op | source)
XLA Modules:
  0.0 95.3 jit_solution(1280090440039525386)
XLA Ops:
  0.6 0.8 fusion.41
  1.4 0.7 compare_and_fusion
  2.1 1.0 %fusion.50 = (bf16[4,96,128]{2,1,0:T(8,128)(2,1)S(1)}, bf16[4,96,128]{2,1,0:T(8,128)(2,1)S(1)}, bf16[4,96,128]{2,1,0:T(8,128)(2,1)S(1)}) fusion(bf16[4,96,384]{2,1,0:T(8,128)(2,1)} %bitcast.70), kind=kLoop, calls=%fused_computation.83 | loop fusion | bytes 589824 | tf_op jit(solution)/shard_map/slice | solution.py:82
  3.2 1.2 %fusion.51 = (f32[4,96]{1,0:T(4,128)S(1)}, f32[4,96,96]{1,2,0:T(8,128)S(1)}) fusion(pred[96,96]{0,1:T(8,128)(4,1)S(1)} %iota_compare_fusion, bf16[4,96,384]{2,1,0:T(8,128)(2,1)} %bitcast.71), kind=kOutput, calls=%fused_computation.84 | convolution fusion | flops 9584735 | bytes 354816 | tf_op jit(solution)/shard_map/vmap()/sub | solution.py:56
  4.4 1.1 %convolution_convert_fusion.1 = bf16[4,96,128]{2,1,0:T(8,128)(2,1)S(1)} fusion(bf16[4,96,96]{1,2,0:T(8,128)(2,1)S(1)} %get-tuple-element.9, bf16[4,96,384]{2,1,0:T(8,128)(2,1)} %bitcast.72), kind=kOutput, calls=%fused_computation.28 | convolution fusion | flops 9486336 | bytes 270336 | tf_op jit(solution)/shard_map/vmap()/dot_general | solution.py:59
  5.5 0.6 gather_fusion.1
  6.6 3.7 %fusion.14 = bf16[4,96,128]{2,1,0:T(8,128)(2,1)S(1)} fusion(bf16[1,6144,1,128]{3,1,2,0:T(8,128)(2,1)S(1)} %copy-done, bf16[1,4,1,96,6144]{4,3,2,1,0:T(8,128)(2,1)} %param.7), kind=kOutput, calls=%fused_computation.27 | convolution fusion | flops 604028928 | bytes 6389760 | tf_op jit(solution)/shard_map/msd,dh->msh/dot_general | solution.py:90
  10.4 0.6 gather_fusion.2
  11.9 0.6 gather_fusion.6
  14.4 4.7 %fusion.2 = bf16[4,24,2,6144]{3,1,0,2:T(8,128)(2,1)S(1)} fusion(bf16[2,4,24,384]{3,2,1,0:T(8,128)(2,1)S(1)} %bitcast.69, bf16[1,6144,1,384]{3,1,2,0:T(8,128)(2,1)} %param.10), kind=kOutput, calls=%fused_computation.11 | convolution fusion | flops 907149312 | bytes 7225344 | tf_op jit(solution)/shard_map/bjsk,dk->jsbd/dot_general | solution.py:107
  19.1 1.1 %slice_bitcast_fusion.2 = (bf16[24,2,6144]{2,0,1:T(8,128)(2,1)}, bf16[24,2,6144]{2,0,1:T(8,128)(2,1)S(1)}, bf16[24,2,6144]{2,0,1:T(8,128)(2,1)S(1)}) fusion(bf16[4,24,2,6144]{3,1,0,2:T(8,128)(2,1)S(1)} %fusion.2), kind=kLoop, calls=%fused_computation.40 | loop fusion | bytes 3538944 | tf_op jit(solution)/shard_map/squeeze | solution.py:35
  20.7 11.4 %collective-permute-start = (bf16[24,2,6144]{2,0,1:T(8,128)(2,1)}, bf16[24,2,6144]{2,0,1:T(8,128)(2,1)}, u32[]{:S(2)}, u32[]{:S(2)}) collective-permute-start(bf16[24,2,6144]{2,0,1:T(8,128)(2,1)} %get-tuple-element.11), channel_id=1, source_target_pairs={{0,1},{1,2},{2,3},{3,0},{4,5},{5,6},{6,7},{7,4},{8,9},{9,10},{10,1... | collective-permute-start | bytes 1769480 | tf_op jit(solution)/shard_map/ppermute | solution.py:35
  32.1 1.9 %collective-permute-start.2 = (bf16[24,2,6144]{2,0,1:T(8,128)(2,1)S(1)}, bf16[24,2,6144]{2,0,1:T(8,128)(2,1)}, u32[]{:S(2)}, u32[]{:S(2)}) collective-permute-start(bf16[24,2,6144]{2,0,1:T(8,128)(2,1)S(1)} %get-tuple-element.12), channel_id=1, source_target_pairs={{0,3},{1,0},{2,1},{3,2},{4,7},{5,4},{6,5},{7,6},{8,11},{9,8},{10,9... | collective-permute-start | bytes 1769480 | tf_op jit(solution)/shard_map/ppermute | solution.py:35
  34.0 3.4 %collective-permute-start.1 = (bf16[24,2,6144]{2,0,1:T(8,128)(2,1)S(1)}, bf16[24,2,6144]{2,0,1:T(8,128)(2,1)}, u32[]{:S(2)}, u32[]{:S(2)}) collective-permute-start(bf16[24,2,6144]{2,0,1:T(8,128)(2,1)S(1)} %get-tuple-element.13), channel_id=1, source_target_pairs={{0,2},{1,3},{2,0},{3,1},{4,6},{5,7},{6,4},{7,5},{8,10},{9,11},{10,... | collective-permute-start | bytes 1769480 | tf_op jit(solution)/shard_map/ppermute | solution.py:35
  37.4 2.0 %fusion.1 = bf16[128,6144]{0,1:T(8,128)(2,1)S(1)} fusion(bf16[4,96,128]{2,1,0:T(8,128)(2,1)S(1)} %convolution_convert_fusion.1, bf16[1,4,1,96,6144]{4,3,2,1,0:T(8,128)(2,1)S(1)} %bitcast.66), kind=kOutput, calls=%fused_computation.10 | convolution fusion | flops 604766208 | bytes 6389760 | tf_op jit(solution)/shard_map/msc,msh->ch/dot_general | solution.py:86
  39.5 5.0 %all_to_all.10 = bf16[24,2,128,128]{3,2,0,1:T(8,128)(2,1)S(1)} all-to-all(bf16[24,2,128,128]{3,2,0,1:T(8,128)(2,1)S(1)} %copy.20), channel_id=1, replica_groups=mesh['pipe'=4,'dp_y'=2,'dp_z'=12,'dp_core'=2,'tensor'=4] {'dp_core'}, dimensions={1} | all-to-all | bytes 3145728 | tf_op jit(solution)/shard_map/all_to_all | solution.py:44
  44.5 1.1 %fusion.23 = bf16[24,128,128]{2,1,0:T(8,128)(2,1)} fusion(bf16[24,2,128,128]{3,2,0,1:T(8,128)(2,1)S(1)} %all_to_all.10), kind=kLoop, calls=%fused_computation.37 | loop fusion | flops 1572864 | bytes 2359296 | tf_op jit(solution)/shard_map/convert_element_type | solution.py:45
  45.7 13.1 %all-to-all-start.1 = ((bf16[24,128,128]{2,1,0:T(8,128)(2,1)}), bf16[24,128,128]{2,1,0:T(8,128)(2,1)S(1)}, u32[]{:S(2)}, u32[]{:S(2)}) async-start(bf16[24,128,128]{2,1,0:T(8,128)(2,1)} %fusion.23), calls=%async_computation.1 | async-start | bytes 1572864 | tf_op jit(solution)/shard_map/all_to_all | solution.py:46
  58.8 1.9 %fusion.10 = bf16[24,2,6144]{2,0,1:T(8,128)(2,1)S(1)} fusion(bf16[24,2,6144]{2,0,1:T(8,128)(2,1)} %collective-permute-done.2, bf16[24,2,6144]{2,0,1:T(8,128)(2,1)} %collective-permute-done.1, bf16[24,2,6144]{2,0,1:T(8,128)(2,1)} %collective-permute-done, bf16[4,24,2,6144]{3,1,0,2:T(8,128)(2,1)} %copy-done.1), kind=kLoop, calls=%fused_computation.22 | loop fusion | flops 2359296 | bytes 2949120 | tf_op jit(solution)/shard_map/convert_element_type | solution.py:109
  60.7 1.3 %collective-permute-start.3 = (bf16[24,2,6144]{2,0,1:T(8,128)(2,1)S(1)}, bf16[24,2,6144]{2,0,1:T(8,128)(2,1)S(1)}, u32[]{:S(2)}, u32[]{:S(2)}) collective-permute-start(bf16[24,2,6144]{2,0,1:T(8,128)(2,1)S(1)} %fusion.10), channel_id=1, source_target_pairs={{192,0},{384,192},{576,384},{193,1},{385,193},{577,385},{194,2},{3... | collective-permute-start | bytes 1769480 | tf_op jit(solution)/shard_map/ppermute | solution.py:15
  62.0 29.7 %collective-permute-done.3 = bf16[24,2,6144]{2,0,1:T(8,128)(2,1)S(1)} collective-permute-done((bf16[24,2,6144]{2,0,1:T(8,128)(2,1)S(1)}, bf16[24,2,6144]{2,0,1:T(8,128)(2,1)S(1)}, u32[]{:S(2)}, u32[]{:S(2)}) %collective-permute-start.3) | collective-permute-done | bytes 589856 | tf_op jit(solution)/shard_map/ppermute | solution.py:15
  91.7 1.4 %copy.21 = bf16[1,1,24,2,6144]{4,3,2,1,0:T(2,128)(2,1)} copy(bf16[1,1,24,2,6144]{4,2,3,1,0:T(8,128)(2,1)S(1)} %bitcast.68) | data formatting | bytes 1179648
  93.2 1.4 %all-to-all-done.1 = bf16[24,128,128]{2,1,0:T(8,128)(2,1)S(1)} async-done(((bf16[24,128,128]{2,1,0:T(8,128)(2,1)}), bf16[24,128,128]{2,1,0:T(8,128)(2,1)S(1)}, u32[]{:S(2)}, u32[]{:S(2)}) %all-to-all-start.1) | async-done | bytes 786464 | tf_op jit(solution)/shard_map/all_to_all | solution.py:46
  94.6 0.7 convert_reduce_fusion
  (27 shorter events, 4.1 us)
Async XLA Ops:
  0.6 6.0 %copy-start = (bf16[1,6144,1,128]{3,1,2,0:T(8,128)(2,1)S(1)}, bf16[1,6144,1,128]{3,1,2,0:T(8,128)(2,1)}, u32[]{:S(2)}) copy-start(bf16[1,6144,1,128]{3,1,2,0:T(8,128)(2,1)} %param.9) | copy-start | bytes 4718596
  14.4 23.0 %slice-start = ((s8[4718592]{0:T(1024)(128)(4,1)}), s8[4194304]{0:T(1024)(128)(4,1)S(1)}, s32[]{:S(2)}) async-start(s8[4718592]{0:T(1024)(128)(4,1)} %bitcast.65), calls=%async_computation.2 | async-start | bytes 8388608
  14.4 23.0 %slice-start.1 = ((s8[4718592]{0:T(1024)(128)(4,1)}), s8[524288]{0:T(1024)(128)(4,1)S(1)}, s32[]{:S(2)}) async-start(s8[4718592]{0:T(1024)(128)(4,1)} %bitcast.65), calls=%async_computation.3 | async-start | bytes 1048576
  19.1 1.6 %copy-start.1 = (bf16[4,24,2,6144]{3,1,0,2:T(8,128)(2,1)}, bf16[4,24,2,6144]{3,1,0,2:T(8,128)(2,1)S(1)}, u32[]{:S(2)}) copy-start(bf16[4,24,2,6144]{3,1,0,2:T(8,128)(2,1)S(1)} %fusion.2) | copy-start | bytes 7077892
  20.7 38.1 %collective-permute-start = (bf16[24,2,6144]{2,0,1:T(8,128)(2,1)}, bf16[24,2,6144]{2,0,1:T(8,128)(2,1)}, u32[]{:S(2)}, u32[]{:S(2)}) collective-permute-start(bf16[24,2,6144]{2,0,1:T(8,128)(2,1)} %get-tuple-element.11), channel_id=1, source_target_pairs={{0,1},{1,2},{2,3},{3,0},{4,5},{5,6},{6,7},{7,4},{8,9},{9,10},{10,1... | collective-permute-start | bytes 1769480 | tf_op jit(solution)/shard_map/ppermute | solution.py:35
  32.1 26.7 %collective-permute-start.2 = (bf16[24,2,6144]{2,0,1:T(8,128)(2,1)S(1)}, bf16[24,2,6144]{2,0,1:T(8,128)(2,1)}, u32[]{:S(2)}, u32[]{:S(2)}) collective-permute-start(bf16[24,2,6144]{2,0,1:T(8,128)(2,1)S(1)} %get-tuple-element.12), channel_id=1, source_target_pairs={{0,3},{1,0},{2,1},{3,2},{4,7},{5,4},{6,5},{7,6},{8,11},{9,8},{10,9... | collective-permute-start | bytes 1769480 | tf_op jit(solution)/shard_map/ppermute | solution.py:35
  34.0 24.8 %collective-permute-start.1 = (bf16[24,2,6144]{2,0,1:T(8,128)(2,1)S(1)}, bf16[24,2,6144]{2,0,1:T(8,128)(2,1)}, u32[]{:S(2)}, u32[]{:S(2)}) collective-permute-start(bf16[24,2,6144]{2,0,1:T(8,128)(2,1)S(1)} %get-tuple-element.13), channel_id=1, source_target_pairs={{0,2},{1,3},{2,0},{3,1},{4,6},{5,7},{6,4},{7,5},{8,10},{9,11},{10,... | collective-permute-start | bytes 1769480 | tf_op jit(solution)/shard_map/ppermute | solution.py:35
  45.7 48.9 %all-to-all-start.1 = ((bf16[24,128,128]{2,1,0:T(8,128)(2,1)}), bf16[24,128,128]{2,1,0:T(8,128)(2,1)S(1)}, u32[]{:S(2)}, u32[]{:S(2)}) async-start(bf16[24,128,128]{2,1,0:T(8,128)(2,1)} %fusion.23), calls=%async_computation.1 | async-start | bytes 1572864 | tf_op jit(solution)/shard_map/all_to_all | solution.py:46
  60.7 31.0 %collective-permute-start.3 = (bf16[24,2,6144]{2,0,1:T(8,128)(2,1)S(1)}, bf16[24,2,6144]{2,0,1:T(8,128)(2,1)S(1)}, u32[]{:S(2)}, u32[]{:S(2)}) collective-permute-start(bf16[24,2,6144]{2,0,1:T(8,128)(2,1)S(1)} %fusion.10), channel_id=1, source_target_pairs={{192,0},{384,192},{576,384},{193,1},{385,193},{577,385},{194,2},{3... | collective-permute-start | bytes 1769480 | tf_op jit(solution)/shard_map/ppermute | solution.py:15

commit v8 on v7

--- a/solution.py
+++ b/solution.py
@@ -87,8 +87,9 @@
     weight_part = with_layout_constraint(weight_part.astype(jnp.bfloat16), Layout((0, 1)))
     weight_grad = weight_grad_sum(weight_part)
     current = plan[0, :BMICRO]
+    grad_rows = jnp.stack([lax.dynamic_index_in_dim(gradients, current[j], 0, keepdims=False) for j in range(BMICRO)])
     grad_heads = jnp.einsum(
-        "msd,dh->msh", gradients, out_proj, preferred_element_type=jnp.float32
+        "msd,dh->msh", grad_rows, out_proj, preferred_element_type=jnp.float32
     ).astype(jnp.bfloat16)
     grad_qkv = jax.vmap(head_backward)(
         jnp.take(queries, current, axis=0),
@@ -97,7 +98,7 @@
         jnp.take(softmax, current, axis=0),
         jnp.take(soft_low, current, axis=0),
         jnp.take(attended, current, axis=0),
-        jnp.take(grad_heads, current, axis=0),
+        grad_heads,
     )
     n_tensor = lax.axis_size("tensor")
     seq_len = grad_qkv.shape[1]
@@ -107,7 +108,8 @@
     partials = jnp.einsum("bjsk,dk->jsbd", grouped, qkv_proj, preferred_element_type=jnp.float32)
     own_rows = rotated_sum(partials.astype(jnp.bfloat16), "tensor")
     received = shifted(own_rows.astype(jnp.bfloat16), "pipe", -1)
-    return (received[None, None], weight_grad[None, :, None, :])
+    weight_grad = with_layout_constraint(weight_grad[None, :, None, :], Layout((0, 1, 2, 3)))
+    return (received[None, None], weight_grad)
 
 
 def solution(mesh):

time: 96.6 us -> 100 us (1.035)
  between operations: 0.91 us -> 4.8 us
  matrix products: 13.6 us -> 10.7 us
  local copies, waits for them, and re-layouts: 8.08 us -> 10.6 us
    dot_general x1, matrix products: 3.72 us -> 0.88 us  [body(): jnp.einsum('msd,dh->msh', grad_rows, out_proj, preferred_element_type=jnp...]
    dynamic_slice x0 -> x1, local copies, waits for them, and re-layouts: none -> 1.79 us  [body(): lax.dynamic_index_in_dim(gradients, current[j], 0, keepdims=False)]
    slice x0 -> x1, local copies, waits for them, and re-layouts: none -> 1.31 us  [body(): current[j]]
where the time goes in v8:
time: 100 us; the launch traced here: 98.7 us
  waiting for transfers between devices  31.2 us (31%)
  starting transfers between devices  31.1 us (31%)
  matrix products  10.7 us (11%)
  local copies, waits for them, and re-layouts  10.6 us (11%)
  other arithmetic  5.38 us (5%)
  blocking collectives  5 us (5%)
  between operations  4.8 us (5%)
    ppermute x1, waiting for transfers between devices, shifted(): return lax.ppermute(block, axis, route)  29.7 us
    ppermute x3, starting transfers between devices, rotated_sum(): lax.ppermute(parts[shift], axis, [(i, (i + shift) % n) for i in range(n)])  16.7 us
    all_to_all x1, starting transfers between devices, weight_grad_sum(): lax.all_to_all(pair, DP_FAR, 0, 0, tiled=True).astype(jnp.float32)  13.1 us
    all_to_all x1, blocking collectives, weight_grad_sum(): pair = lax.all_to_all(blocks, 'dp_core', 1, 1, tiled=True)  5 us
    dot_general x1, matrix products, body(): jnp.einsum('bjsk,dk->jsbd', grouped, qkv_proj, preferred_element_type=jnp...  4.67 us
    dot_general x1, matrix products, body(): jnp.einsum('msc,msh->ch', gradients, attended, preferred_element_type=jnp...  2 us
  transfers between devices with their start and end apart: 5, of which 2 were waited for; matrix products, arithmetic and copies ran while one was open for 7% of the time, Pallas kernels for 0%

profile of v8, /device:TPU:6, one launch (start us, length us, event | category | flops | bytes accessed | tf_op | source)
XLA Modules:
  0.0 98.7 jit_solution(17086836737741245292)
XLA Ops:
  0.6 0.8 fusion.43
  1.4 0.7 compare_and_fusion
  2.1 1.3 %fusion.54 = (s32[1,1]{1,0:T(1,128)}, s32[1,1]{1,0:T(1,128)}) fusion(s32[1,4]{1,0:T(1,128)} %param.11), kind=kLoop, calls=%fused_computation.87 | loop fusion | bytes 16 | tf_op jit(solution)/shard_map/slice | solution.py:90
  6.0 1.0 %fusion.53 = (bf16[4,96,128]{2,1,0:T(8,128)(2,1)S(1)}, bf16[4,96,128]{2,1,0:T(8,128)(2,1)S(1)}, bf16[4,96,128]{2,1,0:T(8,128)(2,1)S(1)}) fusion(bf16[4,96,384]{2,1,0:T(8,128)(2,1)} %bitcast.76), kind=kLoop, calls=%fused_computation.86 | loop fusion | bytes 589824 | tf_op jit(solution)/shard_map/slice | solution.py:82
  7.1 1.2 %fusion.55 = (f32[4,96]{1,0:T(4,128)S(1)}, f32[4,96,96]{1,2,0:T(8,128)S(1)}) fusion(pred[96,96]{0,1:T(8,128)(4,1)S(1)} %iota_compare_fusion, bf16[4,96,384]{2,1,0:T(8,128)(2,1)} %bitcast.77), kind=kOutput, calls=%fused_computation.88 | convolution fusion | flops 9584735 | bytes 354816 | tf_op jit(solution)/shard_map/vmap()/sub | solution.py:56
  8.3 1.1 %convolution_convert_fusion.1 = bf16[4,96,128]{2,1,0:T(8,128)(2,1)S(1)} fusion(bf16[4,96,96]{1,2,0:T(8,128)(2,1)S(1)} %get-tuple-element.9, bf16[4,96,384]{2,1,0:T(8,128)(2,1)} %bitcast.78), kind=kOutput, calls=%fused_computation.30 | convolution fusion | flops 9486336 | bytes 270336 | tf_op jit(solution)/shard_map/vmap()/dot_general | solution.py:59
  9.4 0.6 gather_fusion.1
  14.1 1.8 %dynamic-slice_bitcast_fusion.1 = (bf16[1,96,6144]{2,1,0:T(8,128)(2,1)S(1)}, bf16[1,96,6144]{2,1,0:T(8,128)(2,1)S(1)}) fusion(bf16[1,4,1,96,6144]{4,3,2,1,0:T(8,128)(2,1)} %param.7, s32[]{:T(128)S(6)} %select_n.50, s32[]{:T(128)S(6)} %select_n.51), kind=kLoop, calls=%fused_computation.25 | loop fusion | bytes 4718600 | tf_op jit(solution)/shard_map/jit(dynamic_index_in_dim)/dynamic_slice | solution.py:90
  15.9 0.9 multiply_reduce_fusion
  17.8 4.7 %fusion.2 = bf16[4,24,2,6144]{3,1,0,2:T(8,128)(2,1)S(1)} fusion(bf16[2,4,24,384]{3,2,1,0:T(8,128)(2,1)S(1)} %bitcast.75, bf16[1,6144,1,384]{3,1,2,0:T(8,128)(2,1)} %param.10), kind=kOutput, calls=%fused_computation.10 | convolution fusion | flops 907149312 | bytes 7225344 | tf_op jit(solution)/shard_map/bjsk,dk->jsbd/dot_general | solution.py:108
  22.5 1.1 %slice_bitcast_fusion.2 = (bf16[24,2,6144]{2,0,1:T(8,128)(2,1)}, bf16[24,2,6144]{2,0,1:T(8,128)(2,1)S(1)}, bf16[24,2,6144]{2,0,1:T(8,128)(2,1)S(1)}) fusion(bf16[4,24,2,6144]{3,1,0,2:T(8,128)(2,1)S(1)} %fusion.2), kind=kLoop, calls=%fused_computation.43 | loop fusion | bytes 3538944 | tf_op jit(solution)/shard_map/squeeze | solution.py:35
  24.1 11.4 %collective-permute-start = (bf16[24,2,6144]{2,0,1:T(8,128)(2,1)}, bf16[24,2,6144]{2,0,1:T(8,128)(2,1)}, u32[]{:S(2)}, u32[]{:S(2)}) collective-permute-start(bf16[24,2,6144]{2,0,1:T(8,128)(2,1)} %get-tuple-element.13), channel_id=1, source_target_pairs={{0,1},{1,2},{2,3},{3,0},{4,5},{5,6},{6,7},{7,4},{8,9},{9,10},{10,1... | collective-permute-start | bytes 1769480 | tf_op jit(solution)/shard_map/ppermute | solution.py:35
  35.5 1.9 %collective-permute-start.2 = (bf16[24,2,6144]{2,0,1:T(8,128)(2,1)S(1)}, bf16[24,2,6144]{2,0,1:T(8,128)(2,1)}, u32[]{:S(2)}, u32[]{:S(2)}) collective-permute-start(bf16[24,2,6144]{2,0,1:T(8,128)(2,1)S(1)} %get-tuple-element.14), channel_id=1, source_target_pairs={{0,3},{1,0},{2,1},{3,2},{4,7},{5,4},{6,5},{7,6},{8,11},{9,8},{10,9... | collective-permute-start | bytes 1769480 | tf_op jit(solution)/shard_map/ppermute | solution.py:35
  37.4 3.4 %collective-permute-start.1 = (bf16[24,2,6144]{2,0,1:T(8,128)(2,1)S(1)}, bf16[24,2,6144]{2,0,1:T(8,128)(2,1)}, u32[]{:S(2)}, u32[]{:S(2)}) collective-permute-start(bf16[24,2,6144]{2,0,1:T(8,128)(2,1)S(1)} %get-tuple-element.15), channel_id=1, source_target_pairs={{0,2},{1,3},{2,0},{3,1},{4,6},{5,7},{6,4},{7,5},{8,10},{9,11},{10,... | collective-permute-start | bytes 1769480 | tf_op jit(solution)/shard_map/ppermute | solution.py:35
  40.8 2.0 %fusion.1 = bf16[128,6144]{0,1:T(8,128)(2,1)S(1)} fusion(bf16[4,96,128]{2,1,0:T(8,128)(2,1)S(1)} %convolution_convert_fusion.1, bf16[1,4,1,96,6144]{4,3,2,1,0:T(8,128)(2,1)S(1)} %bitcast.72), kind=kOutput, calls=%fused_computation.9 | convolution fusion | flops 604766208 | bytes 6389760 | tf_op jit(solution)/shard_map/msc,msh->ch/dot_general | solution.py:86
  42.9 5.0 %all_to_all.10 = bf16[24,2,128,128]{3,2,0,1:T(8,128)(2,1)S(1)} all-to-all(bf16[24,2,128,128]{3,2,0,1:T(8,128)(2,1)S(1)} %copy.20), channel_id=1, replica_groups=mesh['pipe'=4,'dp_y'=2,'dp_z'=12,'dp_core'=2,'tensor'=4] {'dp_core'}, dimensions={1} | all-to-all | bytes 3145728 | tf_op jit(solution)/shard_map/all_to_all | solution.py:44
  47.9 1.1 %fusion.25 = bf16[24,128,128]{2,1,0:T(8,128)(2,1)} fusion(bf16[24,2,128,128]{3,2,0,1:T(8,128)(2,1)S(1)} %all_to_all.10), kind=kLoop, calls=%fused_computation.40 | loop fusion | flops 1572864 | bytes 2359296 | tf_op jit(solution)/shard_map/convert_element_type | solution.py:45
  49.1 13.1 %all-to-all-start.1 = ((bf16[24,128,128]{2,1,0:T(8,128)(2,1)}), bf16[24,128,128]{2,1,0:T(8,128)(2,1)S(1)}, u32[]{:S(2)}, u32[]{:S(2)}) async-start(bf16[24,128,128]{2,1,0:T(8,128)(2,1)} %fusion.25), calls=%async_computation.1 | async-start | bytes 1572864 | tf_op jit(solution)/shard_map/all_to_all | solution.py:46
  62.2 1.9 %fusion.12 = bf16[24,2,6144]{2,0,1:T(8,128)(2,1)S(1)} fusion(bf16[24,2,6144]{2,0,1:T(8,128)(2,1)} %collective-permute-done.2, bf16[24,2,6144]{2,0,1:T(8,128)(2,1)} %collective-permute-done.1, bf16[24,2,6144]{2,0,1:T(8,128)(2,1)} %collective-permute-done, bf16[4,24,2,6144]{3,1,0,2:T(8,128)(2,1)} %copy-done.1), kind=kLoop, calls=%fused_computation.23 | loop fusion | flops 2359296 | bytes 2949120 | tf_op jit(solution)/shard_map/convert_element_type | solution.py:110
  64.1 1.3 %collective-permute-start.3 = (bf16[24,2,6144]{2,0,1:T(8,128)(2,1)S(1)}, bf16[24,2,6144]{2,0,1:T(8,128)(2,1)S(1)}, u32[]{:S(2)}, u32[]{:S(2)}) collective-permute-start(bf16[24,2,6144]{2,0,1:T(8,128)(2,1)S(1)} %fusion.12), channel_id=1, source_target_pairs={{192,0},{384,192},{576,384},{193,1},{385,193},{577,385},{194,2},{3... | collective-permute-start | bytes 1769480 | tf_op jit(solution)/shard_map/ppermute | solution.py:15
  65.4 29.7 %collective-permute-done.3 = bf16[24,2,6144]{2,0,1:T(8,128)(2,1)S(1)} collective-permute-done((bf16[24,2,6144]{2,0,1:T(8,128)(2,1)S(1)}, bf16[24,2,6144]{2,0,1:T(8,128)(2,1)S(1)}, u32[]{:S(2)}, u32[]{:S(2)}) %collective-permute-start.3) | collective-permute-done | bytes 589856 | tf_op jit(solution)/shard_map/ppermute | solution.py:15
  95.1 1.4 %copy.21 = bf16[1,1,24,2,6144]{4,3,2,1,0:T(2,128)(2,1)} copy(bf16[1,1,24,2,6144]{4,2,3,1,0:T(8,128)(2,1)S(1)} %bitcast.74) | data formatting | bytes 1179648
  96.5 1.4 %all-to-all-done.1 = bf16[24,128,128]{2,1,0:T(8,128)(2,1)S(1)} async-done(((bf16[24,128,128]{2,1,0:T(8,128)(2,1)}), bf16[24,128,128]{2,1,0:T(8,128)(2,1)S(1)}, u32[]{:S(2)}, u32[]{:S(2)}) %all-to-all-start.1) | async-done | bytes 786464 | tf_op jit(solution)/shard_map/all_to_all | solution.py:46
  98.0 0.7 convert_reduce_fusion
  (27 shorter events, 4.5 us)
Async XLA Ops:
  0.6 15.3 %copy-start = (bf16[1,6144,1,128]{3,1,2,0:T(8,128)(2,1)S(1)}, bf16[1,6144,1,128]{3,1,2,0:T(8,128)(2,1)}, u32[]{:S(2)}) copy-start(bf16[1,6144,1,128]{3,1,2,0:T(8,128)(2,1)} %param.9) | copy-start | bytes 4718596
  17.8 23.0 %slice-start = ((s8[4718592]{0:T(1024)(128)(4,1)}), s8[4194304]{0:T(1024)(128)(4,1)S(1)}, s32[]{:S(2)}) async-start(s8[4718592]{0:T(1024)(128)(4,1)} %bitcast.71), calls=%async_computation.2 | async-start | bytes 8388608
  17.8 23.0 %slice-start.1 = ((s8[4718592]{0:T(1024)(128)(4,1)}), s8[524288]{0:T(1024)(128)(4,1)S(1)}, s32[]{:S(2)}) async-start(s8[4718592]{0:T(1024)(128)(4,1)} %bitcast.71), calls=%async_computation.3 | async-start | bytes 1048576
  22.5 1.6 %copy-start.1 = (bf16[4,24,2,6144]{3,1,0,2:T(8,128)(2,1)}, bf16[4,24,2,6144]{3,1,0,2:T(8,128)(2,1)S(1)}, u32[]{:S(2)}) copy-start(bf16[4,24,2,6144]{3,1,0,2:T(8,128)(2,1)S(1)} %fusion.2) | copy-start | bytes 7077892
  24.1 38.1 %collective-permute-start = (bf16[24,2,6144]{2,0,1:T(8,128)(2,1)}, bf16[24,2,6144]{2,0,1:T(8,128)(2,1)}, u32[]{:S(2)}, u32[]{:S(2)}) collective-permute-start(bf16[24,2,6144]{2,0,1:T(8,128)(2,1)} %get-tuple-element.13), channel_id=1, source_target_pairs={{0,1},{1,2},{2,3},{3,0},{4,5},{5,6},{6,7},{7,4},{8,9},{9,10},{10,1... | collective-permute-start | bytes 1769480 | tf_op jit(solution)/shard_map/ppermute | solution.py:35
  35.5 26.7 %collective-permute-start.2 = (bf16[24,2,6144]{2,0,1:T(8,128)(2,1)S(1)}, bf16[24,2,6144]{2,0,1:T(8,128)(2,1)}, u32[]{:S(2)}, u32[]{:S(2)}) collective-permute-start(bf16[24,2,6144]{2,0,1:T(8,128)(2,1)S(1)} %get-tuple-element.14), channel_id=1, source_target_pairs={{0,3},{1,0},{2,1},{3,2},{4,7},{5,4},{6,5},{7,6},{8,11},{9,8},{10,9... | collective-permute-start | bytes 1769480 | tf_op jit(solution)/shard_map/ppermute | solution.py:35
  37.4 24.8 %collective-permute-start.1 = (bf16[24,2,6144]{2,0,1:T(8,128)(2,1)S(1)}, bf16[24,2,6144]{2,0,1:T(8,128)(2,1)}, u32[]{:S(2)}, u32[]{:S(2)}) collective-permute-start(bf16[24,2,6144]{2,0,1:T(8,128)(2,1)S(1)} %get-tuple-element.15), channel_id=1, source_target_pairs={{0,2},{1,3},{2,0},{3,1},{4,6},{5,7},{6,4},{7,5},{8,10},{9,11},{10,... | collective-permute-start | bytes 1769480 | tf_op jit(solution)/shard_map/ppermute | solution.py:35
  49.1 48.9 %all-to-all-start.1 = ((bf16[24,128,128]{2,1,0:T(8,128)(2,1)}), bf16[24,128,128]{2,1,0:T(8,128)(2,1)S(1)}, u32[]{:S(2)}, u32[]{:S(2)}) async-start(bf16[24,128,128]{2,1,0:T(8,128)(2,1)} %fusion.25), calls=%async_computation.1 | async-start | bytes 1572864 | tf_op jit(solution)/shard_map/all_to_all | solution.py:46
  64.1 31.0 %collective-permute-start.3 = (bf16[24,2,6144]{2,0,1:T(8,128)(2,1)S(1)}, bf16[24,2,6144]{2,0,1:T(8,128)(2,1)S(1)}, u32[]{:S(2)}, u32[]{:S(2)}) collective-permute-start(bf16[24,2,6144]{2,0,1:T(8,128)(2,1)S(1)} %fusion.12), channel_id=1, source_target_pairs={{192,0},{384,192},{576,384},{193,1},{385,193},{577,385},{194,2},{3... | collective-permute-start | bytes 1769480 | tf_op jit(solution)/shard_map/ppermute | solution.py:15

commit v9 on v7

--- a/solution.py
+++ b/solution.py
@@ -107,7 +107,8 @@
     partials = jnp.einsum("bjsk,dk->jsbd", grouped, qkv_proj, preferred_element_type=jnp.float32)
     own_rows = rotated_sum(partials.astype(jnp.bfloat16), "tensor")
     received = shifted(own_rows.astype(jnp.bfloat16), "pipe", -1)
-    return (received[None, None], weight_grad[None, :, None, :])
+    weight_grad = with_layout_constraint(weight_grad[None, :, None, :], Layout((0, 1, 2, 3)))
+    return (received[None, None], weight_grad)
 
 
 def solution(mesh):

time: 96.6 us -> 96.6 us (level)
  no operation moved by 1% of the time
where the time goes in v9:
time: 96.6 us; the launch traced here: 95.3 us
  waiting for transfers between devices  31.2 us (32%)
  starting transfers between devices  31.1 us (32%)
  matrix products  13.6 us (14%)
  local copies, waits for them, and re-layouts  8.08 us (8%)
  other arithmetic  5.56 us (6%)
  blocking collectives  5 us (5%)
    ppermute x1, waiting for transfers between devices, shifted(): return lax.ppermute(block, axis, route)  29.7 us
    ppermute x3, starting transfers between devices, rotated_sum(): lax.ppermute(parts[shift], axis, [(i, (i + shift) % n) for i in range(n)])  16.7 us
    all_to_all x1, starting transfers between devices, weight_grad_sum(): lax.all_to_all(pair, DP_FAR, 0, 0, tiled=True).astype(jnp.float32)  13.1 us
    all_to_all x1, blocking collectives, weight_grad_sum(): pair = lax.all_to_all(blocks, 'dp_core', 1, 1, tiled=True)  5 us
    dot_general x1, matrix products, body(): jnp.einsum('bjsk,dk->jsbd', grouped, qkv_proj, preferred_element_type=jnp...  4.68 us
    dot_general x1, matrix products, body(): jnp.einsum('msd,dh->msh', gradients, out_proj, preferred_element_type=jnp...  3.72 us
    dot_general x1, matrix products, body(): jnp.einsum('msc,msh->ch', gradients, attended, preferred_element_type=jnp...  2 us
    unnamed x9, local copies, waits for them, and re-layouts  1.96 us
  transfers between devices with their start and end apart: 5, of which 2 were waited for; matrix products, arithmetic and copies ran while one was open for 7% of the time, Pallas kernels for 0%

profile of v9, /device:TPU:6, one launch (start us, length us, event | category | flops | bytes accessed | tf_op | source)
XLA Modules:
  0.0 95.3 jit_solution(1280090440039525386)
XLA Ops:
  0.6 0.8 fusion.41
  1.4 0.7 compare_and_fusion
  2.1 1.0 %fusion.50 = (bf16[4,96,128]{2,1,0:T(8,128)(2,1)S(1)}, bf16[4,96,128]{2,1,0:T(8,128)(2,1)S(1)}, bf16[4,96,128]{2,1,0:T(8,128)(2,1)S(1)}) fusion(bf16[4,96,384]{2,1,0:T(8,128)(2,1)} %bitcast.70), kind=kLoop, calls=%fused_computation.83 | loop fusion | bytes 589824 | tf_op jit(solution)/shard_map/slice | solution.py:82
  3.2 1.2 %fusion.51 = (f32[4,96]{1,0:T(4,128)S(1)}, f32[4,96,96]{1,2,0:T(8,128)S(1)}) fusion(pred[96,96]{0,1:T(8,128)(4,1)S(1)} %iota_compare_fusion, bf16[4,96,384]{2,1,0:T(8,128)(2,1)} %bitcast.71), kind=kOutput, calls=%fused_computation.84 | convolution fusion | flops 9584735 | bytes 354816 | tf_op jit(solution)/shard_map/vmap()/sub | solution.py:56
  4.4 1.1 %convolution_convert_fusion.1 = bf16[4,96,128]{2,1,0:T(8,128)(2,1)S(1)} fusion(bf16[4,96,96]{1,2,0:T(8,128)(2,1)S(1)} %get-tuple-element.9, bf16[4,96,384]{2,1,0:T(8,128)(2,1)} %bitcast.72), kind=kOutput, calls=%fused_computation.28 | convolution fusion | flops 9486336 | bytes 270336 | tf_op jit(solution)/shard_map/vmap()/dot_general | solution.py:59
  5.5 0.6 gather_fusion.1
  6.6 3.7 %fusion.14 = bf16[4,96,128]{2,1,0:T(8,128)(2,1)S(1)} fusion(bf16[1,6144,1,128]{3,1,2,0:T(8,128)(2,1)S(1)} %copy-done, bf16[1,4,1,96,6144]{4,3,2,1,0:T(8,128)(2,1)} %param.7), kind=kOutput, calls=%fused_computation.27 | convolution fusion | flops 604028928 | bytes 6389760 | tf_op jit(solution)/shard_map/msd,dh->msh/dot_general | solution.py:90
  10.4 0.6 gather_fusion.2
  11.9 0.6 gather_fusion.6
  14.4 4.7 %fusion.2 = bf16[4,24,2,6144]{3,1,0,2:T(8,128)(2,1)S(1)} fusion(bf16[2,4,24,384]{3,2,1,0:T(8,128)(2,1)S(1)} %bitcast.69, bf16[1,6144,1,384]{3,1,2,0:T(8,128)(2,1)} %param.10), kind=kOutput, calls=%fused_computation.11 | convolution fusion | flops 907149312 | bytes 7225344 | tf_op jit(solution)/shard_map/bjsk,dk->jsbd/dot_general | solution.py:107
  19.1 1.1 %slice_bitcast_fusion.2 = (bf16[24,2,6144]{2,0,1:T(8,128)(2,1)}, bf16[24,2,6144]{2,0,1:T(8,128)(2,1)S(1)}, bf16[24,2,6144]{2,0,1:T(8,128)(2,1)S(1)}) fusion(bf16[4,24,2,6144]{3,1,0,2:T(8,128)(2,1)S(1)} %fusion.2), kind=kLoop, calls=%fused_computation.40 | loop fusion | bytes 3538944 | tf_op jit(solution)/shard_map/squeeze | solution.py:35
  20.7 11.4 %collective-permute-start = (bf16[24,2,6144]{2,0,1:T(8,128)(2,1)}, bf16[24,2,6144]{2,0,1:T(8,128)(2,1)}, u32[]{:S(2)}, u32[]{:S(2)}) collective-permute-start(bf16[24,2,6144]{2,0,1:T(8,128)(2,1)} %get-tuple-element.11), channel_id=1, source_target_pairs={{0,1},{1,2},{2,3},{3,0},{4,5},{5,6},{6,7},{7,4},{8,9},{9,10},{10,1... | collective-permute-start | bytes 1769480 | tf_op jit(solution)/shard_map/ppermute | solution.py:35
  32.1 1.9 %collective-permute-start.2 = (bf16[24,2,6144]{2,0,1:T(8,128)(2,1)S(1)}, bf16[24,2,6144]{2,0,1:T(8,128)(2,1)}, u32[]{:S(2)}, u32[]{:S(2)}) collective-permute-start(bf16[24,2,6144]{2,0,1:T(8,128)(2,1)S(1)} %get-tuple-element.12), channel_id=1, source_target_pairs={{0,3},{1,0},{2,1},{3,2},{4,7},{5,4},{6,5},{7,6},{8,11},{9,8},{10,9... | collective-permute-start | bytes 1769480 | tf_op jit(solution)/shard_map/ppermute | solution.py:35
  34.0 3.4 %collective-permute-start.1 = (bf16[24,2,6144]{2,0,1:T(8,128)(2,1)S(1)}, bf16[24,2,6144]{2,0,1:T(8,128)(2,1)}, u32[]{:S(2)}, u32[]{:S(2)}) collective-permute-start(bf16[24,2,6144]{2,0,1:T(8,128)(2,1)S(1)} %get-tuple-element.13), channel_id=1, source_target_pairs={{0,2},{1,3},{2,0},{3,1},{4,6},{5,7},{6,4},{7,5},{8,10},{9,11},{10,... | collective-permute-start | bytes 1769480 | tf_op jit(solution)/shard_map/ppermute | solution.py:35
  37.4 2.0 %fusion.1 = bf16[128,6144]{0,1:T(8,128)(2,1)S(1)} fusion(bf16[4,96,128]{2,1,0:T(8,128)(2,1)S(1)} %convolution_convert_fusion.1, bf16[1,4,1,96,6144]{4,3,2,1,0:T(8,128)(2,1)S(1)} %bitcast.66), kind=kOutput, calls=%fused_computation.10 | convolution fusion | flops 604766208 | bytes 6389760 | tf_op jit(solution)/shard_map/msc,msh->ch/dot_general | solution.py:86
  39.5 5.0 %all_to_all.10 = bf16[24,2,128,128]{3,2,0,1:T(8,128)(2,1)S(1)} all-to-all(bf16[24,2,128,128]{3,2,0,1:T(8,128)(2,1)S(1)} %copy.20), channel_id=1, replica_groups=mesh['pipe'=4,'dp_y'=2,'dp_z'=12,'dp_core'=2,'tensor'=4] {'dp_core'}, dimensions={1} | all-to-all | bytes 3145728 | tf_op jit(solution)/shard_map/all_to_all | solution.py:44
  44.5 1.1 %fusion.23 = bf16[24,128,128]{2,1,0:T(8,128)(2,1)} fusion(bf16[24,2,128,128]{3,2,0,1:T(8,128)(2,1)S(1)} %all_to_all.10), kind=kLoop, calls=%fused_computation.37 | loop fusion | flops 1572864 | bytes 2359296 | tf_op jit(solution)/shard_map/convert_element_type | solution.py:45
  45.7 13.1 %all-to-all-start.1 = ((bf16[24,128,128]{2,1,0:T(8,128)(2,1)}), bf16[24,128,128]{2,1,0:T(8,128)(2,1)S(1)}, u32[]{:S(2)}, u32[]{:S(2)}) async-start(bf16[24,128,128]{2,1,0:T(8,128)(2,1)} %fusion.23), calls=%async_computation.1 | async-start | bytes 1572864 | tf_op jit(solution)/shard_map/all_to_all | solution.py:46
  58.8 1.9 %fusion.10 = bf16[24,2,6144]{2,0,1:T(8,128)(2,1)S(1)} fusion(bf16[24,2,6144]{2,0,1:T(8,128)(2,1)} %collective-permute-done.2, bf16[24,2,6144]{2,0,1:T(8,128)(2,1)} %collective-permute-done.1, bf16[24,2,6144]{2,0,1:T(8,128)(2,1)} %collective-permute-done, bf16[4,24,2,6144]{3,1,0,2:T(8,128)(2,1)} %copy-done.1), kind=kLoop, calls=%fused_computation.22 | loop fusion | flops 2359296 | bytes 2949120 | tf_op jit(solution)/shard_map/convert_element_type | solution.py:109
  60.7 1.3 %collective-permute-start.3 = (bf16[24,2,6144]{2,0,1:T(8,128)(2,1)S(1)}, bf16[24,2,6144]{2,0,1:T(8,128)(2,1)S(1)}, u32[]{:S(2)}, u32[]{:S(2)}) collective-permute-start(bf16[24,2,6144]{2,0,1:T(8,128)(2,1)S(1)} %fusion.10), channel_id=1, source_target_pairs={{192,0},{384,192},{576,384},{193,1},{385,193},{577,385},{194,2},{3... | collective-permute-start | bytes 1769480 | tf_op jit(solution)/shard_map/ppermute | solution.py:15
  62.0 29.7 %collective-permute-done.3 = bf16[24,2,6144]{2,0,1:T(8,128)(2,1)S(1)} collective-permute-done((bf16[24,2,6144]{2,0,1:T(8,128)(2,1)S(1)}, bf16[24,2,6144]{2,0,1:T(8,128)(2,1)S(1)}, u32[]{:S(2)}, u32[]{:S(2)}) %collective-permute-start.3) | collective-permute-done | bytes 589856 | tf_op jit(solution)/shard_map/ppermute | solution.py:15
  91.7 1.4 %copy.21 = bf16[1,1,24,2,6144]{4,3,2,1,0:T(2,128)(2,1)} copy(bf16[1,1,24,2,6144]{4,2,3,1,0:T(8,128)(2,1)S(1)} %bitcast.68) | data formatting | bytes 1179648
  93.2 1.4 %all-to-all-done.1 = bf16[24,128,128]{2,1,0:T(8,128)(2,1)S(1)} async-done(((bf16[24,128,128]{2,1,0:T(8,128)(2,1)}), bf16[24,128,128]{2,1,0:T(8,128)(2,1)S(1)}, u32[]{:S(2)}, u32[]{:S(2)}) %all-to-all-start.1) | async-done | bytes 786464 | tf_op jit(solution)/shard_map/all_to_all | solution.py:46
  94.6 0.7 convert_reduce_fusion
  (27 shorter events, 4.1 us)
Async XLA Ops:
  0.6 6.0 %copy-start = (bf16[1,6144,1,128]{3,1,2,0:T(8,128)(2,1)S(1)}, bf16[1,6144,1,128]{3,1,2,0:T(8,128)(2,1)}, u32[]{:S(2)}) copy-start(bf16[1,6144,1,128]{3,1,2,0:T(8,128)(2,1)} %param.9) | copy-start | bytes 4718596
  14.4 23.0 %slice-start = ((s8[4718592]{0:T(1024)(128)(4,1)}), s8[4194304]{0:T(1024)(128)(4,1)S(1)}, s32[]{:S(2)}) async-start(s8[4718592]{0:T(1024)(128)(4,1)} %bitcast.65), calls=%async_computation.2 | async-start | bytes 8388608
  14.4 23.0 %slice-start.1 = ((s8[4718592]{0:T(1024)(128)(4,1)}), s8[524288]{0:T(1024)(128)(4,1)S(1)}, s32[]{:S(2)}) async-start(s8[4718592]{0:T(1024)(128)(4,1)} %bitcast.65), calls=%async_computation.3 | async-start | bytes 1048576
  19.1 1.6 %copy-start.1 = (bf16[4,24,2,6144]{3,1,0,2:T(8,128)(2,1)}, bf16[4,24,2,6144]{3,1,0,2:T(8,128)(2,1)S(1)}, u32[]{:S(2)}) copy-start(bf16[4,24,2,6144]{3,1,0,2:T(8,128)(2,1)S(1)} %fusion.2) | copy-start | bytes 7077892
  20.7 38.1 %collective-permute-start = (bf16[24,2,6144]{2,0,1:T(8,128)(2,1)}, bf16[24,2,6144]{2,0,1:T(8,128)(2,1)}, u32[]{:S(2)}, u32[]{:S(2)}) collective-permute-start(bf16[24,2,6144]{2,0,1:T(8,128)(2,1)} %get-tuple-element.11), channel_id=1, source_target_pairs={{0,1},{1,2},{2,3},{3,0},{4,5},{5,6},{6,7},{7,4},{8,9},{9,10},{10,1... | collective-permute-start | bytes 1769480 | tf_op jit(solution)/shard_map/ppermute | solution.py:35
  32.1 26.7 %collective-permute-start.2 = (bf16[24,2,6144]{2,0,1:T(8,128)(2,1)S(1)}, bf16[24,2,6144]{2,0,1:T(8,128)(2,1)}, u32[]{:S(2)}, u32[]{:S(2)}) collective-permute-start(bf16[24,2,6144]{2,0,1:T(8,128)(2,1)S(1)} %get-tuple-element.12), channel_id=1, source_target_pairs={{0,3},{1,0},{2,1},{3,2},{4,7},{5,4},{6,5},{7,6},{8,11},{9,8},{10,9... | collective-permute-start | bytes 1769480 | tf_op jit(solution)/shard_map/ppermute | solution.py:35
  34.0 24.8 %collective-permute-start.1 = (bf16[24,2,6144]{2,0,1:T(8,128)(2,1)S(1)}, bf16[24,2,6144]{2,0,1:T(8,128)(2,1)}, u32[]{:S(2)}, u32[]{:S(2)}) collective-permute-start(bf16[24,2,6144]{2,0,1:T(8,128)(2,1)S(1)} %get-tuple-element.13), channel_id=1, source_target_pairs={{0,2},{1,3},{2,0},{3,1},{4,6},{5,7},{6,4},{7,5},{8,10},{9,11},{10,... | collective-permute-start | bytes 1769480 | tf_op jit(solution)/shard_map/ppermute | solution.py:35
  45.7 48.9 %all-to-all-start.1 = ((bf16[24,128,128]{2,1,0:T(8,128)(2,1)}), bf16[24,128,128]{2,1,0:T(8,128)(2,1)S(1)}, u32[]{:S(2)}, u32[]{:S(2)}) async-start(bf16[24,128,128]{2,1,0:T(8,128)(2,1)} %fusion.23), calls=%async_computation.1 | async-start | bytes 1572864 | tf_op jit(solution)/shard_map/all_to_all | solution.py:46
  60.7 31.0 %collective-permute-start.3 = (bf16[24,2,6144]{2,0,1:T(8,128)(2,1)S(1)}, bf16[24,2,6144]{2,0,1:T(8,128)(2,1)S(1)}, u32[]{:S(2)}, u32[]{:S(2)}) collective-permute-start(bf16[24,2,6144]{2,0,1:T(8,128)(2,1)S(1)} %fusion.10), channel_id=1, source_target_pairs={{192,0},{384,192},{576,384},{193,1},{385,193},{577,385},{194,2},{3... | collective-permute-start | bytes 1769480 | tf_op jit(solution)/shard_map/ppermute | solution.py:15

commit v10 on v7

--- a/solution.py
+++ b/solution.py
@@ -90,15 +90,8 @@
     grad_heads = jnp.einsum(
         "msd,dh->msh", gradients, out_proj, preferred_element_type=jnp.float32
     ).astype(jnp.bfloat16)
-    grad_qkv = jax.vmap(head_backward)(
-        jnp.take(queries, current, axis=0),
-        jnp.take(key_rows, current, axis=0),
-        jnp.take(values, current, axis=0),
-        jnp.take(softmax, current, axis=0),
-        jnp.take(soft_low, current, axis=0),
-        jnp.take(attended, current, axis=0),
-        jnp.take(grad_heads, current, axis=0),
-    )
+    grad_qkv = jax.vmap(head_backward)(queries, key_rows, values, softmax, soft_low, attended, grad_heads)
+    grad_qkv = jnp.take(grad_qkv, current, axis=0)
     n_tensor = lax.axis_size("tensor")
     seq_len = grad_qkv.shape[1]
     start = lax.axis_index("tensor") * (seq_len // n_tensor)

time: 96.6 us -> 92 us (0.952)
  local copies, waits for them, and re-layouts: 8.08 us -> 3.72 us
    gather x7 -> x1, local copies, waits for them, and re-layouts: 3.93 us -> 0.58 us  [body(): grad_qkv = jnp.take(grad_qkv, current, axis=0)]
    sub x1 -> x0, matrix products: 1.18 us -> none  [head_forward(): weights = jnp.exp(scores - row_max)]
    dot_general x0 -> x1, matrix products: none -> 1.12 us  [head_forward(): jnp.dot(queries, key_rows.T, preferred_element_type=jnp.float32)]
    slice x1 -> x0, local copies, waits for them, and re-layouts: 1.01 us -> none  [body(): queries = saved_qkv[:, :, :head_size]]
    unnamed x9 -> x13, local copies, waits for them, and re-layouts: 1.96 us -> 1.96 us
where the time goes in v10:
time: 92 us; the launch traced here: 90.8 us
  waiting for transfers between devices  31.2 us (34%)
  starting transfers between devices  31.1 us (34%)
  matrix products  13.2 us (14%)
  other arithmetic  5.7 us (6%)
  blocking collectives  5 us (5%)
  local copies, waits for them, and re-layouts  3.72 us (4%)
    ppermute x1, waiting for transfers between devices, shifted(): return lax.ppermute(block, axis, route)  29.7 us
    ppermute x3, starting transfers between devices, rotated_sum(): lax.ppermute(parts[shift], axis, [(i, (i + shift) % n) for i in range(n)])  16.7 us
    all_to_all x1, starting transfers between devices, weight_grad_sum(): lax.all_to_all(pair, DP_FAR, 0, 0, tiled=True).astype(jnp.float32)  13.1 us
    all_to_all x1, blocking collectives, weight_grad_sum(): pair = lax.all_to_all(blocks, 'dp_core', 1, 1, tiled=True)  5 us
    dot_general x1, matrix products, body(): jnp.einsum('bjsk,dk->jsbd', grouped, qkv_proj, preferred_element_type=jnp...  4.68 us
    dot_general x1, matrix products, body(): jnp.einsum('msd,dh->msh', gradients, out_proj, preferred_element_type=jnp...  3.76 us
    dot_general x1, matrix products, body(): jnp.einsum('msc,msh->ch', gradients, attended, preferred_element_type=jnp...  2 us
    unnamed x13, local copies, waits for them, and re-layouts  1.96 us
  transfers between devices with their start and end apart: 5, of which 2 were waited for; matrix products, arithmetic and copies ran while one was open for 7% of the time, Pallas kernels for 0%

profile of v10, /device:TPU:6, one launch (start us, length us, event | category | flops | bytes accessed | tf_op | source)
XLA Modules:
  0.0 90.8 jit_solution(9627868121237262379)
XLA Ops:
  0.6 0.8 fusion.32
  1.4 0.7 compare_and_fusion
  2.1 1.1 %fusion.13 = f32[4,96,96]{1,2,0:T(8,128)S(1)} fusion(pred[96,96]{0,1:T(8,128)(4,1)S(1)} %iota_compare_fusion, bf16[4,96,384]{2,1,0:T(8,128)(2,1)} %bitcast.73), kind=kOutput, calls=%fused_computation.23 | convolution fusion | flops 9510912 | bytes 353280 | tf_op jit(solution)/shard_map/vmap()/dot_general | solution.py:51
  3.2 0.2 fusion.35
  3.5 3.8 %fusion.18 = bf16[4,96,128]{2,1,0:T(8,128)(2,1)S(1)} fusion(bf16[1,6144,1,128]{3,1,2,0:T(8,128)(2,1)S(1)} %copy-done, bf16[1,4,1,96,6144]{4,3,2,1,0:T(8,128)(2,1)} %param.5), kind=kOutput, calls=%fused_computation.28 | convolution fusion | flops 604028928 | bytes 6389760 | tf_op jit(solution)/shard_map/msd,dh->msh/dot_general | solution.py:90
  7.5 0.9 multiply_reduce_fusion
  8.7 0.2 fusion.16
  9.0 0.6 gather_fusion
  9.8 4.7 %fusion.2 = bf16[4,24,2,6144]{3,1,0,2:T(8,128)(2,1)S(1)} fusion(bf16[2,4,24,384]{3,2,1,0:T(8,128)(2,1)S(1)} %bitcast.72, bf16[1,6144,1,384]{3,1,2,0:T(8,128)(2,1)} %param.8), kind=kOutput, calls=%fused_computation.5 | convolution fusion | flops 907149312 | bytes 7225344 | tf_op jit(solution)/shard_map/bjsk,dk->jsbd/dot_general | solution.py:100
  14.5 1.1 %slice_bitcast_fusion.2 = (bf16[24,2,6144]{2,0,1:T(8,128)(2,1)}, bf16[24,2,6144]{2,0,1:T(8,128)(2,1)S(1)}, bf16[24,2,6144]{2,0,1:T(8,128)(2,1)S(1)}) fusion(bf16[4,24,2,6144]{3,1,0,2:T(8,128)(2,1)S(1)} %fusion.2), kind=kLoop, calls=%fused_computation.34 | loop fusion | bytes 3538944 | tf_op jit(solution)/shard_map/squeeze | solution.py:35
  15.6 0.5 copy-done.1
  16.1 11.4 %collective-permute-start = (bf16[24,2,6144]{2,0,1:T(8,128)(2,1)}, bf16[24,2,6144]{2,0,1:T(8,128)(2,1)}, u32[]{:S(2)}, u32[]{:S(2)}) collective-permute-start(bf16[24,2,6144]{2,0,1:T(8,128)(2,1)} %get-tuple-element.6), channel_id=1, source_target_pairs={{0,1},{1,2},{2,3},{3,0},{4,5},{5,6},{6,7},{7,4},{8,9},{9,10},{10,1... | collective-permute-start | bytes 1769480 | tf_op jit(solution)/shard_map/ppermute | solution.py:35
  27.5 1.9 %collective-permute-start.2 = (bf16[24,2,6144]{2,0,1:T(8,128)(2,1)S(1)}, bf16[24,2,6144]{2,0,1:T(8,128)(2,1)}, u32[]{:S(2)}, u32[]{:S(2)}) collective-permute-start(bf16[24,2,6144]{2,0,1:T(8,128)(2,1)S(1)} %get-tuple-element.7), channel_id=1, source_target_pairs={{0,3},{1,0},{2,1},{3,2},{4,7},{5,4},{6,5},{7,6},{8,11},{9,8},{10,9... | collective-permute-start | bytes 1769480 | tf_op jit(solution)/shard_map/ppermute | solution.py:35
  29.4 3.4 %collective-permute-start.1 = (bf16[24,2,6144]{2,0,1:T(8,128)(2,1)S(1)}, bf16[24,2,6144]{2,0,1:T(8,128)(2,1)}, u32[]{:S(2)}, u32[]{:S(2)}) collective-permute-start(bf16[24,2,6144]{2,0,1:T(8,128)(2,1)S(1)} %get-tuple-element.8), channel_id=1, source_target_pairs={{0,2},{1,3},{2,0},{3,1},{4,6},{5,7},{6,4},{7,5},{8,10},{9,11},{10,... | collective-permute-start | bytes 1769480 | tf_op jit(solution)/shard_map/ppermute | solution.py:35
  32.9 2.0 %fusion.1 = bf16[128,6144]{0,1:T(8,128)(2,1)S(1)} fusion(bf16[4,96,128]{2,1,0:T(8,128)(2,1)S(1)} %copy-done.3, bf16[1,4,1,96,6144]{4,3,2,1,0:T(8,128)(2,1)S(1)} %bitcast.69), kind=kOutput, calls=%fused_computation.4 | convolution fusion | flops 604766208 | bytes 6389760 | tf_op jit(solution)/shard_map/msc,msh->ch/dot_general | solution.py:86
  35.0 5.0 %all_to_all.10 = bf16[24,2,128,128]{3,2,0,1:T(8,128)(2,1)S(1)} all-to-all(bf16[24,2,128,128]{3,2,0,1:T(8,128)(2,1)S(1)} %copy.20), channel_id=1, replica_groups=mesh['pipe'=4,'dp_y'=2,'dp_z'=12,'dp_core'=2,'tensor'=4] {'dp_core'}, dimensions={1} | all-to-all | bytes 3145728 | tf_op jit(solution)/shard_map/all_to_all | solution.py:44
  40.0 1.2 %fusion.23 = bf16[24,128,128]{2,1,0:T(8,128)(2,1)} fusion(bf16[24,2,128,128]{3,2,0,1:T(8,128)(2,1)S(1)} %all_to_all.10), kind=kLoop, calls=%fused_computation.31 | loop fusion | flops 1572864 | bytes 2359296 | tf_op jit(solution)/shard_map/convert_element_type | solution.py:45
  41.1 13.1 %all-to-all-start.1 = ((bf16[24,128,128]{2,1,0:T(8,128)(2,1)}), bf16[24,128,128]{2,1,0:T(8,128)(2,1)S(1)}, u32[]{:S(2)}, u32[]{:S(2)}) async-start(bf16[24,128,128]{2,1,0:T(8,128)(2,1)} %fusion.23), calls=%async_computation.1 | async-start | bytes 1572864 | tf_op jit(solution)/shard_map/all_to_all | solution.py:46
  54.3 1.9 %fusion.10 = bf16[24,2,6144]{2,0,1:T(8,128)(2,1)S(1)} fusion(bf16[24,2,6144]{2,0,1:T(8,128)(2,1)} %collective-permute-done.2, bf16[24,2,6144]{2,0,1:T(8,128)(2,1)} %collective-permute-done.1, bf16[24,2,6144]{2,0,1:T(8,128)(2,1)} %collective-permute-done, bf16[4,24,2,6144]{3,1,0,2:T(8,128)(2,1)} %copy-done.1), kind=kLoop, calls=%fused_computation.16 | loop fusion | flops 2359296 | bytes 2949120 | tf_op jit(solution)/shard_map/convert_element_type | solution.py:102
  56.2 1.3 %collective-permute-start.3 = (bf16[24,2,6144]{2,0,1:T(8,128)(2,1)S(1)}, bf16[24,2,6144]{2,0,1:T(8,128)(2,1)S(1)}, u32[]{:S(2)}, u32[]{:S(2)}) collective-permute-start(bf16[24,2,6144]{2,0,1:T(8,128)(2,1)S(1)} %fusion.10), channel_id=1, source_target_pairs={{192,0},{384,192},{576,384},{193,1},{385,193},{577,385},{194,2},{3... | collective-permute-start | bytes 1769480 | tf_op jit(solution)/shard_map/ppermute | solution.py:15
  57.5 29.7 %collective-permute-done.3 = bf16[24,2,6144]{2,0,1:T(8,128)(2,1)S(1)} collective-permute-done((bf16[24,2,6144]{2,0,1:T(8,128)(2,1)S(1)}, bf16[24,2,6144]{2,0,1:T(8,128)(2,1)S(1)}, u32[]{:S(2)}, u32[]{:S(2)}) %collective-permute-start.3) | collective-permute-done | bytes 589856 | tf_op jit(solution)/shard_map/ppermute | solution.py:15
  87.2 1.4 %copy.21 = bf16[1,1,24,2,6144]{4,3,2,1,0:T(2,128)(2,1)} copy(bf16[1,1,24,2,6144]{4,2,3,1,0:T(8,128)(2,1)S(1)} %bitcast.71) | data formatting | bytes 1179648
  88.6 1.4 %all-to-all-done.1 = bf16[24,128,128]{2,1,0:T(8,128)(2,1)S(1)} async-done(((bf16[24,128,128]{2,1,0:T(8,128)(2,1)}), bf16[24,128,128]{2,1,0:T(8,128)(2,1)S(1)}, u32[]{:S(2)}, u32[]{:S(2)}) %all-to-all-start.1) | async-done | bytes 786464 | tf_op jit(solution)/shard_map/all_to_all | solution.py:46
  90.0 0.7 convert_reduce_fusion
  (24 shorter events, 0.9 us)
Async XLA Ops:
  0.6 2.8 %copy-start = (bf16[1,6144,1,128]{3,1,2,0:T(8,128)(2,1)S(1)}, bf16[1,6144,1,128]{3,1,2,0:T(8,128)(2,1)}, u32[]{:S(2)}) copy-start(bf16[1,6144,1,128]{3,1,2,0:T(8,128)(2,1)} %param.7) | copy-start | bytes 4718596
  3.5 4.0 %copy-start.2 = (bf16[1,4,1,96,1,384]{5,3,4,2,1,0:T(8,128)(2,1)S(1)}, bf16[1,4,1,96,1,384]{5,3,4,2,1,0:T(8,128)(2,1)}, u32[]{:S(2)}) copy-start(bf16[1,4,1,96,1,384]{5,3,4,2,1,0:T(8,128)(2,1)} %param.6) | copy-start | bytes 884740
  9.8 23.0 %slice-start = ((s8[4718592]{0:T(1024)(128)(4,1)}), s8[4194304]{0:T(1024)(128)(4,1)S(1)}, s32[]{:S(2)}) async-start(s8[4718592]{0:T(1024)(128)(4,1)} %bitcast.68), calls=%async_computation.2 | async-start | bytes 8388608
  9.8 23.0 %slice-start.1 = ((s8[4718592]{0:T(1024)(128)(4,1)}), s8[524288]{0:T(1024)(128)(4,1)S(1)}, s32[]{:S(2)}) async-start(s8[4718592]{0:T(1024)(128)(4,1)} %bitcast.68), calls=%async_computation.3 | async-start | bytes 1048576
  14.5 1.6 %copy-start.1 = (bf16[4,24,2,6144]{3,1,0,2:T(8,128)(2,1)}, bf16[4,24,2,6144]{3,1,0,2:T(8,128)(2,1)S(1)}, u32[]{:S(2)}) copy-start(bf16[4,24,2,6144]{3,1,0,2:T(8,128)(2,1)S(1)} %fusion.2) | copy-start | bytes 7077892
  14.5 18.3 %copy-start.3 = (bf16[4,96,128]{2,1,0:T(8,128)(2,1)S(1)}, bf16[4,96,128]{2,1,0:T(8,128)(2,1)}, u32[]{:S(2)}) copy-start(bf16[4,96,128]{2,1,0:T(8,128)(2,1)} %get-tuple-element.12) | copy-start | bytes 294916
  16.1 38.1 %collective-permute-start = (bf16[24,2,6144]{2,0,1:T(8,128)(2,1)}, bf16[24,2,6144]{2,0,1:T(8,128)(2,1)}, u32[]{:S(2)}, u32[]{:S(2)}) collective-permute-start(bf16[24,2,6144]{2,0,1:T(8,128)(2,1)} %get-tuple-element.6), channel_id=1, source_target_pairs={{0,1},{1,2},{2,3},{3,0},{4,5},{5,6},{6,7},{7,4},{8,9},{9,10},{10,1... | collective-permute-start | bytes 1769480 | tf_op jit(solution)/shard_map/ppermute | solution.py:35
  27.5 26.7 %collective-permute-start.2 = (bf16[24,2,6144]{2,0,1:T(8,128)(2,1)S(1)}, bf16[24,2,6144]{2,0,1:T(8,128)(2,1)}, u32[]{:S(2)}, u32[]{:S(2)}) collective-permute-start(bf16[24,2,6144]{2,0,1:T(8,128)(2,1)S(1)} %get-tuple-element.7), channel_id=1, source_target_pairs={{0,3},{1,0},{2,1},{3,2},{4,7},{5,4},{6,5},{7,6},{8,11},{9,8},{10,9... | collective-permute-start | bytes 1769480 | tf_op jit(solution)/shard_map/ppermute | solution.py:35
  29.4 24.8 %collective-permute-start.1 = (bf16[24,2,6144]{2,0,1:T(8,128)(2,1)S(1)}, bf16[24,2,6144]{2,0,1:T(8,128)(2,1)}, u32[]{:S(2)}, u32[]{:S(2)}) collective-permute-start(bf16[24,2,6144]{2,0,1:T(8,128)(2,1)S(1)} %get-tuple-element.8), channel_id=1, source_target_pairs={{0,2},{1,3},{2,0},{3,1},{4,6},{5,7},{6,4},{7,5},{8,10},{9,11},{10,... | collective-permute-start | bytes 1769480 | tf_op jit(solution)/shard_map/ppermute | solution.py:35
  41.1 48.9 %all-to-all-start.1 = ((bf16[24,128,128]{2,1,0:T(8,128)(2,1)}), bf16[24,128,128]{2,1,0:T(8,128)(2,1)S(1)}, u32[]{:S(2)}, u32[]{:S(2)}) async-start(bf16[24,128,128]{2,1,0:T(8,128)(2,1)} %fusion.23), calls=%async_computation.1 | async-start | bytes 1572864 | tf_op jit(solution)/shard_map/all_to_all | solution.py:46
  56.2 31.0 %collective-permute-start.3 = (bf16[24,2,6144]{2,0,1:T(8,128)(2,1)S(1)}, bf16[24,2,6144]{2,0,1:T(8,128)(2,1)S(1)}, u32[]{:S(2)}, u32[]{:S(2)}) collective-permute-start(bf16[24,2,6144]{2,0,1:T(8,128)(2,1)S(1)} %fusion.10), channel_id=1, source_target_pairs={{192,0},{384,192},{576,384},{193,1},{385,193},{577,385},{194,2},{3... | collective-permute-start | bytes 1769480 | tf_op jit(solution)/shard_map/ppermute | solution.py:15

commit v11 on v10

--- a/solution.py
+++ b/solution.py
@@ -29,7 +29,7 @@
 
 
 def rotated_sum(parts, axis):
-    n = parts.shape[0]
+    n = len(parts)
     total = parts[0].astype(jnp.float32)
     for shift in range(1, n):
         moved = lax.ppermute(parts[shift], axis, [(i, (i + shift) % n) for i in range(n)])
@@ -97,8 +97,11 @@
     start = lax.axis_index("tensor") * (seq_len // n_tensor)
     grad_qkv = lax.dynamic_slice_in_dim(jnp.concatenate([grad_qkv, grad_qkv], axis=1), start, seq_len, axis=1)
     grouped = grad_qkv.reshape(grad_qkv.shape[0], n_tensor, seq_len // n_tensor, grad_qkv.shape[2])
-    partials = jnp.einsum("bjsk,dk->jsbd", grouped, qkv_proj, preferred_element_type=jnp.float32)
-    own_rows = rotated_sum(partials.astype(jnp.bfloat16), "tensor")
+    partials = [
+        jnp.einsum("bsk,dk->sbd", grouped[:, k], qkv_proj, preferred_element_type=jnp.float32).astype(jnp.bfloat16)
+        for k in range(n_tensor)
+    ]
+    own_rows = rotated_sum(partials, "tensor")
     received = shifted(own_rows.astype(jnp.bfloat16), "pipe", -1)
     return (received[None, None], weight_grad[None, :, None, :])
 

time: 92 us -> 106 us (1.15)
  the two profiles are of different devices: /device:TPU:6 before, /device:TPU:48 now
where the time goes in v11:
time: 106 us; the launch traced here: 105 us
  starting transfers between devices  34.7 us (33%)
  waiting for transfers between devices  31.8 us (30%)
  matrix products  27.2 us (26%)
  blocking collectives  5 us (5%)
  other arithmetic  3.79 us (4%)
  local copies, waits for them, and re-layouts  2.13 us (2%)
    all_to_all x1, starting transfers between devices, weight_grad_sum(): lax.all_to_all(pair, DP_FAR, 0, 0, tiled=True).astype(jnp.float32)  20.7 us
    ppermute x3, waiting for transfers between devices, rotated_sum(): lax.ppermute(parts[shift], axis, [(i, (i + shift) % n) for i in range(n)])  20.1 us
    dot_general x4, matrix products, body(): jnp.einsum('bsk,dk->sbd', grouped[:, k], qkv_proj, preferred_element_type...  16.9 us
    ppermute x1, waiting for transfers between devices, shifted(): return lax.ppermute(block, axis, route)  11.6 us
    ppermute x3, starting transfers between devices, rotated_sum(): lax.ppermute(parts[shift], axis, [(i, (i + shift) % n) for i in range(n)])  10.8 us
    all_to_all x1, blocking collectives, weight_grad_sum(): pair = lax.all_to_all(blocks, 'dp_core', 1, 1, tiled=True)  5 us
    dot_general x1, matrix products, body(): jnp.einsum('msc,msh->ch', gradients, attended, preferred_element_type=jnp...  4.28 us
    dot_general x1, matrix products, body(): jnp.einsum('msd,dh->msh', gradients, out_proj, preferred_element_type=jnp...  3.76 us
  transfers between devices with their start and end apart: 5, of which 2 were waited for; matrix products, arithmetic and copies ran while one was open for 18% of the time, Pallas kernels for 0%

profile of v11, /device:TPU:48, one launch (start us, length us, event | category | flops | bytes accessed | tf_op | source)
XLA Modules:
  0.0 105.4 jit_solution(4669719086979176521)
XLA Ops:
  0.6 0.8 fusion.38
  1.4 0.7 compare_and_fusion
  2.1 1.1 %fusion.17 = f32[4,96,96]{1,2,0:T(8,128)S(1)} fusion(pred[96,96]{0,1:T(8,128)(4,1)S(1)} %iota_compare_fusion, bf16[4,96,384]{2,1,0:T(8,128)(2,1)} %bitcast.94), kind=kOutput, calls=%fused_computation.30 | convolution fusion | flops 9510912 | bytes 353280 | tf_op jit(solution)/shard_map/vmap()/dot_general | solution.py:51
  3.2 0.2 fusion.41
  3.5 3.8 %fusion.22 = bf16[4,96,128]{2,1,0:T(8,128)(2,1)S(1)} fusion(bf16[1,6144,1,128]{3,1,2,0:T(8,128)(2,1)S(1)} %copy-done, bf16[1,4,1,96,6144]{4,3,2,1,0:T(8,128)(2,1)} %param.5), kind=kOutput, calls=%fused_computation.35 | convolution fusion | flops 604028928 | bytes 6389760 | tf_op jit(solution)/shard_map/msd,dh->msh/dot_general | solution.py:90
  7.5 0.4 multiply_reduce_fusion
  8.2 0.2 fusion.20
  8.5 0.6 gather_fusion
  9.3 5.1 %fusion.6 = bf16[24,2,6144]{2,0,1:T(8,128)(2,1)} fusion(bf16[1,6144,1,384]{3,1,2,0:T(8,128)(2,1)} %param.8, bf16[2,4,24,384]{3,2,1,0:T(8,128)(2,1)S(1)} %bitcast.89), kind=kOutput, calls=%fused_computation.12 | convolution fusion | flops 226787328 | bytes 5345280 | tf_op jit(solution)/shard_map/bsk,dk->sbd/dot_general | solution.py:101
  14.4 4.7 %collective-permute-start.2 = (bf16[24,2,6144]{2,0,1:T(8,128)(2,1)}, bf16[24,2,6144]{2,0,1:T(8,128)(2,1)}, u32[]{:S(2)}, u32[]{:S(2)}) collective-permute-start(bf16[24,2,6144]{2,0,1:T(8,128)(2,1)} %fusion.6), channel_id=1, source_target_pairs={{0,3},{1,0},{2,1},{3,2},{4,7},{5,4},{6,5},{7,6},{8,11},{9,8},{10,9... | collective-permute-start | bytes 1769480 | tf_op jit(solution)/shard_map/ppermute | solution.py:35
  19.1 4.3 %fusion.1 = bf16[128,6144]{0,1:T(8,128)(2,1)S(1)} fusion(bf16[4,96,128]{2,1,0:T(8,128)(2,1)S(1)} %get-tuple-element.11, bf16[1,4,1,96,6144]{4,3,2,1,0:T(8,128)(2,1)} %param.5), kind=kOutput, calls=%fused_computation.3 | convolution fusion | flops 604766208 | bytes 6389760 | tf_op jit(solution)/shard_map/msc,msh->ch/dot_general | solution.py:86
  23.5 5.0 %all_to_all.10 = bf16[24,2,128,128]{3,2,0,1:T(8,128)(2,1)S(1)} all-to-all(bf16[24,2,128,128]{3,2,0,1:T(8,128)(2,1)S(1)} %copy.26), channel_id=1, replica_groups=mesh['pipe'=4,'dp_y'=2,'dp_z'=12,'dp_core'=2,'tensor'=4] {'dp_core'}, dimensions={1} | all-to-all | bytes 3145728 | tf_op jit(solution)/shard_map/all_to_all | solution.py:44
  28.5 1.1 %fusion.27 = bf16[24,128,128]{2,1,0:T(8,128)(2,1)} fusion(bf16[24,2,128,128]{3,2,0,1:T(8,128)(2,1)S(1)} %all_to_all.10), kind=kLoop, calls=%fused_computation.38 | loop fusion | flops 1572864 | bytes 2359296 | tf_op jit(solution)/shard_map/convert_element_type | solution.py:45
  29.6 20.7 %all-to-all-start.1 = ((bf16[24,128,128]{2,1,0:T(8,128)(2,1)}), bf16[24,128,128]{2,1,0:T(8,128)(2,1)S(1)}, u32[]{:S(2)}, u32[]{:S(2)}) async-start(bf16[24,128,128]{2,1,0:T(8,128)(2,1)} %fusion.27), calls=%async_computation.1 | async-start | bytes 1572864 | tf_op jit(solution)/shard_map/all_to_all | solution.py:46
  50.3 4.4 %fusion.4 = bf16[24,2,6144]{2,0,1:T(8,128)(2,1)S(1)} fusion(bf16[1,6144,1,384]{3,1,2,0:T(8,128)(2,1)} %param.8, bf16[2,4,24,384]{3,2,1,0:T(8,128)(2,1)S(1)} %bitcast.90), kind=kOutput, calls=%fused_computation.10 | convolution fusion | flops 226787328 | bytes 5345280 | tf_op jit(solution)/shard_map/bsk,dk->sbd/dot_general | solution.py:101
  54.7 1.9 %collective-permute-start = (bf16[24,2,6144]{2,0,1:T(8,128)(2,1)S(1)}, bf16[24,2,6144]{2,0,1:T(8,128)(2,1)S(1)}, u32[]{:S(2)}, u32[]{:S(2)}) collective-permute-start(bf16[24,2,6144]{2,0,1:T(8,128)(2,1)S(1)} %fusion.4), channel_id=1, source_target_pairs={{0,1},{1,2},{2,3},{3,0},{4,5},{5,6},{6,7},{7,4},{8,9},{9,10},{10,1... | collective-permute-start | bytes 1769480 | tf_op jit(solution)/shard_map/ppermute | solution.py:35
  56.7 4.3 %fusion.5 = bf16[24,2,6144]{2,0,1:T(8,128)(2,1)S(1)} fusion(bf16[1,6144,1,384]{3,1,2,0:T(8,128)(2,1)} %param.8, bf16[2,4,24,384]{3,2,1,0:T(8,128)(2,1)S(1)} %bitcast.91), kind=kOutput, calls=%fused_computation.11 | convolution fusion | flops 226787328 | bytes 5345280 | tf_op jit(solution)/shard_map/bsk,dk->sbd/dot_general | solution.py:101
  61.0 4.2 %collective-permute-start.1 = (bf16[24,2,6144]{2,0,1:T(8,128)(2,1)S(1)}, bf16[24,2,6144]{2,0,1:T(8,128)(2,1)S(1)}, u32[]{:S(2)}, u32[]{:S(2)}) collective-permute-start(bf16[24,2,6144]{2,0,1:T(8,128)(2,1)S(1)} %fusion.5), channel_id=1, source_target_pairs={{0,2},{1,3},{2,0},{3,1},{4,6},{5,7},{6,4},{7,5},{8,10},{9,11},{10,... | collective-permute-start | bytes 1769480 | tf_op jit(solution)/shard_map/ppermute | solution.py:35
  65.2 20.1 %collective-permute-done = bf16[24,2,6144]{2,0,1:T(8,128)(2,1)S(1)} collective-permute-done((bf16[24,2,6144]{2,0,1:T(8,128)(2,1)S(1)}, bf16[24,2,6144]{2,0,1:T(8,128)(2,1)S(1)}, u32[]{:S(2)}, u32[]{:S(2)}) %collective-permute-start) | collective-permute-done | bytes 589856 | tf_op jit(solution)/shard_map/ppermute | solution.py:35
  85.3 3.1 %add_convert_fusion.1 = bf16[24,2,6144]{2,0,1:T(8,128)(2,1)S(1)} fusion(bf16[24,2,6144]{2,0,1:T(8,128)(2,1)} %collective-permute-done.2, bf16[24,2,6144]{2,0,1:T(8,128)(2,1)S(1)} %collective-permute-done.1, bf16[24,2,6144]{2,0,1:T(8,128)(2,1)S(1)} %collective-permute-done, bf16[1,6144,1,384]{3,1,2,0:T(8,128)(2,1)S(1)} %bitcast.87, ...), kind=kOutput, calls=%fused_computation.23 | convolution fusion | flops 229146624 | bytes 7114752 | tf_op jit(solution)/shard_map/bsk,dk->sbd/dot_general | solution.py:101
  88.4 3.2 %collective-permute-start.3 = (bf16[24,2,6144]{2,0,1:T(8,128)(2,1)S(1)}, bf16[24,2,6144]{2,0,1:T(8,128)(2,1)S(1)}, u32[]{:S(2)}, u32[]{:S(2)}) collective-permute-start(bf16[24,2,6144]{2,0,1:T(8,128)(2,1)S(1)} %add_convert_fusion.1), channel_id=1, source_target_pairs={{192,0},{384,192},{576,384},{193,1},{385,193},{577,385},{194,2},{3... | collective-permute-start | bytes 1769480 | tf_op jit(solution)/shard_map/ppermute | solution.py:15
  91.6 11.6 %collective-permute-done.3 = bf16[24,2,6144]{2,0,1:T(8,128)(2,1)S(1)} collective-permute-done((bf16[24,2,6144]{2,0,1:T(8,128)(2,1)S(1)}, bf16[24,2,6144]{2,0,1:T(8,128)(2,1)S(1)}, u32[]{:S(2)}, u32[]{:S(2)}) %collective-permute-start.3) | collective-permute-done | bytes 589856 | tf_op jit(solution)/shard_map/ppermute | solution.py:15
  103.3 1.4 %copy.27 = bf16[1,1,24,2,6144]{4,3,2,1,0:T(2,128)(2,1)} copy(bf16[1,1,24,2,6144]{4,2,3,1,0:T(8,128)(2,1)S(1)} %bitcast.93) | data formatting | bytes 1179648
  104.7 0.7 convert_reduce_fusion
  (21 shorter events, 0.9 us)
Async XLA Ops:
  0.6 2.8 %copy-start = (bf16[1,6144,1,128]{3,1,2,0:T(8,128)(2,1)S(1)}, bf16[1,6144,1,128]{3,1,2,0:T(8,128)(2,1)}, u32[]{:S(2)}) copy-start(bf16[1,6144,1,128]{3,1,2,0:T(8,128)(2,1)} %param.7) | copy-start | bytes 4718596
  3.5 4.0 %copy-start.1 = (bf16[1,4,1,96,1,384]{5,3,4,2,1,0:T(8,128)(2,1)S(1)}, bf16[1,4,1,96,1,384]{5,3,4,2,1,0:T(8,128)(2,1)}, u32[]{:S(2)}) copy-start(bf16[1,4,1,96,1,384]{5,3,4,2,1,0:T(8,128)(2,1)} %param.6) | copy-start | bytes 884740
  14.4 50.8 %collective-permute-start.2 = (bf16[24,2,6144]{2,0,1:T(8,128)(2,1)}, bf16[24,2,6144]{2,0,1:T(8,128)(2,1)}, u32[]{:S(2)}, u32[]{:S(2)}) collective-permute-start(bf16[24,2,6144]{2,0,1:T(8,128)(2,1)} %fusion.6), channel_id=1, source_target_pairs={{0,3},{1,0},{2,1},{3,2},{4,7},{5,4},{6,5},{7,6},{8,11},{9,8},{10,9... | collective-permute-start | bytes 1769480 | tf_op jit(solution)/shard_map/ppermute | solution.py:35
  29.6 55.7 %slice-start = ((s8[4718592]{0:T(1024)(128)(4,1)}), s8[524288]{0:T(1024)(128)(4,1)S(1)}, s32[]{:S(2)}) async-start(s8[4718592]{0:T(1024)(128)(4,1)} %bitcast.86), calls=%async_computation.2 | async-start | bytes 1048576
  29.6 75.1 %all-to-all-start.1 = ((bf16[24,128,128]{2,1,0:T(8,128)(2,1)}), bf16[24,128,128]{2,1,0:T(8,128)(2,1)S(1)}, u32[]{:S(2)}, u32[]{:S(2)}) async-start(bf16[24,128,128]{2,1,0:T(8,128)(2,1)} %fusion.27), calls=%async_computation.1 | async-start | bytes 1572864 | tf_op jit(solution)/shard_map/all_to_all | solution.py:46
  50.3 35.0 %slice-start.1 = ((s8[4718592]{0:T(1024)(128)(4,1)}), s8[4194304]{0:T(1024)(128)(4,1)S(1)}, s32[]{:S(2)}) async-start(s8[4718592]{0:T(1024)(128)(4,1)} %bitcast.86), calls=%async_computation.3 | async-start | bytes 8388608
  54.7 30.6 %collective-permute-start = (bf16[24,2,6144]{2,0,1:T(8,128)(2,1)S(1)}, bf16[24,2,6144]{2,0,1:T(8,128)(2,1)S(1)}, u32[]{:S(2)}, u32[]{:S(2)}) collective-permute-start(bf16[24,2,6144]{2,0,1:T(8,128)(2,1)S(1)} %fusion.4), channel_id=1, source_target_pairs={{0,1},{1,2},{2,3},{3,0},{4,5},{5,6},{6,7},{7,4},{8,9},{9,10},{10,1... | collective-permute-start | bytes 1769480 | tf_op jit(solution)/shard_map/ppermute | solution.py:35
  61.0 24.3 %collective-permute-start.1 = (bf16[24,2,6144]{2,0,1:T(8,128)(2,1)S(1)}, bf16[24,2,6144]{2,0,1:T(8,128)(2,1)S(1)}, u32[]{:S(2)}, u32[]{:S(2)}) collective-permute-start(bf16[24,2,6144]{2,0,1:T(8,128)(2,1)S(1)} %fusion.5), channel_id=1, source_target_pairs={{0,2},{1,3},{2,0},{3,1},{4,6},{5,7},{6,4},{7,5},{8,10},{9,11},{10,... | collective-permute-start | bytes 1769480 | tf_op jit(solution)/shard_map/ppermute | solution.py:35
  88.4 14.9 %collective-permute-start.3 = (bf16[24,2,6144]{2,0,1:T(8,128)(2,1)S(1)}, bf16[24,2,6144]{2,0,1:T(8,128)(2,1)S(1)}, u32[]{:S(2)}, u32[]{:S(2)}) collective-permute-start(bf16[24,2,6144]{2,0,1:T(8,128)(2,1)S(1)} %add_convert_fusion.1), channel_id=1, source_target_pairs={{192,0},{384,192},{576,384},{193,1},{385,193},{577,385},{194,2},{3... | collective-permute-start | bytes 1769480 | tf_op jit(solution)/shard_map/ppermute | solution.py:15

commit v12 on v10

--- a/solution.py
+++ b/solution.py
@@ -100,7 +100,8 @@
     partials = jnp.einsum("bjsk,dk->jsbd", grouped, qkv_proj, preferred_element_type=jnp.float32)
     own_rows = rotated_sum(partials.astype(jnp.bfloat16), "tensor")
     received = shifted(own_rows.astype(jnp.bfloat16), "pipe", -1)
-    return (received[None, None], weight_grad[None, :, None, :])
+    weight_grad = with_layout_constraint(weight_grad[None, :, None, :], Layout((0, 1, 2, 3)))
+    return (received[None, None], weight_grad)
 
 
 def solution(mesh):

time: 92 us -> 92 us (level)
  no operation moved by 1% of the time
where the time goes in v12:
time: 92 us; the launch traced here: 90.8 us
  waiting for transfers between devices  31.2 us (34%)
  starting transfers between devices  31.1 us (34%)
  matrix products  13.2 us (14%)
  other arithmetic  5.7 us (6%)
  blocking collectives  5 us (5%)
  local copies, waits for them, and re-layouts  3.72 us (4%)
    ppermute x1, waiting for transfers between devices, shifted(): return lax.ppermute(block, axis, route)  29.7 us
    ppermute x3, starting transfers between devices, rotated_sum(): lax.ppermute(parts[shift], axis, [(i, (i + shift) % n) for i in range(n)])  16.7 us
    all_to_all x1, starting transfers between devices, weight_grad_sum(): lax.all_to_all(pair, DP_FAR, 0, 0, tiled=True).astype(jnp.float32)  13.1 us
    all_to_all x1, blocking collectives, weight_grad_sum(): pair = lax.all_to_all(blocks, 'dp_core', 1, 1, tiled=True)  5 us
    dot_general x1, matrix products, body(): jnp.einsum('bjsk,dk->jsbd', grouped, qkv_proj, preferred_element_type=jnp...  4.68 us
    dot_general x1, matrix products, body(): jnp.einsum('msd,dh->msh', gradients, out_proj, preferred_element_type=jnp...  3.76 us
    dot_general x1, matrix products, body(): jnp.einsum('msc,msh->ch', gradients, attended, preferred_element_type=jnp...  2 us
    unnamed x13, local copies, waits for them, and re-layouts  1.96 us
  transfers between devices with their start and end apart: 5, of which 2 were waited for; matrix products, arithmetic and copies ran while one was open for 7% of the time, Pallas kernels for 0%

profile of v12, /device:TPU:6, one launch (start us, length us, event | category | flops | bytes accessed | tf_op | source)
XLA Modules:
  0.0 90.8 jit_solution(9627868121237262379)
XLA Ops:
  0.6 0.8 fusion.32
  1.4 0.7 compare_and_fusion
  2.1 1.1 %fusion.13 = f32[4,96,96]{1,2,0:T(8,128)S(1)} fusion(pred[96,96]{0,1:T(8,128)(4,1)S(1)} %iota_compare_fusion, bf16[4,96,384]{2,1,0:T(8,128)(2,1)} %bitcast.73), kind=kOutput, calls=%fused_computation.23 | convolution fusion | flops 9510912 | bytes 353280 | tf_op jit(solution)/shard_map/vmap()/dot_general | solution.py:51
  3.2 0.2 fusion.35
  3.5 3.8 %fusion.18 = bf16[4,96,128]{2,1,0:T(8,128)(2,1)S(1)} fusion(bf16[1,6144,1,128]{3,1,2,0:T(8,128)(2,1)S(1)} %copy-done, bf16[1,4,1,96,6144]{4,3,2,1,0:T(8,128)(2,1)} %param.5), kind=kOutput, calls=%fused_computation.28 | convolution fusion | flops 604028928 | bytes 6389760 | tf_op jit(solution)/shard_map/msd,dh->msh/dot_general | solution.py:90
  7.5 0.9 multiply_reduce_fusion
  8.7 0.2 fusion.16
  9.0 0.6 gather_fusion
  9.8 4.7 %fusion.2 = bf16[4,24,2,6144]{3,1,0,2:T(8,128)(2,1)S(1)} fusion(bf16[2,4,24,384]{3,2,1,0:T(8,128)(2,1)S(1)} %bitcast.72, bf16[1,6144,1,384]{3,1,2,0:T(8,128)(2,1)} %param.8), kind=kOutput, calls=%fused_computation.5 | convolution fusion | flops 907149312 | bytes 7225344 | tf_op jit(solution)/shard_map/bjsk,dk->jsbd/dot_general | solution.py:100
  14.5 1.1 %slice_bitcast_fusion.2 = (bf16[24,2,6144]{2,0,1:T(8,128)(2,1)}, bf16[24,2,6144]{2,0,1:T(8,128)(2,1)S(1)}, bf16[24,2,6144]{2,0,1:T(8,128)(2,1)S(1)}) fusion(bf16[4,24,2,6144]{3,1,0,2:T(8,128)(2,1)S(1)} %fusion.2), kind=kLoop, calls=%fused_computation.34 | loop fusion | bytes 3538944 | tf_op jit(solution)/shard_map/squeeze | solution.py:35
  15.6 0.5 copy-done.1
  16.1 11.4 %collective-permute-start = (bf16[24,2,6144]{2,0,1:T(8,128)(2,1)}, bf16[24,2,6144]{2,0,1:T(8,128)(2,1)}, u32[]{:S(2)}, u32[]{:S(2)}) collective-permute-start(bf16[24,2,6144]{2,0,1:T(8,128)(2,1)} %get-tuple-element.6), channel_id=1, source_target_pairs={{0,1},{1,2},{2,3},{3,0},{4,5},{5,6},{6,7},{7,4},{8,9},{9,10},{10,1... | collective-permute-start | bytes 1769480 | tf_op jit(solution)/shard_map/ppermute | solution.py:35
  27.5 1.9 %collective-permute-start.2 = (bf16[24,2,6144]{2,0,1:T(8,128)(2,1)S(1)}, bf16[24,2,6144]{2,0,1:T(8,128)(2,1)}, u32[]{:S(2)}, u32[]{:S(2)}) collective-permute-start(bf16[24,2,6144]{2,0,1:T(8,128)(2,1)S(1)} %get-tuple-element.7), channel_id=1, source_target_pairs={{0,3},{1,0},{2,1},{3,2},{4,7},{5,4},{6,5},{7,6},{8,11},{9,8},{10,9... | collective-permute-start | bytes 1769480 | tf_op jit(solution)/shard_map/ppermute | solution.py:35
  29.4 3.4 %collective-permute-start.1 = (bf16[24,2,6144]{2,0,1:T(8,128)(2,1)S(1)}, bf16[24,2,6144]{2,0,1:T(8,128)(2,1)}, u32[]{:S(2)}, u32[]{:S(2)}) collective-permute-start(bf16[24,2,6144]{2,0,1:T(8,128)(2,1)S(1)} %get-tuple-element.8), channel_id=1, source_target_pairs={{0,2},{1,3},{2,0},{3,1},{4,6},{5,7},{6,4},{7,5},{8,10},{9,11},{10,... | collective-permute-start | bytes 1769480 | tf_op jit(solution)/shard_map/ppermute | solution.py:35
  32.9 2.0 %fusion.1 = bf16[128,6144]{0,1:T(8,128)(2,1)S(1)} fusion(bf16[4,96,128]{2,1,0:T(8,128)(2,1)S(1)} %copy-done.3, bf16[1,4,1,96,6144]{4,3,2,1,0:T(8,128)(2,1)S(1)} %bitcast.69), kind=kOutput, calls=%fused_computation.4 | convolution fusion | flops 604766208 | bytes 6389760 | tf_op jit(solution)/shard_map/msc,msh->ch/dot_general | solution.py:86
  35.0 5.0 %all_to_all.10 = bf16[24,2,128,128]{3,2,0,1:T(8,128)(2,1)S(1)} all-to-all(bf16[24,2,128,128]{3,2,0,1:T(8,128)(2,1)S(1)} %copy.20), channel_id=1, replica_groups=mesh['pipe'=4,'dp_y'=2,'dp_z'=12,'dp_core'=2,'tensor'=4] {'dp_core'}, dimensions={1} | all-to-all | bytes 3145728 | tf_op jit(solution)/shard_map/all_to_all | solution.py:44
  40.0 1.2 %fusion.23 = bf16[24,128,128]{2,1,0:T(8,128)(2,1)} fusion(bf16[24,2,128,128]{3,2,0,1:T(8,128)(2,1)S(1)} %all_to_all.10), kind=kLoop, calls=%fused_computation.31 | loop fusion | flops 1572864 | bytes 2359296 | tf_op jit(solution)/shard_map/convert_element_type | solution.py:45
  41.1 13.1 %all-to-all-start.1 = ((bf16[24,128,128]{2,1,0:T(8,128)(2,1)}), bf16[24,128,128]{2,1,0:T(8,128)(2,1)S(1)}, u32[]{:S(2)}, u32[]{:S(2)}) async-start(bf16[24,128,128]{2,1,0:T(8,128)(2,1)} %fusion.23), calls=%async_computation.1 | async-start | bytes 1572864 | tf_op jit(solution)/shard_map/all_to_all | solution.py:46
  54.3 1.9 %fusion.10 = bf16[24,2,6144]{2,0,1:T(8,128)(2,1)S(1)} fusion(bf16[24,2,6144]{2,0,1:T(8,128)(2,1)} %collective-permute-done.2, bf16[24,2,6144]{2,0,1:T(8,128)(2,1)} %collective-permute-done.1, bf16[24,2,6144]{2,0,1:T(8,128)(2,1)} %collective-permute-done, bf16[4,24,2,6144]{3,1,0,2:T(8,128)(2,1)} %copy-done.1), kind=kLoop, calls=%fused_computation.16 | loop fusion | flops 2359296 | bytes 2949120 | tf_op jit(solution)/shard_map/convert_element_type | solution.py:102
  56.2 1.3 %collective-permute-start.3 = (bf16[24,2,6144]{2,0,1:T(8,128)(2,1)S(1)}, bf16[24,2,6144]{2,0,1:T(8,128)(2,1)S(1)}, u32[]{:S(2)}, u32[]{:S(2)}) collective-permute-start(bf16[24,2,6144]{2,0,1:T(8,128)(2,1)S(1)} %fusion.10), channel_id=1, source_target_pairs={{192,0},{384,192},{576,384},{193,1},{385,193},{577,385},{194,2},{3... | collective-permute-start | bytes 1769480 | tf_op jit(solution)/shard_map/ppermute | solution.py:15
  57.5 29.7 %collective-permute-done.3 = bf16[24,2,6144]{2,0,1:T(8,128)(2,1)S(1)} collective-permute-done((bf16[24,2,6144]{2,0,1:T(8,128)(2,1)S(1)}, bf16[24,2,6144]{2,0,1:T(8,128)(2,1)S(1)}, u32[]{:S(2)}, u32[]{:S(2)}) %collective-permute-start.3) | collective-permute-done | bytes 589856 | tf_op jit(solution)/shard_map/ppermute | solution.py:15
  87.2 1.4 %copy.21 = bf16[1,1,24,2,6144]{4,3,2,1,0:T(2,128)(2,1)} copy(bf16[1,1,24,2,6144]{4,2,3,1,0:T(8,128)(2,1)S(1)} %bitcast.71) | data formatting | bytes 1179648
  88.6 1.4 %all-to-all-done.1 = bf16[24,128,128]{2,1,0:T(8,128)(2,1)S(1)} async-done(((bf16[24,128,128]{2,1,0:T(8,128)(2,1)}), bf16[24,128,128]{2,1,0:T(8,128)(2,1)S(1)}, u32[]{:S(2)}, u32[]{:S(2)}) %all-to-all-start.1) | async-done | bytes 786464 | tf_op jit(solution)/shard_map/all_to_all | solution.py:46
  90.0 0.7 convert_reduce_fusion
  (24 shorter events, 0.9 us)
Async XLA Ops:
  0.6 2.8 %copy-start = (bf16[1,6144,1,128]{3,1,2,0:T(8,128)(2,1)S(1)}, bf16[1,6144,1,128]{3,1,2,0:T(8,128)(2,1)}, u32[]{:S(2)}) copy-start(bf16[1,6144,1,128]{3,1,2,0:T(8,128)(2,1)} %param.7) | copy-start | bytes 4718596
  3.5 4.0 %copy-start.2 = (bf16[1,4,1,96,1,384]{5,3,4,2,1,0:T(8,128)(2,1)S(1)}, bf16[1,4,1,96,1,384]{5,3,4,2,1,0:T(8,128)(2,1)}, u32[]{:S(2)}) copy-start(bf16[1,4,1,96,1,384]{5,3,4,2,1,0:T(8,128)(2,1)} %param.6) | copy-start | bytes 884740
  9.8 23.0 %slice-start = ((s8[4718592]{0:T(1024)(128)(4,1)}), s8[4194304]{0:T(1024)(128)(4,1)S(1)}, s32[]{:S(2)}) async-start(s8[4718592]{0:T(1024)(128)(4,1)} %bitcast.68), calls=%async_computation.2 | async-start | bytes 8388608
  9.8 23.0 %slice-start.1 = ((s8[4718592]{0:T(1024)(128)(4,1)}), s8[524288]{0:T(1024)(128)(4,1)S(1)}, s32[]{:S(2)}) async-start(s8[4718592]{0:T(1024)(128)(4,1)} %bitcast.68), calls=%async_computation.3 | async-start | bytes 1048576
  14.5 1.6 %copy-start.1 = (bf16[4,24,2,6144]{3,1,0,2:T(8,128)(2,1)}, bf16[4,24,2,6144]{3,1,0,2:T(8,128)(2,1)S(1)}, u32[]{:S(2)}) copy-start(bf16[4,24,2,6144]{3,1,0,2:T(8,128)(2,1)S(1)} %fusion.2) | copy-start | bytes 7077892
  14.5 18.3 %copy-start.3 = (bf16[4,96,128]{2,1,0:T(8,128)(2,1)S(1)}, bf16[4,96,128]{2,1,0:T(8,128)(2,1)}, u32[]{:S(2)}) copy-start(bf16[4,96,128]{2,1,0:T(8,128)(2,1)} %get-tuple-element.12) | copy-start | bytes 294916
  16.1 38.1 %collective-permute-start = (bf16[24,2,6144]{2,0,1:T(8,128)(2,1)}, bf16[24,2,6144]{2,0,1:T(8,128)(2,1)}, u32[]{:S(2)}, u32[]{:S(2)}) collective-permute-start(bf16[24,2,6144]{2,0,1:T(8,128)(2,1)} %get-tuple-element.6), channel_id=1, source_target_pairs={{0,1},{1,2},{2,3},{3,0},{4,5},{5,6},{6,7},{7,4},{8,9},{9,10},{10,1... | collective-permute-start | bytes 1769480 | tf_op jit(solution)/shard_map/ppermute | solution.py:35
  27.5 26.7 %collective-permute-start.2 = (bf16[24,2,6144]{2,0,1:T(8,128)(2,1)S(1)}, bf16[24,2,6144]{2,0,1:T(8,128)(2,1)}, u32[]{:S(2)}, u32[]{:S(2)}) collective-permute-start(bf16[24,2,6144]{2,0,1:T(8,128)(2,1)S(1)} %get-tuple-element.7), channel_id=1, source_target_pairs={{0,3},{1,0},{2,1},{3,2},{4,7},{5,4},{6,5},{7,6},{8,11},{9,8},{10,9... | collective-permute-start | bytes 1769480 | tf_op jit(solution)/shard_map/ppermute | solution.py:35
  29.4 24.8 %collective-permute-start.1 = (bf16[24,2,6144]{2,0,1:T(8,128)(2,1)S(1)}, bf16[24,2,6144]{2,0,1:T(8,128)(2,1)}, u32[]{:S(2)}, u32[]{:S(2)}) collective-permute-start(bf16[24,2,6144]{2,0,1:T(8,128)(2,1)S(1)} %get-tuple-element.8), channel_id=1, source_target_pairs={{0,2},{1,3},{2,0},{3,1},{4,6},{5,7},{6,4},{7,5},{8,10},{9,11},{10,... | collective-permute-start | bytes 1769480 | tf_op jit(solution)/shard_map/ppermute | solution.py:35
  41.1 48.9 %all-to-all-start.1 = ((bf16[24,128,128]{2,1,0:T(8,128)(2,1)}), bf16[24,128,128]{2,1,0:T(8,128)(2,1)S(1)}, u32[]{:S(2)}, u32[]{:S(2)}) async-start(bf16[24,128,128]{2,1,0:T(8,128)(2,1)} %fusion.23), calls=%async_computation.1 | async-start | bytes 1572864 | tf_op jit(solution)/shard_map/all_to_all | solution.py:46
  56.2 31.0 %collective-permute-start.3 = (bf16[24,2,6144]{2,0,1:T(8,128)(2,1)S(1)}, bf16[24,2,6144]{2,0,1:T(8,128)(2,1)S(1)}, u32[]{:S(2)}, u32[]{:S(2)}) collective-permute-start(bf16[24,2,6144]{2,0,1:T(8,128)(2,1)S(1)} %fusion.10), channel_id=1, source_target_pairs={{192,0},{384,192},{576,384},{193,1},{385,193},{577,385},{194,2},{3... | collective-permute-start | bytes 1769480 | tf_op jit(solution)/shard_map/ppermute | solution.py:15

commit v13 on v10

--- a/solution.py
+++ b/solution.py
@@ -91,7 +91,7 @@
         "msd,dh->msh", gradients, out_proj, preferred_element_type=jnp.float32
     ).astype(jnp.bfloat16)
     grad_qkv = jax.vmap(head_backward)(queries, key_rows, values, softmax, soft_low, attended, grad_heads)
-    grad_qkv = jnp.take(grad_qkv, current, axis=0)
+    grad_qkv = jnp.take(grad_qkv, current, axis=0, mode="clip")
     n_tensor = lax.axis_size("tensor")
     seq_len = grad_qkv.shape[1]
     start = lax.axis_index("tensor") * (seq_len // n_tensor)

time: 92 us -> 90.6 us (0.985)
  other arithmetic: 5.7 us -> 4.17 us
    unnamed x13 -> x15, local copies, waits for them, and re-layouts: 1.96 us -> 1.97 us
where the time goes in v13:
time: 90.6 us; the launch traced here: 89.4 us
  waiting for transfers between devices  31.2 us (34%)
  starting transfers between devices  31.1 us (34%)
  matrix products  13.3 us (15%)
  blocking collectives  5 us (6%)
  other arithmetic  4.17 us (5%)
  local copies, waits for them, and re-layouts  3.74 us (4%)
  between operations  0.94 us (1%)
    ppermute x1, waiting for transfers between devices, shifted(): return lax.ppermute(block, axis, route)  29.7 us
    ppermute x3, starting transfers between devices, rotated_sum(): lax.ppermute(parts[shift], axis, [(i, (i + shift) % n) for i in range(n)])  16.7 us
    all_to_all x1, starting transfers between devices, weight_grad_sum(): lax.all_to_all(pair, DP_FAR, 0, 0, tiled=True).astype(jnp.float32)  13.1 us
    all_to_all x1, blocking collectives, weight_grad_sum(): pair = lax.all_to_all(blocks, 'dp_core', 1, 1, tiled=True)  5 us
    dot_general x1, matrix products, body(): jnp.einsum('bjsk,dk->jsbd', grouped, qkv_proj, preferred_element_type=jnp...  4.68 us
    dot_general x1, matrix products, body(): jnp.einsum('msd,dh->msh', gradients, out_proj, preferred_element_type=jnp...  3.76 us
    dot_general x1, matrix products, body(): jnp.einsum('msc,msh->ch', gradients, attended, preferred_element_type=jnp...  2 us
    unnamed x15, local copies, waits for them, and re-layouts  1.97 us
  transfers between devices with their start and end apart: 5, of which 2 were waited for; matrix products, arithmetic and copies ran while one was open for 7% of the time, Pallas kernels for 0%

profile of v13, /device:TPU:6, one launch (start us, length us, event | category | flops | bytes accessed | tf_op | source)
XLA Modules:
  0.0 89.4 jit_solution(1500921075237311622)
XLA Ops:
  0.7 1.2 %fusion.13 = f32[4,96,96]{1,2,0:T(8,128)S(1)} fusion(pred[96,96]{0,1:T(8,128)(4,1)S(1)} %iota_compare_fusion, bf16[4,96,384]{2,1,0:T(8,128)(2,1)} %bitcast.69), kind=kOutput, calls=%fused_computation.23 | convolution fusion | flops 9510912 | bytes 353280 | tf_op jit(solution)/shard_map/vmap()/dot_general | solution.py:51
  1.9 0.2 fusion.34
  2.2 3.8 %fusion.18 = bf16[4,96,128]{2,1,0:T(8,128)(2,1)S(1)} fusion(bf16[1,6144,1,128]{3,1,2,0:T(8,128)(2,1)S(1)} %copy-done, bf16[1,4,1,96,6144]{4,3,2,1,0:T(8,128)(2,1)} %param.5), kind=kOutput, calls=%fused_computation.28 | convolution fusion | flops 604028928 | bytes 6389760 | tf_op jit(solution)/shard_map/msd,dh->msh/dot_general | solution.py:90
  6.0 0.2 convolution_convert_fusion.1
  6.2 0.9 multiply_reduce_fusion
  7.0 0.2 fusion.15
  7.4 0.2 fusion.16
  7.7 0.6 gather_fusion
  8.5 4.7 %fusion.2 = bf16[4,24,2,6144]{3,1,0,2:T(8,128)(2,1)S(1)} fusion(bf16[2,4,24,384]{3,2,1,0:T(8,128)(2,1)S(1)} %bitcast.68, bf16[1,6144,1,384]{3,1,2,0:T(8,128)(2,1)} %param.8), kind=kOutput, calls=%fused_computation.5 | convolution fusion | flops 907149312 | bytes 7225344 | tf_op jit(solution)/shard_map/bjsk,dk->jsbd/dot_general | solution.py:100
  13.2 1.1 %slice_bitcast_fusion.2 = (bf16[24,2,6144]{2,0,1:T(8,128)(2,1)}, bf16[24,2,6144]{2,0,1:T(8,128)(2,1)S(1)}, bf16[24,2,6144]{2,0,1:T(8,128)(2,1)S(1)}) fusion(bf16[4,24,2,6144]{3,1,0,2:T(8,128)(2,1)S(1)} %fusion.2), kind=kLoop, calls=%fused_computation.34 | loop fusion | bytes 3538944 | tf_op jit(solution)/shard_map/squeeze | solution.py:35
  14.2 0.5 copy-done.1
  14.7 11.4 %collective-permute-start = (bf16[24,2,6144]{2,0,1:T(8,128)(2,1)}, bf16[24,2,6144]{2,0,1:T(8,128)(2,1)}, u32[]{:S(2)}, u32[]{:S(2)}) collective-permute-start(bf16[24,2,6144]{2,0,1:T(8,128)(2,1)} %get-tuple-element.6), channel_id=1, source_target_pairs={{0,1},{1,2},{2,3},{3,0},{4,5},{5,6},{6,7},{7,4},{8,9},{9,10},{10,1... | collective-permute-start | bytes 1769480 | tf_op jit(solution)/shard_map/ppermute | solution.py:35
  26.1 1.9 %collective-permute-start.2 = (bf16[24,2,6144]{2,0,1:T(8,128)(2,1)S(1)}, bf16[24,2,6144]{2,0,1:T(8,128)(2,1)}, u32[]{:S(2)}, u32[]{:S(2)}) collective-permute-start(bf16[24,2,6144]{2,0,1:T(8,128)(2,1)S(1)} %get-tuple-element.7), channel_id=1, source_target_pairs={{0,3},{1,0},{2,1},{3,2},{4,7},{5,4},{6,5},{7,6},{8,11},{9,8},{10,9... | collective-permute-start | bytes 1769480 | tf_op jit(solution)/shard_map/ppermute | solution.py:35
  28.1 3.4 %collective-permute-start.1 = (bf16[24,2,6144]{2,0,1:T(8,128)(2,1)S(1)}, bf16[24,2,6144]{2,0,1:T(8,128)(2,1)}, u32[]{:S(2)}, u32[]{:S(2)}) collective-permute-start(bf16[24,2,6144]{2,0,1:T(8,128)(2,1)S(1)} %get-tuple-element.8), channel_id=1, source_target_pairs={{0,2},{1,3},{2,0},{3,1},{4,6},{5,7},{6,4},{7,5},{8,10},{9,11},{10,... | collective-permute-start | bytes 1769480 | tf_op jit(solution)/shard_map/ppermute | solution.py:35
  31.5 2.0 %fusion.1 = bf16[128,6144]{0,1:T(8,128)(2,1)S(1)} fusion(bf16[4,96,128]{2,1,0:T(8,128)(2,1)S(1)} %copy-done.3, bf16[1,4,1,96,6144]{4,3,2,1,0:T(8,128)(2,1)S(1)} %bitcast.65), kind=kOutput, calls=%fused_computation.4 | convolution fusion | flops 604766208 | bytes 6389760 | tf_op jit(solution)/shard_map/msc,msh->ch/dot_general | solution.py:86
  33.6 5.0 %all_to_all.10 = bf16[24,2,128,128]{3,2,0,1:T(8,128)(2,1)S(1)} all-to-all(bf16[24,2,128,128]{3,2,0,1:T(8,128)(2,1)S(1)} %copy.20), channel_id=1, replica_groups=mesh['pipe'=4,'dp_y'=2,'dp_z'=12,'dp_core'=2,'tensor'=4] {'dp_core'}, dimensions={1} | all-to-all | bytes 3145728 | tf_op jit(solution)/shard_map/all_to_all | solution.py:44
  38.6 1.1 %fusion.23 = bf16[24,128,128]{2,1,0:T(8,128)(2,1)} fusion(bf16[24,2,128,128]{3,2,0,1:T(8,128)(2,1)S(1)} %all_to_all.10), kind=kLoop, calls=%fused_computation.31 | loop fusion | flops 1572864 | bytes 2359296 | tf_op jit(solution)/shard_map/convert_element_type | solution.py:45
  39.8 13.1 %all-to-all-start.1 = ((bf16[24,128,128]{2,1,0:T(8,128)(2,1)}), bf16[24,128,128]{2,1,0:T(8,128)(2,1)S(1)}, u32[]{:S(2)}, u32[]{:S(2)}) async-start(bf16[24,128,128]{2,1,0:T(8,128)(2,1)} %fusion.23), calls=%async_computation.1 | async-start | bytes 1572864 | tf_op jit(solution)/shard_map/all_to_all | solution.py:46
  52.9 1.9 %fusion.10 = bf16[24,2,6144]{2,0,1:T(8,128)(2,1)S(1)} fusion(bf16[24,2,6144]{2,0,1:T(8,128)(2,1)} %collective-permute-done.2, bf16[24,2,6144]{2,0,1:T(8,128)(2,1)} %collective-permute-done.1, bf16[24,2,6144]{2,0,1:T(8,128)(2,1)} %collective-permute-done, bf16[4,24,2,6144]{3,1,0,2:T(8,128)(2,1)} %copy-done.1), kind=kLoop, calls=%fused_computation.16 | loop fusion | flops 2359296 | bytes 2949120 | tf_op jit(solution)/shard_map/convert_element_type | solution.py:102
  54.8 1.3 %collective-permute-start.3 = (bf16[24,2,6144]{2,0,1:T(8,128)(2,1)S(1)}, bf16[24,2,6144]{2,0,1:T(8,128)(2,1)S(1)}, u32[]{:S(2)}, u32[]{:S(2)}) collective-permute-start(bf16[24,2,6144]{2,0,1:T(8,128)(2,1)S(1)} %fusion.10), channel_id=1, source_target_pairs={{192,0},{384,192},{576,384},{193,1},{385,193},{577,385},{194,2},{3... | collective-permute-start | bytes 1769480 | tf_op jit(solution)/shard_map/ppermute | solution.py:15
  56.1 29.7 %collective-permute-done.3 = bf16[24,2,6144]{2,0,1:T(8,128)(2,1)S(1)} collective-permute-done((bf16[24,2,6144]{2,0,1:T(8,128)(2,1)S(1)}, bf16[24,2,6144]{2,0,1:T(8,128)(2,1)S(1)}, u32[]{:S(2)}, u32[]{:S(2)}) %collective-permute-start.3) | collective-permute-done | bytes 589856 | tf_op jit(solution)/shard_map/ppermute | solution.py:15
  85.8 1.4 %copy.21 = bf16[1,1,24,2,6144]{4,3,2,1,0:T(2,128)(2,1)} copy(bf16[1,1,24,2,6144]{4,2,3,1,0:T(8,128)(2,1)S(1)} %bitcast.67) | data formatting | bytes 1179648
  87.2 1.4 %all-to-all-done.1 = bf16[24,128,128]{2,1,0:T(8,128)(2,1)S(1)} async-done(((bf16[24,128,128]{2,1,0:T(8,128)(2,1)}), bf16[24,128,128]{2,1,0:T(8,128)(2,1)S(1)}, u32[]{:S(2)}, u32[]{:S(2)}) %all-to-all-start.1) | async-done | bytes 786464 | tf_op jit(solution)/shard_map/all_to_all | solution.py:46
  88.7 0.7 convert_reduce_fusion
  (24 shorter events, 0.5 us)
Async XLA Ops:
  0.6 1.5 %copy-start = (bf16[1,6144,1,128]{3,1,2,0:T(8,128)(2,1)S(1)}, bf16[1,6144,1,128]{3,1,2,0:T(8,128)(2,1)}, u32[]{:S(2)}) copy-start(bf16[1,6144,1,128]{3,1,2,0:T(8,128)(2,1)} %param.7) | copy-start | bytes 4718596
  2.2 4.0 %copy-start.2 = (bf16[1,4,1,96,1,384]{5,3,4,2,1,0:T(8,128)(2,1)S(1)}, bf16[1,4,1,96,1,384]{5,3,4,2,1,0:T(8,128)(2,1)}, u32[]{:S(2)}) copy-start(bf16[1,4,1,96,1,384]{5,3,4,2,1,0:T(8,128)(2,1)} %param.6) | copy-start | bytes 884740
  5.9 1.7 %copy-start.4 = (s32[1,4]{1,0:T(1,128)S(1)}, s32[1,4]{1,0:T(1,128)}, u32[]{:S(2)}) copy-start(s32[1,4]{1,0:T(1,128)} %param.9) | copy-start | bytes 52
  8.4 23.0 %slice-start = ((s8[4718592]{0:T(1024)(128)(4,1)}), s8[4194304]{0:T(1024)(128)(4,1)S(1)}, s32[]{:S(2)}) async-start(s8[4718592]{0:T(1024)(128)(4,1)} %bitcast.64), calls=%async_computation.2 | async-start | bytes 8388608
  8.4 23.0 %slice-start.1 = ((s8[4718592]{0:T(1024)(128)(4,1)}), s8[524288]{0:T(1024)(128)(4,1)S(1)}, s32[]{:S(2)}) async-start(s8[4718592]{0:T(1024)(128)(4,1)} %bitcast.64), calls=%async_computation.3 | async-start | bytes 1048576
  13.1 1.6 %copy-start.1 = (bf16[4,24,2,6144]{3,1,0,2:T(8,128)(2,1)}, bf16[4,24,2,6144]{3,1,0,2:T(8,128)(2,1)S(1)}, u32[]{:S(2)}) copy-start(bf16[4,24,2,6144]{3,1,0,2:T(8,128)(2,1)S(1)} %fusion.2) | copy-start | bytes 7077892
  13.1 18.3 %copy-start.3 = (bf16[4,96,128]{2,1,0:T(8,128)(2,1)S(1)}, bf16[4,96,128]{2,1,0:T(8,128)(2,1)}, u32[]{:S(2)}) copy-start(bf16[4,96,128]{2,1,0:T(8,128)(2,1)} %get-tuple-element.12) | copy-start | bytes 294916
  14.7 38.1 %collective-permute-start = (bf16[24,2,6144]{2,0,1:T(8,128)(2,1)}, bf16[24,2,6144]{2,0,1:T(8,128)(2,1)}, u32[]{:S(2)}, u32[]{:S(2)}) collective-permute-start(bf16[24,2,6144]{2,0,1:T(8,128)(2,1)} %get-tuple-element.6), channel_id=1, source_target_pairs={{0,1},{1,2},{2,3},{3,0},{4,5},{5,6},{6,7},{7,4},{8,9},{9,10},{10,1... | collective-permute-start | bytes 1769480 | tf_op jit(solution)/shard_map/ppermute | solution.py:35
  26.1 26.7 %collective-permute-start.2 = (bf16[24,2,6144]{2,0,1:T(8,128)(2,1)S(1)}, bf16[24,2,6144]{2,0,1:T(8,128)(2,1)}, u32[]{:S(2)}, u32[]{:S(2)}) collective-permute-start(bf16[24,2,6144]{2,0,1:T(8,128)(2,1)S(1)} %get-tuple-element.7), channel_id=1, source_target_pairs={{0,3},{1,0},{2,1},{3,2},{4,7},{5,4},{6,5},{7,6},{8,11},{9,8},{10,9... | collective-permute-start | bytes 1769480 | tf_op jit(solution)/shard_map/ppermute | solution.py:35
  28.1 24.8 %collective-permute-start.1 = (bf16[24,2,6144]{2,0,1:T(8,128)(2,1)S(1)}, bf16[24,2,6144]{2,0,1:T(8,128)(2,1)}, u32[]{:S(2)}, u32[]{:S(2)}) collective-permute-start(bf16[24,2,6144]{2,0,1:T(8,128)(2,1)S(1)} %get-tuple-element.8), channel_id=1, source_target_pairs={{0,2},{1,3},{2,0},{3,1},{4,6},{5,7},{6,4},{7,5},{8,10},{9,11},{10,... | collective-permute-start | bytes 1769480 | tf_op jit(solution)/shard_map/ppermute | solution.py:35
  39.8 48.9 %all-to-all-start.1 = ((bf16[24,128,128]{2,1,0:T(8,128)(2,1)}), bf16[24,128,128]{2,1,0:T(8,128)(2,1)S(1)}, u32[]{:S(2)}, u32[]{:S(2)}) async-start(bf16[24,128,128]{2,1,0:T(8,128)(2,1)} %fusion.23), calls=%async_computation.1 | async-start | bytes 1572864 | tf_op jit(solution)/shard_map/all_to_all | solution.py:46
  54.8 31.0 %collective-permute-start.3 = (bf16[24,2,6144]{2,0,1:T(8,128)(2,1)S(1)}, bf16[24,2,6144]{2,0,1:T(8,128)(2,1)S(1)}, u32[]{:S(2)}, u32[]{:S(2)}) collective-permute-start(bf16[24,2,6144]{2,0,1:T(8,128)(2,1)S(1)} %fusion.10), channel_id=1, source_target_pairs={{192,0},{384,192},{576,384},{193,1},{385,193},{577,385},{194,2},{3... | collective-permute-start | bytes 1769480 | tf_op jit(solution)/shard_map/ppermute | solution.py:15
